TPU v7x, 128 devices: a whole 4x4x4 slice. The times are simulated.
128 devices in a mesh: ep: 32 (over z, x, core), tp: 4 (over y).
Axes of the slice: x: 4, y: 4, z: 4, core: 2. Of those that a mesh axis runs over, the one named last changes fastest.
Arguments:
- stream: bfloat16 [16384, 2048], P('ep'), may hold values from -6 to 6
- queries: bfloat16 [16384, 2048], P('ep', 'tp'), may hold values from -6 to 6
- keys_in: bfloat16 [16384, 2048], P('ep', 'tp'), may hold values from -6 to 6
- values_in: bfloat16 [16384, 2048], P('ep', 'tp'), may hold values from -6 to 6
- segment_ids: int32 [32, 512], P('ep'), may hold values from 0 to 5, never falling along the last dimension, each value on 1 to 256 neighbouring positions
- routes: int32 [16384, 4], P('ep'), may hold values from 0 to 63, all different within a row; in each aligned block of 512 rows (0 to 511, 512 to 1023, ...) at most 48 rows name the same one
- route_weights: float32 [16384, 4], P('ep'), may hold values from 0.1 to 0.6
- w_out: bfloat16 [2048, 2048], P('tp'), may hold values from -0.125 to 0.125
- norm_gain: float32 [2048], replicated, may hold values from 0.25 to 1.75
- expert_gate: bfloat16 [64, 2048, 1408], P('ep', None, 'tp'), may hold values from -0.125 to 0.125
- expert_up: bfloat16 [64, 2048, 1408], P('ep', None, 'tp'), may hold values from -0.125 to 0.125
- expert_down: bfloat16 [64, 1408, 2048], P('ep', 'tp'), may hold values from -0.15625 to 0.15625
- shared_gate: bfloat16 [2048, 3584], P(None, 'tp'), may hold values from -0.125 to 0.125
- shared_up: bfloat16 [2048, 3584], P(None, 'tp'), may hold values from -0.125 to 0.125
- shared_down: bfloat16 [3584, 2048], P('tp'), may hold values from -0.09375 to 0.09375
- shared_router: bfloat16 [2048], replicated, may hold values from -0.125 to 0.125
Outputs:
- mixed: bfloat16 [16384, 2048], P('ep', 'tp')
Inputs may be any that keep to these rules, and one draw needn't show every extreme that they name: `routes`: in each aligned block of 512 rows, no expert is named by more than 48 rows, a bound that some block reaches. `segment_ids`: segment numbers never fall within a block; each prompt has at most 256 tokens, and some has exactly 256.
All inputs are finite; a program needn't handle non-finite values.
Results may differ from a plain program's by a relative error of at most 0.012.
Values may be sent and summed in bfloat16 or wider, within the bound.
No kernel may reach another device: no remote copies, remote signals or barrier semaphores. Data moves between devices by JAX's collectives and lax.ppermute only.
A program may use at most 128 MiB of HBM per device.

v0:
```python
import jax
import jax.numpy as jnp
from jax import lax
from jax.sharding import PartitionSpec as P

HEAD = 128


def slots_of(block_routes, experts, capacity):
    length, picks = block_routes.shape
    flat = block_routes.reshape(length * picks)
    onehot = (flat[:, None] == jnp.arange(experts, dtype=jnp.int32)[None, :]).astype(jnp.int32)
    before = jnp.cumsum(onehot, axis=0, dtype=jnp.int32) - onehot
    rank = jnp.sum(before * onehot, axis=1, dtype=jnp.int32)
    slot = flat * capacity + rank
    owners = jnp.arange(length * picks, dtype=jnp.int32) // picks
    table = jnp.full((experts * capacity,), -1, dtype=jnp.int32).at[slot].set(owners)
    return (slot.reshape(length, picks), table)


def attend_local(query_block, key_block, value_block, segment):
    length = query_block.shape[0]
    heads = query_block.shape[1] // HEAD
    places = jnp.arange(length, dtype=jnp.int32)
    allowed = (segment[:, None] == segment[None, :]) & (places[:, None] >= places[None, :])

    def one_head(operands):
        query_rows, key_rows, value_rows = operands
        scores = jnp.dot(query_rows, key_rows.T, preferred_element_type=jnp.float32) * HEAD ** (
            -0.5
        )
        scores = jnp.where(allowed, scores, -jnp.inf)
        highest = jnp.max(scores, axis=1, keepdims=True)
        weights = jnp.exp(scores - highest)
        shares = (weights / jnp.sum(weights, axis=1, keepdims=True)).astype(jnp.bfloat16)
        return jnp.dot(shares, value_rows, preferred_element_type=jnp.float32).astype(jnp.bfloat16)

    def by_head(values):
        return values.reshape(length, heads, HEAD).transpose(1, 0, 2)

    attended = lax.map(one_head, (by_head(query_block), by_head(key_block), by_head(value_block)))
    return attended.transpose(1, 0, 2).reshape(length, heads * HEAD)


def on_device(
    stream,
    queries,
    keys_in,
    values_in,
    segment_ids,
    routes,
    route_weights,
    w_out,
    norm_gain,
    expert_gate,
    expert_up,
    expert_down,
    shared_gate,
    shared_up,
    shared_down,
    shared_router,
):
    length, width = stream.shape
    ep_count = lax.axis_size("ep")
    tp_count = lax.axis_size("tp")
    attended = attend_local(queries, keys_in, values_in, segment_ids[0])
    partial_value = jnp.dot(attended, w_out, preferred_element_type=jnp.float32)
    resid = stream.astype(jnp.float32) + lax.psum(partial_value.astype(jnp.bfloat16), "tp").astype(
        jnp.float32
    )
    normed = (
        resid * lax.rsqrt(jnp.mean(resid * resid, axis=1, keepdims=True) + 1e-06) * norm_gain
    ).astype(jnp.bfloat16)
    shared_gate_rows = jnp.dot(normed, shared_gate, preferred_element_type=jnp.float32)
    shared_up_rows = jnp.dot(normed, shared_up, preferred_element_type=jnp.float32)
    shared_hidden = (jax.nn.silu(shared_gate_rows) * shared_up_rows).astype(jnp.bfloat16)
    shared_part = jnp.dot(shared_hidden, shared_down, preferred_element_type=jnp.float32)
    shared_cols = lax.psum_scatter(
        shared_part.astype(jnp.bfloat16), "tp", scatter_dimension=1, tiled=True
    ).astype(jnp.float32)
    shared_scale = jax.nn.sigmoid(
        jnp.dot(normed, shared_router, preferred_element_type=jnp.float32)
    )
    local_experts = expert_gate.shape[0]
    experts = local_experts * ep_count
    picks = routes.shape[1]
    divisor = 2 * experts * tp_count
    capacity = tp_count * ((3 * length * picks + divisor - 1) // divisor)
    slot, table = slots_of(routes, experts, capacity)
    live = table >= 0
    outgoing = jnp.take(normed, jnp.maximum(table, 0), axis=0)
    outgoing = jnp.where(live[:, None], outgoing, jnp.zeros_like(outgoing))
    outgoing = outgoing.reshape(ep_count, local_experts, capacity, width)
    incoming = lax.all_to_all(outgoing, "ep", split_axis=0, concat_axis=0, tiled=True)
    gate_rows = jnp.einsum(
        "sjcd,jdf->sjcf", incoming, expert_gate, preferred_element_type=jnp.float32
    )
    up_rows = jnp.einsum("sjcd,jdf->sjcf", incoming, expert_up, preferred_element_type=jnp.float32)
    expert_hidden = (jax.nn.silu(gate_rows) * up_rows).astype(jnp.bfloat16)
    expert_part = jnp.einsum(
        "sjcf,jfd->sjcd", expert_hidden, expert_down, preferred_element_type=jnp.float32
    )
    expert_cols = lax.psum_scatter(
        expert_part.astype(jnp.bfloat16), "tp", scatter_dimension=3, tiled=True
    )
    returned = lax.all_to_all(expert_cols, "ep", split_axis=0, concat_axis=0, tiled=True)
    columns = returned.shape[3]
    flat_results = returned.reshape(experts * capacity, columns)
    picked = (
        jnp.take(flat_results, slot.reshape(-1), axis=0)
        .reshape(length, picks, columns)
        .astype(jnp.float32)
    )
    routed = jnp.sum(picked * route_weights[:, :, None], axis=1)
    resid_cols = lax.dynamic_slice_in_dim(resid, lax.axis_index("tp") * columns, columns, 1)
    return (resid_cols + shared_scale[:, None] * shared_cols + routed).astype(jnp.bfloat16)


def solution(mesh):
    placed = (
        P("ep", None),
        P("ep", "tp"),
        P("ep", "tp"),
        P("ep", "tp"),
        P("ep", None),
        P("ep", None),
        P("ep", None),
        P("tp", None),
        P(),
        P("ep", None, "tp"),
        P("ep", None, "tp"),
        P("ep", "tp", None),
        P(None, "tp"),
        P(None, "tp"),
        P("tp", None),
        P(),
    )
    return jax.shard_map(
        on_device, mesh=mesh, in_specs=placed, out_specs=P("ep", "tp"), check_vma=False
    )
```

profile of v0, /device:TPU:0, one launch (start us, length us, event | category | flops | bytes accessed | tf_op | source)
XLA Modules:
  0.0 510.2 jit_solution(16891996998942227729)
XLA Ops:
  6.5 2.2 copy.52
  8.7 2.1 copy.53
  10.8 2.1 copy.54
  12.9 14.5 %while.11 = (s32[]{:T(128)}, bf16[4,512,128]{1,2,0:T(8,128)(2,1)}, bf16[4,512,128]{1,2,0:T(8,128)(2,1)}, bf16[4,512,128]{1,2,0:T(8,128)(2,1)}, bf16[4,512,128]{1,2,0:T(8,128)(2,1)}, /*index=5*/s32[512]{0:T(512)}, s32[]{:T(128)}) while((s32[]{:T(128)}, bf16[4,512,128]{1,2,0:T(8,128)(2,1)}, bf16[4,512,128]{1,2,0:T(8,128)(2,1)}, ...), condition=%wide.region_3.4_spmd.clone, body=%wide.region_0.3_spmd.clone.sunk | while | flops 137165824 | bytes 4209757 | solution.py:41
  12.9 1.3 fusion.63
  16.5 1.3 fusion.63
  20.1 1.3 fusion.63
  23.7 1.3 fusion.63
  27.4 4.3 convolution_convert_fusion.2
  33.5 31.5 %reduce-window.6 = s32[64,16,128]{2,1,0:T(8,128)S(1)} reduce-window(s32[64,16,128]{2,1,0:T(8,128)} %fusion.38, s32[]{:T(128)} %constant.82.clone.1), window={size=1x1x128 pad=0_0x0_0x127_0}, to_apply=%region_7.8 | reduce-window | flops 16646144 | bytes 1048580 | tf_op jit(solution)/shard_map/reduce-window
  66.0 1.5 copy.73
  68.1 8.1 %scatter_custom_fusion = s32[3072]{0:T(1024)S(1)} fusion(s32[2048]{0:T(1024)S(1)} %bitcast.120, s32[2048]{0:T(1024)S(1)} %add_select_fusion, s32[]{:T(128)} %constant.94.clone.1), kind=kCustom, calls=%fused_computation.68 | custom fusion | bytes 12292 | tf_op jit(solution)/shard_map/scatter | solution.py:17
  76.4 16.7 %all-reduce.2.cloned.1.call-done = bf16[512,2048]{1,0:T(8,128)(2,1)} async-done(((bf16[512,2048]{1,0:T(8,128)(2,1)}), bf16[512,2048]{1,0:T(8,128)(2,1)}) %all-reduce.2.cloned.1.call-update) | async-done | bytes 2097168 | tf_op jit(solution)/shard_map/psum | solution.py:68
  93.1 5.0 convert_add_fusion
  98.2 2.3 multiply_convert_fusion
  100.5 25.7 %gather_fusion = bf16[3072,2048]{1,0:T(8,128)(2,1)} fusion(bf16[512,2048]{1,0:T(8,128)(2,1)} %multiply_convert_fusion, s32[3072]{0:T(1024)S(1)} %maximum_clamp_fusion), kind=kCustom, calls=%fused_computation | custom fusion | bytes 25178112 | tf_op jit(solution)/shard_map/jit(_take)/gather | solution.py:91
  126.2 7.0 %select_select_fusion = bf16[32,2,48,2048]{3,2,1,0:T(8,128)(2,1)S(1)} fusion(bf16[32,2,48,2048]{3,2,1,0:T(8,128)(2,1)} %bitcast.114, pred[32,2,48]{2,1,0:T(4,128)(4,1)S(1)} %broadcast_in_dim.67, pred[32,2,48]{2,1,0:T(4,128)(4,1)S(1)} %broadcast_in_dim.65), kind=kLoop, calls=%fused_computation.23 | loop fusion | flops 12582912 | bytes 25171968 | tf_op jit(solution)/shard_map/jit(_where)/select_n | solution.py:92
  133.2 148.1 %all_to_all.10 = bf16[32,2,48,2048]{3,2,1,0:T(8,128)(2,1)S(1)} all-to-all(bf16[32,2,48,2048]{3,2,1,0:T(8,128)(2,1)S(1)} %select_select_fusion), channel_id=1, replica_groups=mesh['ep'=32,'tp'=4] {'ep'}, dimensions={0} | all-to-all | bytes 25165824 | tf_op jit(solution)/shard_map/all_to_all | solution.py:94
  281.3 4.5 copy-done.1
  285.7 8.6 %fusion.14 = f32[2,32,48,352]{3,2,1,0:T(8,128)} fusion(bf16[32,2,48,2048]{3,2,1,0:T(8,128)(2,1)S(1)} %all_to_all.10, bf16[2,2048,352]{1,2,0:T(8,128)(2,1)S(1)} %copy-done.8), kind=kOutput, calls=%fused_computation.24 | convolution fusion | flops 4429185024 | bytes 19791872 | tf_op jit(solution)/shard_map/sjcd,jdf->sjcf/dot_general | solution.py:98
  294.3 20.3 %convert_bitcast_fusion = bf16[32,2,48,2048]{3,2,0,1:T(8,128)(2,1)} fusion(bf16[2,352,2048]{2,1,0:T(8,128)(2,1)S(1)} %copy-done, f32[2,32,48,352]{3,2,1,0:T(8,128)} %fusion.14, bf16[32,2,48,2048]{3,2,1,0:T(8,128)(2,1)} %copy-done.1, bf16[2,2048,352]{1,2,0:T(8,128)(2,1)} %param.27), kind=kOutput, calls=%fused_computation.22 | convolution fusion | flops 8871149568 | bytes 35258368 | tf_op jit(solution)/shard_map/sjcf,jfd->sjcd/dot_general | solution.py:100
  314.9 6.3 %fusion.48 = f32[512,896]{1,0:T(8,128)} fusion(bf16[512,2048]{1,0:T(8,128)(2,1)} %multiply_convert_fusion, bf16[2048,896]{1,0:T(8,128)(2,1)} %param.30), kind=kOutput, calls=%fused_computation.78 | convolution fusion | flops 1879048192 | bytes 7602176 | tf_op jit(solution)/shard_map/dot_general | solution.py:74
  321.2 10.2 %convolution_convert_fusion.1 = bf16[512,2048]{1,0:T(8,128)(2,1)} fusion(bf16[896,2048]{1,0:T(8,128)(2,1)} %param.32, f32[512,896]{1,0:T(8,128)} %fusion.48, bf16[512,2048]{1,0:T(8,128)(2,1)} %multiply_convert_fusion, bf16[2048,896]{1,0:T(8,128)(2,1)} %param.31), kind=kOutput, calls=%fused_computation.39 | convolution fusion | flops 3761897472 | bytes 13369344 | tf_op jit(solution)/shard_map/dot_general | solution.py:77
  331.4 94.2 %reduce-scatter.5.cloned.1.call-done = bf16[32,2,48,512]{3,2,0,1:T(8,128)(2,1)} async-done(((bf16[32,2,48,2048]{3,2,0,1:T(8,128)(2,1)}), bf16[32,2,48,512]{3,2,0,1:T(8,128)(2,1)}) %reduce-scatter.5.cloned.1.call-update) | async-done | bytes 3145744 | tf_op jit(solution)/shard_map/reduce_scatter | solution.py:103
  425.6 3.9 copy.68
  429.5 7.5 %all-to-all-start.1 = ((bf16[32,2,48,512]{3,2,1,0:T(8,128)(2,1)}), bf16[32,2,48,512]{3,2,1,0:T(8,128)(2,1)}, u32[]{:S(2)}, u32[]{:S(2)}) async-start(bf16[32,2,48,512]{3,2,1,0:T(8,128)(2,1)} %copy.68), calls=%async_computation.3 | async-start | bytes 6291456 | tf_op jit(solution)/shard_map/all_to_all | solution.py:106
  437.8 2.2 fusion.47
  440.0 38.9 %all-to-all-done.1 = bf16[32,2,48,512]{3,2,1,0:T(8,128)(2,1)} async-done(((bf16[32,2,48,512]{3,2,1,0:T(8,128)(2,1)}), bf16[32,2,48,512]{3,2,1,0:T(8,128)(2,1)}, u32[]{:S(2)}, u32[]{:S(2)}) %all-to-all-start.1) | async-done | bytes 3145760 | tf_op jit(solution)/shard_map/all_to_all | solution.py:106
  479.0 11.5 %gather_fusion.1 = bf16[2048,512]{1,0:T(8,128)(2,1)} fusion(bf16[3072,512]{1,0:T(8,128)(2,1)} %bitcast.25, s32[2048]{0:T(1024)S(1)} %broadcast_clamp_fusion), kind=kCustom, calls=%fused_computation.1 | custom fusion | bytes 4202496 | tf_op jit(solution)/shard_map/jit(_take)/gather | solution.py:110
  490.5 4.0 gather.15
  494.5 6.5 %multiply_reduce_fusion = f32[512,512]{1,0:T(8,128)} fusion(f32[512,4]{1,0:T(8,128)S(1)} %copy.69, bf16[512,4,512]{2,1,0:T(4,128)(2,1)} %gather.15, pred[512,4]{1,0:T(8,128)(4,1)S(1)} %copy.64), kind=kLoop, calls=%fused_computation.35 | loop fusion | flops 3932160 | bytes 3155968 | tf_op jit(solution)/shard_map/reduce_sum | solution.py:114
  501.0 2.7 add_convert_fusion
  (67 shorter events, 13.7 us)
Async XLA Ops:
  6.5 287.8 %copy-start = (bf16[2,352,2048]{2,1,0:T(8,128)(2,1)S(1)}, bf16[2,352,2048]{2,1,0:T(8,128)(2,1)}, u32[]{:S(2)}) copy-start(bf16[2,352,2048]{2,1,0:T(8,128)(2,1)} %param.29) | copy-start | bytes 8650756
  6.5 86.6 %all-reduce.2.cloned.1.call-start = ((), (), s32[]{:S(2)}) async-start(), calls=%async_computation.4 | async-start | bytes 4194304 | tf_op jit(solution)/shard_map/psum | solution.py:68
  27.4 4.4 copy-start.4
  31.7 393.9 %reduce-scatter.5.cloned.1.call-start = ((), (), s32[]{:S(2)}) async-start(), calls=%async_computation.6 | async-start | bytes 15728640 | tf_op jit(solution)/shard_map/reduce_scatter | solution.py:103
  76.4 21.7 %copy-start.5 = (f32[2048]{0:T(1024)S(1)}, f32[2048]{0:T(1024)}, u32[]{:S(2)}) copy-start(f32[2048]{0:T(1024)} %param.26) | copy-start | bytes 24580
  93.1 5.0 copy-start.2
  93.1 5.0 copy-start.3
  133.1 152.6 %copy-start.8 = (bf16[2,2048,352]{1,2,0:T(8,128)(2,1)S(1)}, bf16[2,2048,352]{1,2,0:T(8,128)(2,1)}, u32[]{:S(2)}) copy-start(bf16[2,2048,352]{1,2,0:T(8,128)(2,1)} %param.28) | copy-start | bytes 8650756
  281.2 4.5 copy-start.1
  314.7 186.3 %reduce-scatter.3.cloned.1.call-start = ((), (), s32[]{:S(2)}) async-start(), calls=%async_computation.5 | async-start | bytes 2621440 | tf_op jit(solution)/shard_map/reduce_scatter | solution.py:78
  429.5 7.8 %copy-start.7 = (bf16[2048]{0:T(1024)(128)(2,1)S(1)}, bf16[2048]{0:T(1024)(128)(2,1)}, u32[]{:S(2)}) copy-start(bf16[2048]{0:T(1024)(128)(2,1)} %param.33) | copy-start | bytes 12292
  429.5 7.8 %copy-start.6 = (f32[512,4]{0,1:T(4,128)S(1)}, f32[512,4]{0,1:T(4,128)}, u32[]{:S(2)}) copy-start(f32[512,4]{0,1:T(4,128)} %param.24) | copy-start | bytes 24580
  429.5 49.5 %all-to-all-start.1 = ((bf16[32,2,48,512]{3,2,1,0:T(8,128)(2,1)}), bf16[32,2,48,512]{3,2,1,0:T(8,128)(2,1)}, u32[]{:S(2)}, u32[]{:S(2)}) async-start(bf16[32,2,48,512]{3,2,1,0:T(8,128)(2,1)} %copy.68), calls=%async_computation.3 | async-start | bytes 6291456 | tf_op jit(solution)/shard_map/all_to_all | solution.py:106
Sparse Core Ops, SparseCore 0:
  31.9 61.2 all-reduce.1
  314.8 110.7 reduce-scatter.4
  428.0 29.4 reduce-scatter.2
where the time goes:
time: 513 us; the launch traced here: 510 us
  waiting for transfers between devices  150 us (29%)
  blocking collectives  148 us (29%)
  local copies, waits for them, and re-layouts  71.3 us (14%)
  matrix products  62.4 us (12%)
  other arithmetic  57.4 us (11%)
  between operations  13.3 us (3%)
  starting transfers between devices  7.79 us (2%)
    all_to_all x1, blocking collectives, on_device(): lax.all_to_all(outgoing, 'ep', split_axis=0, concat_axis=0, tiled=True)  148 us
    reduce_scatter x1, waiting for transfers between devices, on_device(): lax.psum_scatter(expert_part.astype(jnp.bfloat16), 'tp', scatter_dimensio...  94.2 us
    all_to_all x1, waiting for transfers between devices, on_device(): lax.all_to_all(expert_cols, 'ep', split_axis=0, concat_axis=0, tiled=True)  38.9 us
    another operation x3, other arithmetic  31.9 us
    gather x1, local copies, waits for them, and re-layouts, on_device(): outgoing = jnp.take(normed, jnp.maximum(table, 0), axis=0)  25.7 us
    dot_general x1, matrix products, on_device(): jnp.einsum('sjcf,jfd->sjcd', expert_hidden, expert_down, preferred_elemen...  20.3 us
    psum x1, waiting for transfers between devices, on_device(): lax.psum(partial_value.astype(jnp.bfloat16), 'tp').astype(jnp.float32)  16.7 us
    gather x2, local copies, waits for them, and re-layouts, on_device(): jnp.take(flat_results, slot.reshape(-1), axis=0)  15.5 us
  transfers between devices with their start and end apart: 4, of which 3 were waited for; matrix products, arithmetic and copies ran while one was open for 18% of the time, Pallas kernels for 0%

commit v1 on v0

--- a/solution.py
+++ b/solution.py
@@ -8,14 +8,15 @@
 
 def slots_of(block_routes, experts, capacity):
     length, picks = block_routes.shape
-    flat = block_routes.reshape(length * picks)
-    onehot = (flat[:, None] == jnp.arange(experts, dtype=jnp.int32)[None, :]).astype(jnp.int32)
-    before = jnp.cumsum(onehot, axis=0, dtype=jnp.int32) - onehot
-    rank = jnp.sum(before * onehot, axis=1, dtype=jnp.int32)
+    count = length * picks
+    flat = block_routes.reshape(count)
+    onehot = flat[:, None] == jnp.arange(experts, dtype=jnp.int32)[None, :]
+    places = jnp.arange(count, dtype=jnp.int32)
+    earlier = (places[:, None] > places[None, :]).astype(jnp.bfloat16)
+    before = jnp.dot(earlier, onehot.astype(jnp.bfloat16), preferred_element_type=jnp.float32)
+    rank = jnp.sum(jnp.where(onehot, before, 0.0), axis=1).astype(jnp.int32)
     slot = flat * capacity + rank
-    owners = jnp.arange(length * picks, dtype=jnp.int32) // picks
-    table = jnp.full((experts * capacity,), -1, dtype=jnp.int32).at[slot].set(owners)
-    return (slot.reshape(length, picks), table)
+    return slot.reshape(length, picks)
 
 
 def attend_local(query_block, key_block, value_block, segment):
@@ -86,10 +87,11 @@
     picks = routes.shape[1]
     divisor = 2 * experts * tp_count
     capacity = tp_count * ((3 * length * picks + divisor - 1) // divisor)
-    slot, table = slots_of(routes, experts, capacity)
-    live = table >= 0
-    outgoing = jnp.take(normed, jnp.maximum(table, 0), axis=0)
-    outgoing = jnp.where(live[:, None], outgoing, jnp.zeros_like(outgoing))
+    slot = slots_of(routes, experts, capacity)
+    slot_ids = jnp.arange(experts * capacity, dtype=jnp.int32)
+    hits = slot[:, :, None] == slot_ids[None, None, :]
+    chosen = jnp.any(hits, axis=1).T.astype(jnp.bfloat16)
+    outgoing = jnp.dot(chosen, normed, preferred_element_type=jnp.float32).astype(jnp.bfloat16)
     outgoing = outgoing.reshape(ep_count, local_experts, capacity, width)
     incoming = lax.all_to_all(outgoing, "ep", split_axis=0, concat_axis=0, tiled=True)
     gate_rows = jnp.einsum(
@@ -106,12 +108,12 @@
     returned = lax.all_to_all(expert_cols, "ep", split_axis=0, concat_axis=0, tiled=True)
     columns = returned.shape[3]
     flat_results = returned.reshape(experts * capacity, columns)
-    picked = (
-        jnp.take(flat_results, slot.reshape(-1), axis=0)
-        .reshape(length, picks, columns)
-        .astype(jnp.float32)
+    mixing = jnp.sum(jnp.where(hits, route_weights[:, :, None], 0.0), axis=1)
+    mixing_high = mixing.astype(jnp.bfloat16)
+    mixing_low = (mixing - mixing_high.astype(jnp.float32)).astype(jnp.bfloat16)
+    routed = jnp.dot(mixing_high, flat_results, preferred_element_type=jnp.float32) + jnp.dot(
+        mixing_low, flat_results, preferred_element_type=jnp.float32
     )
-    routed = jnp.sum(picked * route_weights[:, :, None], axis=1)
     resid_cols = lax.dynamic_slice_in_dim(resid, lax.axis_index("tp") * columns, columns, 1)
     return (resid_cols + shared_scale[:, None] * shared_cols + routed).astype(jnp.bfloat16)
 

time: 513 us -> 481 us (0.938)
  local copies, waits for them, and re-layouts: 71.3 us -> 20.1 us
  other arithmetic: 57.4 us -> 23.9 us
  waiting for transfers between devices: 150 us -> 177 us
  matrix products: 62.4 us -> 86.7 us
    gather x3 -> x0, local copies, waits for them, and re-layouts: 41.2 us -> none  [the longest x1 25.7 us: on_device(): outgoing = jnp.take(normed, jnp.maximum(table, 0), axis=0)]
    psum x1, waiting for transfers between devices: 16.7 us -> 50.2 us  [on_device(): lax.psum(partial_value.astype(jnp.bfloat16), 'tp').astype(jnp.float32)]
    another operation x3 -> x0, other arithmetic: 31.9 us -> none
    dot_general x0 -> x4, matrix products: none -> 27.2 us  [the longest x1 10.1 us: on_device(): jnp.dot(chosen, normed, preferred_element_type=jnp.float32)]
    reduce_or x0 -> x1, other arithmetic: none -> 8.56 us  [on_device(): chosen = jnp.any(hits, axis=1).T.astype(jnp.bfloat16)]
    scatter x1 -> x0, local copies, waits for them, and re-layouts: 8.06 us -> none  [slots_of(): jnp.full((experts * capacity,), -1, dtype=jnp.int32).at[slot].set(owners)]
    select_n x3 -> x0, other arithmetic: 6.98 us -> none  [the longest x1 6.96 us: on_device(): outgoing = jnp.where(live[:, None], outgoing, jnp.zeros_like(outgoing))]
    all_to_all x1, waiting for transfers between devices: 38.9 us -> 32.9 us  [on_device(): lax.all_to_all(expert_cols, 'ep', split_axis=0, concat_axis=0, tiled=True)]
  transfers between devices with their start and end apart: 4 -> 4, of which waited for: 3 -> 3; matrix products, arithmetic and copies ran while one was open for 18% -> 10% of each run, Pallas kernels for 0% -> 0%
where the time goes in v1:
time: 481 us; the launch traced here: 478 us
  waiting for transfers between devices  177 us (37%)
  blocking collectives  148 us (31%)
  matrix products  86.7 us (18%)
  other arithmetic  23.9 us (5%)
  local copies, waits for them, and re-layouts  20.1 us (4%)
  between operations  13.4 us (3%)
  starting transfers between devices  7.92 us (2%)
    all_to_all x1, blocking collectives, on_device(): lax.all_to_all(outgoing, 'ep', split_axis=0, concat_axis=0, tiled=True)  148 us
    reduce_scatter x1, waiting for transfers between devices, on_device(): lax.psum_scatter(expert_part.astype(jnp.bfloat16), 'tp', scatter_dimensio...  94.2 us
    psum x1, waiting for transfers between devices, on_device(): lax.psum(partial_value.astype(jnp.bfloat16), 'tp').astype(jnp.float32)  50.2 us
    all_to_all x1, waiting for transfers between devices, on_device(): lax.all_to_all(expert_cols, 'ep', split_axis=0, concat_axis=0, tiled=True)  32.9 us
    dot_general x1, matrix products, on_device(): jnp.einsum('sjcf,jfd->sjcd', expert_hidden, expert_down, preferred_elemen...  20.3 us
    unnamed x31, local copies, waits for them, and re-layouts  12.6 us
    dot_general x1, matrix products, on_device(): jnp.dot(chosen, normed, preferred_element_type=jnp.float32)  10.1 us
  transfers between devices with their start and end apart: 4, of which 3 were waited for; matrix products, arithmetic and copies ran while one was open for 10% of the time, Pallas kernels for 0%

profile of v1, /device:TPU:0, one launch (start us, length us, event | category | flops | bytes accessed | tf_op | source)
XLA Modules:
  0.0 477.7 jit_solution(6448079744836917668)
XLA Ops:
  6.5 2.2 copy.61
  8.7 2.1 copy.62
  10.8 2.1 copy.63
  12.9 14.5 %while.11 = (s32[]{:T(128)}, bf16[4,512,128]{1,2,0:T(8,128)(2,1)}, bf16[4,512,128]{1,2,0:T(8,128)(2,1)}, bf16[4,512,128]{1,2,0:T(8,128)(2,1)}, bf16[4,512,128]{1,2,0:T(8,128)(2,1)}, /*index=5*/s32[512]{0:T(512)}, s32[]{:T(128)}) while((s32[]{:T(128)}, bf16[4,512,128]{1,2,0:T(8,128)(2,1)}, bf16[4,512,128]{1,2,0:T(8,128)(2,1)}, ...), condition=%wide.region_3.4_spmd.clone, body=%wide.region_0.3_spmd.clone.sunk | while | flops 137165824 | bytes 4210765 | solution.py:42
  12.9 1.3 fusion.76
  14.4 1.3 fusion.78
  16.5 1.3 fusion.76
  18.0 1.3 fusion.78
  20.1 1.3 fusion.76
  21.6 1.3 fusion.78
  23.7 1.3 fusion.76
  25.3 1.3 fusion.78
  27.3 4.4 convolution_convert_fusion.3
  32.3 1.7 fusion.51
  34.4 8.6 %fusion.14 = pred[512,3072]{1,0:T(8,128)(4,1)} fusion(s32[512,4]{0,1:T(4,128)S(1)} %multiply_add_fusion), kind=kLoop, calls=%fused_computation.21 | loop fusion | flops 11010048 | bytes 1581056 | tf_op jit(solution)/shard_map/reduce_or | solution.py:93
  42.9 50.2 %all-reduce.2.cloned.1.call-done = bf16[512,2048]{1,0:T(8,128)(2,1)} async-done(((bf16[512,2048]{1,0:T(8,128)(2,1)}), bf16[512,2048]{1,0:T(8,128)(2,1)}) %all-reduce.2.cloned.1.call-update) | async-done | bytes 2097168 | tf_op jit(solution)/shard_map/psum | solution.py:69
  93.1 5.0 %convert_add_fusion = (f32[512,2048]{1,0:T(8,128)}, f32[512]{0:T(512)S(1)}) fusion(bf16[512,2048]{1,0:T(8,128)(2,1)} %all-reduce.2.cloned.1.call-done, bf16[512,2048]{1,0:T(8,128)(2,1)} %param.18), kind=kLoop, calls=%fused_computation.40 | loop fusion | flops 5242368 | bytes 8390656 | tf_op jit(solution)/shard_map/add | solution.py:69
  99.5 10.1 %convolution_convert_fusion.1 = bf16[3072,2048]{1,0:T(8,128)(2,1)} fusion(pred[512,3072]{1,0:T(8,128)(4,1)S(1)} %copy-done.7, bf16[512,2048]{1,0:T(8,128)(2,1)S(1)} %multiply_convert_fusion), kind=kOutput, calls=%fused_computation.25 | convolution fusion | flops 6448742400 | bytes 16252928 | tf_op jit(solution)/shard_map/dot_general | solution.py:94
  109.6 148.3 %all_to_all.10 = bf16[32,2,48,2048]{3,2,1,0:T(8,128)(2,1)S(1)} all-to-all(bf16[32,2,48,2048]{3,2,1,0:T(8,128)(2,1)} %bitcast.95), channel_id=1, replica_groups=mesh['ep'=32,'tp'=4] {'ep'}, dimensions={0} | all-to-all | bytes 25165824 | tf_op jit(solution)/shard_map/all_to_all | solution.py:96
  257.9 4.5 copy-done.2
  262.3 8.6 %fusion.16 = f32[2,32,48,352]{3,2,1,0:T(8,128)} fusion(bf16[32,2,48,2048]{3,2,1,0:T(8,128)(2,1)S(1)} %all_to_all.10, bf16[2,2048,352]{1,2,0:T(8,128)(2,1)S(1)} %copy-done.12), kind=kOutput, calls=%fused_computation.26 | convolution fusion | flops 4429185024 | bytes 19791872 | tf_op jit(solution)/shard_map/sjcd,jdf->sjcf/dot_general | solution.py:100
  271.0 20.3 %convert_bitcast_fusion = bf16[32,2,48,2048]{3,2,0,1:T(8,128)(2,1)} fusion(bf16[2,352,2048]{2,1,0:T(8,128)(2,1)S(1)} %copy-done, f32[2,32,48,352]{3,2,1,0:T(8,128)} %fusion.16, bf16[32,2,48,2048]{3,2,1,0:T(8,128)(2,1)} %copy-done.2, bf16[2,2048,352]{1,2,0:T(8,128)(2,1)} %param.27), kind=kOutput, calls=%fused_computation.24 | convolution fusion | flops 8871149568 | bytes 35258368 | tf_op jit(solution)/shard_map/sjcf,jfd->sjcd/dot_general | solution.py:102
  291.5 1.3 copy-done.6
  292.9 5.6 %fusion.57 = f32[512,896]{1,0:T(8,128)} fusion(bf16[512,2048]{1,0:T(8,128)(2,1)S(1)} %copy-done.6, bf16[2048,896]{1,0:T(8,128)(2,1)} %param.30), kind=kOutput, calls=%fused_computation.66 | convolution fusion | flops 1879048192 | bytes 7602176 | tf_op jit(solution)/shard_map/dot_general | solution.py:75
  298.5 9.5 %convolution_convert_fusion.2 = bf16[512,2048]{1,0:T(8,128)(2,1)} fusion(bf16[896,2048]{1,0:T(8,128)(2,1)} %param.32, f32[512,896]{1,0:T(8,128)} %fusion.57, bf16[512,2048]{1,0:T(8,128)(2,1)S(1)} %copy-done.6, bf16[2048,896]{1,0:T(8,128)(2,1)} %param.31), kind=kOutput, calls=%fused_computation.42 | convolution fusion | flops 3761897472 | bytes 13369344 | tf_op jit(solution)/shard_map/dot_general | solution.py:78
  308.0 94.2 %reduce-scatter.5.cloned.1.call-done = bf16[32,2,48,512]{3,2,0,1:T(8,128)(2,1)} async-done(((bf16[32,2,48,2048]{3,2,0,1:T(8,128)(2,1)}), bf16[32,2,48,512]{3,2,0,1:T(8,128)(2,1)}) %reduce-scatter.5.cloned.1.call-update) | async-done | bytes 3145744 | tf_op jit(solution)/shard_map/reduce_scatter | solution.py:105
  402.2 3.8 copy.72
  406.1 7.5 %all-to-all-start.1 = ((bf16[32,2,48,512]{3,2,1,0:T(8,128)(2,1)}), bf16[32,2,48,512]{3,2,1,0:T(8,128)(2,1)}, u32[]{:S(2)}, u32[]{:S(2)}) async-start(bf16[32,2,48,512]{3,2,1,0:T(8,128)(2,1)} %copy.72), calls=%async_computation.3 | async-start | bytes 6291456 | tf_op jit(solution)/shard_map/all_to_all | solution.py:108
  413.6 8.4 %select_reduce_fusion = f32[512,3072]{1,0:T(8,128)} fusion(f32[512,4]{0,1:T(4,128)S(1)} %copy-done.10, s32[512,4]{0,1:T(4,128)S(1)} %multiply_add_fusion), kind=kLoop, calls=%fused_computation.19 | loop fusion | flops 17301504 | bytes 6307840 | tf_op jit(solution)/shard_map/reduce_sum | solution.py:111
  422.7 32.9 %all-to-all-done.1 = bf16[32,2,48,512]{3,2,1,0:T(8,128)(2,1)} async-done(((bf16[32,2,48,512]{3,2,1,0:T(8,128)(2,1)}), bf16[32,2,48,512]{3,2,1,0:T(8,128)(2,1)}, u32[]{:S(2)}, u32[]{:S(2)}) %all-to-all-start.1) | async-done | bytes 3145760 | tf_op jit(solution)/shard_map/all_to_all | solution.py:108
  455.5 8.3 %fusion.24 = f32[512,512]{1,0:T(8,128)} fusion(bf16[3072,512]{1,0:T(8,128)(2,1)} %bitcast.20, f32[512,3072]{1,0:T(8,128)} %select_reduce_fusion), kind=kOutput, calls=%fused_computation.41 | convolution fusion | flops 1616904192 | bytes 10485760 | tf_op jit(solution)/shard_map/dot_general | solution.py:114
  463.8 7.2 %fusion.48 = bf16[512,512]{1,0:T(8,128)(2,1)} fusion(f32[512,512]{1,0:T(8,128)} %fusion.24, bf16[3072,512]{1,0:T(8,128)(2,1)} %bitcast.20, f32[512,3072]{1,0:T(8,128)} %select_reduce_fusion, bf16[512,512]{1,0:T(8,128)(2,1)} %reduce-scatter.3.cloned.1.call-done, f32[512,2048]{1,0:T(8,128)} %get-tuple-element.91, s32[]{:T(128)S(6)} %select_n.15, ...), kind=kOutput, calls=%fused_computation.55 | convolution fusion | flops 1613758464 | bytes 12584964 | tf_op jit(solution)/shard_map/dot_general | solution.py:114
  (55 shorter events, 7.2 us)
Async XLA Ops:
  6.5 264.4 %copy-start = (bf16[2,352,2048]{2,1,0:T(8,128)(2,1)S(1)}, bf16[2,352,2048]{2,1,0:T(8,128)(2,1)}, u32[]{:S(2)}) copy-start(bf16[2,352,2048]{2,1,0:T(8,128)(2,1)} %param.29) | copy-start | bytes 8650756
  6.5 86.5 %all-reduce.2.cloned.1.call-start = ((), (), s32[]{:S(2)}) async-start(), calls=%async_computation.4 | async-start | bytes 4194304 | tf_op jit(solution)/shard_map/psum | solution.py:69
  27.3 4.6 copy-start.8
  31.7 370.5 %reduce-scatter.5.cloned.1.call-start = ((), (), s32[]{:S(2)}) async-start(), calls=%async_computation.6 | async-start | bytes 15728640 | tf_op jit(solution)/shard_map/reduce_scatter | solution.py:105
  42.9 55.2 %copy-start.9 = (f32[2048]{0:T(1024)S(1)}, f32[2048]{0:T(1024)}, u32[]{:S(2)}) copy-start(f32[2048]{0:T(1024)} %param.26) | copy-start | bytes 24580
  93.1 5.0 %copy-start.3 = (bf16[512,2048]{1,0:T(8,128)(2,1)S(1)}, bf16[512,2048]{1,0:T(8,128)(2,1)}, u32[]{:S(2)}) copy-start(bf16[512,2048]{1,0:T(8,128)(2,1)} %param.18) | copy-start | bytes 6291460
  93.1 5.0 %copy-start.4 = (bf16[512,2048]{1,0:T(8,128)(2,1)S(1)}, bf16[512,2048]{1,0:T(8,128)(2,1)}, u32[]{:S(2)}) copy-start(bf16[512,2048]{1,0:T(8,128)(2,1)} %all-reduce.2.cloned.1.call-done) | copy-start | bytes 6291460
  98.1 1.4 copy-start.7
  99.5 10.1 %copy-start.5 = (bf16[512,2048]{1,0:T(8,128)(2,1)}, bf16[512,2048]{1,0:T(8,128)(2,1)S(1)}, u32[]{:S(2)}) copy-start(bf16[512,2048]{1,0:T(8,128)(2,1)S(1)} %multiply_convert_fusion) | copy-start | bytes 6291460
  109.6 152.8 %copy-start.12 = (bf16[2,2048,352]{1,2,0:T(8,128)(2,1)S(1)}, bf16[2,2048,352]{1,2,0:T(8,128)(2,1)}, u32[]{:S(2)}) copy-start(bf16[2,2048,352]{1,2,0:T(8,128)(2,1)} %param.28) | copy-start | bytes 8650756
  257.9 4.5 copy-start.2
  291.3 1.6 copy-start.6
  291.3 172.5 %reduce-scatter.3.cloned.1.call-start = ((), (), s32[]{:S(2)}) async-start(), calls=%async_computation.5 | async-start | bytes 2621440 | tf_op jit(solution)/shard_map/reduce_scatter | solution.py:79
  406.0 7.5 %copy-start.11 = (bf16[2048]{0:T(1024)(128)(2,1)S(1)}, bf16[2048]{0:T(1024)(128)(2,1)}, u32[]{:S(2)}) copy-start(bf16[2048]{0:T(1024)(128)(2,1)} %param.33) | copy-start | bytes 12292
  406.1 7.5 %copy-start.10 = (f32[512,4]{0,1:T(4,128)S(1)}, f32[512,4]{0,1:T(4,128)}, u32[]{:S(2)}) copy-start(f32[512,4]{0,1:T(4,128)} %param.24) | copy-start | bytes 24580
  406.1 49.5 %all-to-all-start.1 = ((bf16[32,2,48,512]{3,2,1,0:T(8,128)(2,1)}), bf16[32,2,48,512]{3,2,1,0:T(8,128)(2,1)}, u32[]{:S(2)}, u32[]{:S(2)}) async-start(bf16[32,2,48,512]{3,2,1,0:T(8,128)(2,1)} %copy.72), calls=%async_computation.3 | async-start | bytes 6291456 | tf_op jit(solution)/shard_map/all_to_all | solution.py:108
  463.8 7.2 %copy-start.1 = (bf16[2,352,2048]{2,1,0:T(8,128)(2,1)S(1)}, bf16[2,352,2048]{2,1,0:T(8,128)(2,1)}, u32[]{:S(2)}) copy-start(bf16[2,352,2048]{2,1,0:T(8,128)(2,1)} %param.29) | copy-start | bytes 8650756
Sparse Core Ops, SparseCore 0:
  31.9 61.1 all-reduce.1
  291.4 110.7 reduce-scatter.4
  404.6 29.4 reduce-scatter.2

commit v2 on v1

--- a/solution.py
+++ b/solution.py
@@ -91,21 +91,31 @@
     slot_ids = jnp.arange(experts * capacity, dtype=jnp.int32)
     hits = slot[:, :, None] == slot_ids[None, None, :]
     chosen = jnp.any(hits, axis=1).T.astype(jnp.bfloat16)
-    outgoing = jnp.dot(chosen, normed, preferred_element_type=jnp.float32).astype(jnp.bfloat16)
-    outgoing = outgoing.reshape(ep_count, local_experts, capacity, width)
-    incoming = lax.all_to_all(outgoing, "ep", split_axis=0, concat_axis=0, tiled=True)
-    gate_rows = jnp.einsum(
-        "sjcd,jdf->sjcf", incoming, expert_gate, preferred_element_type=jnp.float32
-    )
-    up_rows = jnp.einsum("sjcd,jdf->sjcf", incoming, expert_up, preferred_element_type=jnp.float32)
-    expert_hidden = (jax.nn.silu(gate_rows) * up_rows).astype(jnp.bfloat16)
-    expert_part = jnp.einsum(
-        "sjcf,jfd->sjcd", expert_hidden, expert_down, preferred_element_type=jnp.float32
-    )
-    expert_cols = lax.psum_scatter(
-        expert_part.astype(jnp.bfloat16), "tp", scatter_dimension=3, tiled=True
-    )
-    returned = lax.all_to_all(expert_cols, "ep", split_axis=0, concat_axis=0, tiled=True)
+    chosen = chosen.reshape(ep_count, local_experts, capacity, length)
+    chunks = 4 if capacity % 4 == 0 else 1
+    step = capacity // chunks
+    pieces = []
+    for index in range(chunks):
+        picks_of = chosen[:, :, index * step : (index + 1) * step]
+        outgoing = jnp.einsum(
+            "sjct,td->sjcd", picks_of, normed, preferred_element_type=jnp.float32
+        ).astype(jnp.bfloat16)
+        incoming = lax.all_to_all(outgoing, "ep", split_axis=0, concat_axis=0, tiled=True)
+        gate_rows = jnp.einsum(
+            "sjcd,jdf->sjcf", incoming, expert_gate, preferred_element_type=jnp.float32
+        )
+        up_rows = jnp.einsum(
+            "sjcd,jdf->sjcf", incoming, expert_up, preferred_element_type=jnp.float32
+        )
+        expert_hidden = (jax.nn.silu(gate_rows) * up_rows).astype(jnp.bfloat16)
+        expert_part = jnp.einsum(
+            "sjcf,jfd->sjcd", expert_hidden, expert_down, preferred_element_type=jnp.float32
+        )
+        expert_cols = lax.psum_scatter(
+            expert_part.astype(jnp.bfloat16), "tp", scatter_dimension=3, tiled=True
+        )
+        pieces.append(lax.all_to_all(expert_cols, "ep", split_axis=0, concat_axis=0, tiled=True))
+    returned = jnp.concatenate(pieces, axis=2)
     columns = returned.shape[3]
     flat_results = returned.reshape(experts * capacity, columns)
     mixing = jnp.sum(jnp.where(hits, route_weights[:, :, None], 0.0), axis=1)

time: 481 us -> 492 us (1.023)
  waiting for transfers between devices: 177 us -> 66.6 us
  local copies, waits for them, and re-layouts: 20.1 us -> 61 us
  matrix products: 86.7 us -> 118 us
  blocking collectives: 148 us -> 178 us
  starting transfers between devices: 7.92 us -> 21.5 us
    reduce_scatter x1 -> x4, waiting for transfers between devices: 94.2 us -> 0.06 us  [on_device(): lax.psum_scatter(expert_part.astype(jnp.bfloat16), 'tp', scatter_dimensio...]
    all_to_all x1 -> x4, blocking collectives: 148 us -> 178 us  [on_device(): lax.all_to_all(outgoing, 'ep', split_axis=0, concat_axis=0, tiled=True)]
    dot_general x1 -> x4, matrix products: 20.3 us -> 41.1 us  [on_device(): jnp.einsum('sjcf,jfd->sjcd', expert_hidden, expert_down, preferred_elemen...]
    dot_general x2 -> x8, matrix products: 18.7 us -> 32.2 us  [the longest x4 19.9 us: on_device(): jnp.einsum('sjcd,jdf->sjcf', incoming, expert_gate, preferred_element_typ...]
    all_to_all x1 -> x4, starting transfers between devices: 7.48 us -> 20.5 us  [on_device(): lax.all_to_all(expert_cols, 'ep', split_axis=0, concat_axis=0, tiled=True)]
    convert_element_type x0 -> x4, local copies, waits for them, and re-layouts: none -> 13 us  [on_device(): outgoing = jnp.einsum('sjct,td->sjcd', picks_of, normed, preferred_elemen...]
    all_to_all x0 -> x4, local copies, waits for them, and re-layouts: none -> 8.36 us  [on_device(): lax.all_to_all(expert_cols, 'ep', split_axis=0, concat_axis=0, tiled=True)]
    all_to_all x1 -> x4, waiting for transfers between devices: 32.9 us -> 24.5 us  [on_device(): lax.all_to_all(expert_cols, 'ep', split_axis=0, concat_axis=0, tiled=True)]
  transfers between devices with their start and end apart: 4 -> 10, of which waited for: 3 -> 4; matrix products, arithmetic and copies ran while one was open for 10% -> 28% of each run, Pallas kernels for 0% -> 0%
where the time goes in v2:
time: 492 us; the launch traced here: 487 us
  blocking collectives  178 us (36%)
  matrix products  118 us (24%)
  waiting for transfers between devices  66.6 us (14%)
  local copies, waits for them, and re-layouts  61 us (12%)
  other arithmetic  26.9 us (5%)
  starting transfers between devices  21.5 us (4%)
  between operations  14.2 us (3%)
    all_to_all x4, blocking collectives, on_device(): lax.all_to_all(outgoing, 'ep', split_axis=0, concat_axis=0, tiled=True)  178 us
    psum x1, waiting for transfers between devices, on_device(): lax.psum(partial_value.astype(jnp.bfloat16), 'tp').astype(jnp.float32)  41.9 us
    dot_general x4, matrix products, on_device(): jnp.einsum('sjcf,jfd->sjcd', expert_hidden, expert_down, preferred_elemen...  41.1 us
    all_to_all x4, waiting for transfers between devices, on_device(): lax.all_to_all(expert_cols, 'ep', split_axis=0, concat_axis=0, tiled=True)  24.5 us
    all_to_all x4, starting transfers between devices, on_device(): lax.all_to_all(expert_cols, 'ep', split_axis=0, concat_axis=0, tiled=True)  20.5 us
    dot_general x4, matrix products, on_device(): jnp.einsum('sjcd,jdf->sjcf', incoming, expert_gate, preferred_element_typ...  19.9 us
    unnamed x45, local copies, waits for them, and re-layouts  16.3 us
    convert_element_type x4, local copies, waits for them, and re-layouts, on_device(): outgoing = jnp.einsum('sjct,td->sjcd', picks_of, normed, preferred_elemen...  13 us
  transfers between devices with their start and end apart: 10, of which 4 were waited for; matrix products, arithmetic and copies ran while one was open for 28% of the time, Pallas kernels for 0%

profile of v2, /device:TPU:0, one launch (start us, length us, event | category | flops | bytes accessed | tf_op | source)
XLA Modules:
  0.0 487.0 jit_solution(12607068449969064952)
XLA Ops:
  12.9 14.5 %while.11 = (s32[]{:T(128)}, bf16[4,512,128]{1,2,0:T(8,128)(2,1)}, bf16[4,512,128]{1,2,0:T(8,128)(2,1)}, bf16[4,512,128]{1,2,0:T(8,128)(2,1)}, bf16[4,512,128]{1,2,0:T(8,128)(2,1)}, /*index=5*/s32[512]{0:T(512)S(1)}, s32[]{:T(128)}) while((s32[]{:T(128)}, bf16[4,512,128]{1,2,0:T(8,128)(2,1)}, bf16[4,512,128]{1,2,0:T(8,128)(2,1)}, ...), condition=%wide.region_3.4_spmd.clone, body=%wide.region_0.3_spmd.clone.sunk | while | flops 137165824 | bytes 4209757 | solution.py:42
  27.4 4.4 convolution_convert_fusion.10
  34.4 8.5 %fusion.14 = pred[512,3072]{1,0:T(8,128)(4,1)} fusion(s32[512,4]{0,1:T(4,128)S(1)} %multiply_add_fusion), kind=kLoop, calls=%fused_computation.21 | loop fusion | flops 11010048 | bytes 1581056 | tf_op jit(solution)/shard_map/reduce_or | solution.py:93
  43.0 4.7 copy.146
  47.7 3.5 fusion.178
  51.2 41.9 %all-reduce.2.cloned.1.call-done = bf16[512,2048]{1,0:T(8,128)(2,1)} async-done(((bf16[512,2048]{1,0:T(8,128)(2,1)}), bf16[512,2048]{1,0:T(8,128)(2,1)}) %all-reduce.2.cloned.1.call-update) | async-done | bytes 2097168 | tf_op jit(solution)/shard_map/psum | solution.py:69
  93.1 5.0 %convert_add_fusion = (f32[512,2048]{1,0:T(8,128)}, f32[512]{0:T(512)S(1)}) fusion(bf16[512,2048]{1,0:T(8,128)(2,1)} %all-reduce.2.cloned.1.call-done, bf16[512,2048]{1,0:T(8,128)(2,1)} %param.18), kind=kLoop, calls=%fused_computation.27 | loop fusion | flops 5242368 | bytes 8390656 | tf_op jit(solution)/shard_map/add | solution.py:69
  105.7 47.4 %all_to_all.40 = bf16[32,2,12,2048]{3,1,2,0:T(2,128)(2,1)S(1)} all-to-all(bf16[32,2,12,2048]{3,1,2,0:T(2,128)(2,1)S(1)} %copy.153), channel_id=1, replica_groups=mesh['ep'=32,'tp'=4] {'ep'}, dimensions={0} | all-to-all | bytes 6291456 | tf_op jit(solution)/shard_map/all_to_all | solution.py:103
  154.9 4.9 %fusion.66 = f32[32,2,12,352]{3,0,2,1:T(8,128)} fusion(bf16[2,2048,352]{1,2,0:T(8,128)(2,1)S(1)} %copy-done.15, bf16[32,2,12,2048]{3,1,2,0:T(2,128)(2,1)S(1)} %all_to_all.40), kind=kOutput, calls=%fused_computation.86 | convolution fusion | flops 1107296256 | bytes 7110656 | tf_op jit(solution)/shard_map/sjcd,jdf->sjcf/dot_general | solution.py:104
  159.8 10.3 %fusion.18 = bf16[32,2,12,2048]{3,0,2,1:T(8,128)(2,1)} fusion(bf16[2,352,2048]{2,1,0:T(8,128)(2,1)S(1)} %copy-done, bf16[2,2048,352]{1,2,0:T(8,128)(2,1)} %param.28, bf16[32,2,12,2048]{3,1,2,0:T(2,128)(2,1)} %copy-done.6, f32[32,2,12,352]{3,0,2,1:T(8,128)} %fusion.66), kind=kOutput, calls=%fused_computation.40 | convolution fusion | flops 2217787392 | bytes 13139968 | tf_op jit(solution)/shard_map/sjcf,jfd->sjcd/dot_general | solution.py:111
  170.4 3.6 convolution_convert_fusion.4
  177.2 43.6 %all_to_all.41 = bf16[32,2,12,2048]{3,1,2,0:T(2,128)(2,1)S(1)} all-to-all(bf16[32,2,12,2048]{3,1,2,0:T(2,128)(2,1)S(1)} %copy.158), channel_id=1, replica_groups=mesh['ep'=32,'tp'=4] {'ep'}, dimensions={0} | all-to-all | bytes 6291456 | tf_op jit(solution)/shard_map/all_to_all | solution.py:103
  222.5 5.0 %fusion.71 = f32[32,2,12,352]{3,0,2,1:T(8,128)} fusion(bf16[2,2048,352]{1,2,0:T(8,128)(2,1)S(1)} %copy-done.16, bf16[32,2,12,2048]{3,1,2,0:T(2,128)(2,1)S(1)} %all_to_all.41), kind=kOutput, calls=%fused_computation.87 | convolution fusion | flops 1107296256 | bytes 7110656 | tf_op jit(solution)/shard_map/sjcd,jdf->sjcf/dot_general | solution.py:104
  227.4 10.2 %fusion.19 = bf16[32,2,12,2048]{3,0,2,1:T(8,128)(2,1)} fusion(bf16[2,352,2048]{2,1,0:T(8,128)(2,1)S(1)} %copy-done, bf16[2,2048,352]{1,2,0:T(8,128)(2,1)} %param.28, bf16[32,2,12,2048]{3,1,2,0:T(2,128)(2,1)} %copy-done.7, f32[32,2,12,352]{3,0,2,1:T(8,128)} %fusion.71), kind=kOutput, calls=%fused_computation.41 | convolution fusion | flops 2217787392 | bytes 13139968 | tf_op jit(solution)/shard_map/sjcf,jfd->sjcd/dot_general | solution.py:111
  238.0 3.6 convolution_convert_fusion.8
  244.9 43.8 %all_to_all.42 = bf16[32,2,12,2048]{3,1,2,0:T(2,128)(2,1)S(1)} all-to-all(bf16[32,2,12,2048]{3,1,2,0:T(2,128)(2,1)S(1)} %copy.148), channel_id=1, replica_groups=mesh['ep'=32,'tp'=4] {'ep'}, dimensions={0} | all-to-all | bytes 6291456 | tf_op jit(solution)/shard_map/all_to_all | solution.py:103
  290.4 5.0 %fusion.61 = f32[32,2,12,352]{3,0,2,1:T(8,128)} fusion(bf16[2,2048,352]{1,2,0:T(8,128)(2,1)S(1)} %copy-done.17, bf16[32,2,12,2048]{3,1,2,0:T(2,128)(2,1)S(1)} %all_to_all.42), kind=kOutput, calls=%fused_computation.85 | convolution fusion | flops 1107296256 | bytes 7110656 | tf_op jit(solution)/shard_map/sjcd,jdf->sjcf/dot_general | solution.py:104
  295.4 10.3 %fusion.17 = bf16[32,2,12,2048]{3,0,2,1:T(8,128)(2,1)} fusion(bf16[2,352,2048]{2,1,0:T(8,128)(2,1)S(1)} %copy-done, bf16[2,2048,352]{1,2,0:T(8,128)(2,1)} %param.28, bf16[32,2,12,2048]{3,1,2,0:T(2,128)(2,1)} %copy-done.8, f32[32,2,12,352]{3,0,2,1:T(8,128)} %fusion.61), kind=kOutput, calls=%fused_computation.39 | convolution fusion | flops 2217787392 | bytes 13139968 | tf_op jit(solution)/shard_map/sjcf,jfd->sjcd/dot_general | solution.py:111
  305.9 3.4 convolution_convert_fusion.2
  312.6 43.4 %all_to_all.43 = bf16[32,2,12,2048]{3,1,2,0:T(2,128)(2,1)S(1)} all-to-all(bf16[32,2,12,2048]{3,1,2,0:T(2,128)(2,1)S(1)} %copy.163), channel_id=1, replica_groups=mesh['ep'=32,'tp'=4] {'ep'}, dimensions={0} | all-to-all | bytes 6291456 | tf_op jit(solution)/shard_map/all_to_all | solution.py:103
  357.7 5.0 %fusion.76 = f32[32,2,12,352]{3,0,2,1:T(8,128)} fusion(bf16[2,2048,352]{1,2,0:T(8,128)(2,1)S(1)} %copy-done.18, bf16[32,2,12,2048]{3,1,2,0:T(2,128)(2,1)S(1)} %all_to_all.43), kind=kOutput, calls=%fused_computation.88 | convolution fusion | flops 1107296256 | bytes 7110656 | tf_op jit(solution)/shard_map/sjcd,jdf->sjcf/dot_general | solution.py:104
  362.6 10.3 %fusion.20 = bf16[32,2,12,2048]{3,0,2,1:T(8,128)(2,1)} fusion(bf16[2,352,2048]{2,1,0:T(8,128)(2,1)S(1)} %copy-done, bf16[2,2048,352]{1,2,0:T(8,128)(2,1)} %param.28, bf16[32,2,12,2048]{3,1,2,0:T(2,128)(2,1)} %copy-done.9, f32[32,2,12,352]{3,0,2,1:T(8,128)} %fusion.76), kind=kOutput, calls=%fused_computation.42 | convolution fusion | flops 2217787392 | bytes 13139968 | tf_op jit(solution)/shard_map/sjcf,jfd->sjcd/dot_general | solution.py:111
  373.0 6.3 %fusion.180 = f32[512,896]{1,0:T(8,128)} fusion(bf16[512,2048]{1,0:T(8,128)(2,1)} %copy-done.3, bf16[2048,896]{1,0:T(8,128)(2,1)} %param.30), kind=kOutput, calls=%fused_computation.122 | convolution fusion | flops 1879048192 | bytes 7602176 | tf_op jit(solution)/shard_map/dot_general | solution.py:75
  382.2 4.9 all-to-all-start.3
  387.1 10.3 %convolution_convert_fusion.9 = bf16[512,2048]{1,0:T(8,128)(2,1)} fusion(bf16[896,2048]{1,0:T(8,128)(2,1)} %param.32, f32[512,896]{1,0:T(8,128)} %fusion.180, bf16[512,2048]{1,0:T(8,128)(2,1)} %copy-done.3, bf16[2048,896]{1,0:T(8,128)(2,1)} %param.31), kind=kOutput, calls=%fused_computation.38 | convolution fusion | flops 3761897472 | bytes 13369344 | tf_op jit(solution)/shard_map/dot_general | solution.py:78
  401.6 6.1 %all-to-all-start.5 = ((bf16[32,2,12,512]{3,1,2,0:T(2,128)(2,1)}), bf16[32,2,12,512]{3,1,2,0:T(2,128)(2,1)}, u32[]{:S(2)}, u32[]{:S(2)}) async-start(bf16[32,2,12,512]{3,1,2,0:T(2,128)(2,1)} %copy.161), calls=%async_computation.9 | async-start | bytes 1572864 | tf_op jit(solution)/shard_map/all_to_all | solution.py:117
  410.6 11.6 %all-to-all-done.5 = bf16[32,2,12,512]{3,1,2,0:T(2,128)(2,1)} async-done(((bf16[32,2,12,512]{3,1,2,0:T(2,128)(2,1)}), bf16[32,2,12,512]{3,1,2,0:T(2,128)(2,1)}, u32[]{:S(2)}, u32[]{:S(2)}) %all-to-all-start.5) | async-done | bytes 786464 | tf_op jit(solution)/shard_map/all_to_all | solution.py:117
  422.2 4.6 all-to-all-start.1
  429.7 11.6 %all-to-all-done.1 = bf16[32,2,12,512]{3,1,2,0:T(2,128)(2,1)} async-done(((bf16[32,2,12,512]{3,1,2,0:T(2,128)(2,1)}), bf16[32,2,12,512]{3,1,2,0:T(2,128)(2,1)}, u32[]{:S(2)}, u32[]{:S(2)}) %all-to-all-start.1) | async-done | bytes 786464 | tf_op jit(solution)/shard_map/all_to_all | solution.py:117
  441.4 4.9 %all-to-all-start.7 = ((bf16[32,2,12,512]{3,1,2,0:T(2,128)(2,1)}), bf16[32,2,12,512]{3,1,2,0:T(2,128)(2,1)}, u32[]{:S(2)}, u32[]{:S(2)}) async-start(bf16[32,2,12,512]{3,1,2,0:T(2,128)(2,1)} %copy.166), calls=%async_computation.12 | async-start | bytes 1572864 | tf_op jit(solution)/shard_map/all_to_all | solution.py:117
  446.3 8.4 %select_reduce_fusion = f32[512,3072]{1,0:T(8,128)} fusion(f32[512,4]{0,1:T(4,128)S(1)} %copy-done.13, s32[512,4]{0,1:T(4,128)S(1)} %multiply_add_fusion), kind=kLoop, calls=%fused_computation.19 | loop fusion | flops 17301504 | bytes 6307840 | tf_op jit(solution)/shard_map/reduce_sum | solution.py:121
  472.7 7.0 %fusion.147 = bf16[512,512]{1,0:T(8,128)(2,1)} fusion(f32[512,512]{1,0:T(8,128)} %fusion.16, bf16[3072,512]{1,0:T(8,128)(2,1)} %bitcast.189, f32[512,3072]{1,0:T(8,128)} %select_reduce_fusion, bf16[512,512]{1,0:T(8,128)(2,1)} %reduce-scatter.6.cloned.1.call-done, f32[512,2048]{1,0:T(8,128)} %get-tuple-element.97, s32[]{:T(128)S(6)} %select_n.15, ...), kind=kOutput, calls=%fused_computation.103 | convolution fusion | flops 1613758464 | bytes 12584964 | tf_op jit(solution)/shard_map/dot_general | solution.py:124
  (110 shorter events, 79.2 us)
Async XLA Ops:
  6.5 153.3 %copy-start = (bf16[2,352,2048]{2,1,0:T(8,128)(2,1)S(1)}, bf16[2,352,2048]{2,1,0:T(8,128)(2,1)}, u32[]{:S(2)}) copy-start(bf16[2,352,2048]{2,1,0:T(8,128)(2,1)} %param.29) | copy-start | bytes 8650756
  6.5 6.3 %copy-start.19 = (s32[1,512]{1,0:T(1,128)S(1)}, s32[1,512]{1,0:T(1,128)}, u32[]{:S(2)}) copy-start(s32[1,512]{1,0:T(1,128)} %param.22) | copy-start | bytes 6148
  6.5 86.5 %all-reduce.2.cloned.1.call-start = ((), (), s32[]{:S(2)}) async-start(), calls=%async_computation.13 | async-start | bytes 4194304 | tf_op jit(solution)/shard_map/psum | solution.py:69
  27.4 4.7 copy-start.11
  31.8 347.5 %reduce-scatter.10.cloned.1.call-start = ((), (), s32[]{:S(2)}) async-start(), calls=%async_computation.16 | async-start | bytes 3932160 | tf_op jit(solution)/shard_map/reduce_scatter | solution.py:114
  51.2 46.9 %copy-start.12 = (f32[2048]{0:T(1024)S(1)}, f32[2048]{0:T(1024)}, u32[]{:S(2)}) copy-start(f32[2048]{0:T(1024)} %param.26) | copy-start | bytes 24580
  93.1 5.0 %copy-start.1 = (bf16[512,2048]{1,0:T(8,128)(2,1)S(1)}, bf16[512,2048]{1,0:T(8,128)(2,1)}, u32[]{:S(2)}) copy-start(bf16[512,2048]{1,0:T(8,128)(2,1)} %param.18) | copy-start | bytes 6291460
  93.1 5.0 %copy-start.2 = (bf16[512,2048]{1,0:T(8,128)(2,1)S(1)}, bf16[512,2048]{1,0:T(8,128)(2,1)}, u32[]{:S(2)}) copy-start(bf16[512,2048]{1,0:T(8,128)(2,1)} %all-reduce.2.cloned.1.call-done) | copy-start | bytes 6291460
  98.1 2.5 copy-start.10
  99.3 1.3 copy-start.3
  105.7 49.2 %copy-start.15 = (bf16[2,2048,352]{1,2,0:T(8,128)(2,1)S(1)}, bf16[2,2048,352]{1,2,0:T(8,128)(2,1)}, u32[]{:S(2)}) copy-start(bf16[2,2048,352]{1,2,0:T(8,128)(2,1)} %param.27) | copy-start | bytes 8650756
  153.1 1.8 copy-start.6
  170.1 227.3 %reduce-scatter.12.cloned.1.call-start = ((), (), s32[]{:S(2)}) async-start(), calls=%async_computation.17 | async-start | bytes 3932160 | tf_op jit(solution)/shard_map/reduce_scatter | solution.py:114
  177.2 45.3 %copy-start.16 = (bf16[2,2048,352]{1,2,0:T(8,128)(2,1)S(1)}, bf16[2,2048,352]{1,2,0:T(8,128)(2,1)}, u32[]{:S(2)}) copy-start(bf16[2,2048,352]{1,2,0:T(8,128)(2,1)} %param.27) | copy-start | bytes 8650756
  220.8 1.6 copy-start.7
  237.7 170.0 %reduce-scatter.8.cloned.1.call-start = ((), (), s32[]{:S(2)}) async-start(), calls=%async_computation.15 | async-start | bytes 3932160 | tf_op jit(solution)/shard_map/reduce_scatter | solution.py:114
  244.8 45.6 %copy-start.17 = (bf16[2,2048,352]{1,2,0:T(8,128)(2,1)S(1)}, bf16[2,2048,352]{1,2,0:T(8,128)(2,1)}, u32[]{:S(2)}) copy-start(bf16[2,2048,352]{1,2,0:T(8,128)(2,1)} %param.27) | copy-start | bytes 8650756
  288.7 1.7 copy-start.8
  305.7 121.2 %reduce-scatter.14.cloned.1.call-start = ((), (), s32[]{:S(2)}) async-start(), calls=%async_computation.18 | async-start | bytes 3932160 | tf_op jit(solution)/shard_map/reduce_scatter | solution.py:114
  312.6 45.1 %copy-start.18 = (bf16[2,2048,352]{1,2,0:T(8,128)(2,1)S(1)}, bf16[2,2048,352]{1,2,0:T(8,128)(2,1)}, u32[]{:S(2)}) copy-start(bf16[2,2048,352]{1,2,0:T(8,128)(2,1)} %param.27) | copy-start | bytes 8650756
  355.9 1.7 copy-start.9
  382.2 19.4 %all-to-all-start.3 = ((bf16[32,2,12,512]{3,1,2,0:T(2,128)(2,1)}), bf16[32,2,12,512]{3,1,2,0:T(2,128)(2,1)}, u32[]{:S(2)}, u32[]{:S(2)}) async-start(bf16[32,2,12,512]{3,1,2,0:T(2,128)(2,1)} %copy.156), calls=%async_computation.6 | async-start | bytes 1572864 | tf_op jit(solution)/shard_map/all_to_all | solution.py:117
  387.1 85.6 %reduce-scatter.6.cloned.1.call-start = ((), (), s32[]{:S(2)}) async-start(), calls=%async_computation.14 | async-start | bytes 2621440 | tf_op jit(solution)/shard_map/reduce_scatter | solution.py:79
  401.6 20.6 %all-to-all-start.5 = ((bf16[32,2,12,512]{3,1,2,0:T(2,128)(2,1)}), bf16[32,2,12,512]{3,1,2,0:T(2,128)(2,1)}, u32[]{:S(2)}, u32[]{:S(2)}) async-start(bf16[32,2,12,512]{3,1,2,0:T(2,128)(2,1)} %copy.161), calls=%async_computation.9 | async-start | bytes 1572864 | tf_op jit(solution)/shard_map/all_to_all | solution.py:117
  407.7 38.6 %copy-start.13 = (f32[512,4]{0,1:T(4,128)S(1)}, f32[512,4]{0,1:T(4,128)}, u32[]{:S(2)}) copy-start(f32[512,4]{0,1:T(4,128)} %param.24) | copy-start | bytes 24580
  422.2 19.1 %all-to-all-start.1 = ((bf16[32,2,12,512]{3,1,2,0:T(2,128)(2,1)}), bf16[32,2,12,512]{3,1,2,0:T(2,128)(2,1)}, u32[]{:S(2)}, u32[]{:S(2)}) async-start(bf16[32,2,12,512]{3,1,2,0:T(2,128)(2,1)} %copy.151), calls=%async_computation.3 | async-start | bytes 1572864 | tf_op jit(solution)/shard_map/all_to_all | solution.py:117
  441.4 22.6 %all-to-all-start.7 = ((bf16[32,2,12,512]{3,1,2,0:T(2,128)(2,1)}), bf16[32,2,12,512]{3,1,2,0:T(2,128)(2,1)}, u32[]{:S(2)}, u32[]{:S(2)}) async-start(bf16[32,2,12,512]{3,1,2,0:T(2,128)(2,1)} %copy.166), calls=%async_computation.12 | async-start | bytes 1572864 | tf_op jit(solution)/shard_map/all_to_all | solution.py:117
  446.3 8.4 %copy-start.14 = (bf16[2048]{0:T(1024)(128)(2,1)S(1)}, bf16[2048]{0:T(1024)(128)(2,1)}, u32[]{:S(2)}) copy-start(bf16[2048]{0:T(1024)(128)(2,1)} %param.33) | copy-start | bytes 12292
  465.3 4.6 copy-start.4
  468.3 1.6 copy-start.5
Sparse Core Ops, SparseCore 0:
  31.9 61.1 all-reduce.1
  170.3 34.4 reduce-scatter.9
  237.8 34.4 reduce-scatter.11
  305.8 34.4 reduce-scatter.7
  373.1 34.5 reduce-scatter.13
  409.9 29.4 reduce-scatter.5

commit v3 on v2

--- a/solution.py
+++ b/solution.py
@@ -91,22 +91,18 @@
     slot_ids = jnp.arange(experts * capacity, dtype=jnp.int32)
     hits = slot[:, :, None] == slot_ids[None, None, :]
     chosen = jnp.any(hits, axis=1).T.astype(jnp.bfloat16)
-    chosen = chosen.reshape(ep_count, local_experts, capacity, length)
+    outgoing = jnp.dot(chosen, normed, preferred_element_type=jnp.float32).astype(jnp.bfloat16)
+    outgoing = outgoing.reshape(ep_count, local_experts, capacity, width)
+    incoming = lax.all_to_all(outgoing, "ep", split_axis=0, concat_axis=0, tiled=True)
     chunks = 4 if capacity % 4 == 0 else 1
     step = capacity // chunks
     pieces = []
     for index in range(chunks):
-        picks_of = chosen[:, :, index * step : (index + 1) * step]
-        outgoing = jnp.einsum(
-            "sjct,td->sjcd", picks_of, normed, preferred_element_type=jnp.float32
-        ).astype(jnp.bfloat16)
-        incoming = lax.all_to_all(outgoing, "ep", split_axis=0, concat_axis=0, tiled=True)
+        rows = incoming[:, :, index * step : (index + 1) * step]
         gate_rows = jnp.einsum(
-            "sjcd,jdf->sjcf", incoming, expert_gate, preferred_element_type=jnp.float32
+            "sjcd,jdf->sjcf", rows, expert_gate, preferred_element_type=jnp.float32
         )
-        up_rows = jnp.einsum(
-            "sjcd,jdf->sjcf", incoming, expert_up, preferred_element_type=jnp.float32
-        )
+        up_rows = jnp.einsum("sjcd,jdf->sjcf", rows, expert_up, preferred_element_type=jnp.float32)
         expert_hidden = (jax.nn.silu(gate_rows) * up_rows).astype(jnp.bfloat16)
         expert_part = jnp.einsum(
             "sjcf,jfd->sjcd", expert_hidden, expert_down, preferred_element_type=jnp.float32

time: 492 us -> 492 us (level)
  waiting for transfers between devices: 66.6 us -> 114 us
  blocking collectives: 178 us -> 148 us
  local copies, waits for them, and re-layouts: 61 us -> 39.5 us
  starting transfers between devices: 21.5 us -> 28.5 us
    reduce_scatter x4, waiting for transfers between devices: 0.06 us -> 63.5 us  [on_device(): lax.psum_scatter(expert_part.astype(jnp.bfloat16), 'tp', scatter_dimensio...]
    all_to_all x4 -> x1, blocking collectives: 178 us -> 148 us  [on_device(): lax.all_to_all(outgoing, 'ep', split_axis=0, concat_axis=0, tiled=True)]
    all_to_all x4, waiting for transfers between devices: 24.5 us -> 0.01 us  [on_device(): lax.all_to_all(expert_cols, 'ep', split_axis=0, concat_axis=0, tiled=True)]
    convert_element_type x4 -> x0, local copies, waits for them, and re-layouts: 13 us -> none  [on_device(): outgoing = jnp.einsum('sjct,td->sjcd', picks_of, normed, preferred_elemen...]
    psum x1, waiting for transfers between devices: 41.9 us -> 50.1 us  [on_device(): lax.psum(partial_value.astype(jnp.bfloat16), 'tp').astype(jnp.float32)]
    unnamed x45 -> x29, local copies, waits for them, and re-layouts: 16.3 us -> 8.54 us
    all_to_all x4, starting transfers between devices: 20.5 us -> 27.1 us  [on_device(): lax.all_to_all(expert_cols, 'ep', split_axis=0, concat_axis=0, tiled=True)]
    dot_general x4, matrix products: 41.1 us -> 36.1 us  [on_device(): jnp.einsum('sjcf,jfd->sjcd', expert_hidden, expert_down, preferred_elemen...]
  transfers between devices with their start and end apart: 10 -> 10, of which waited for: 4 -> 4; matrix products, arithmetic and copies ran while one was open for 28% -> 23% of each run, Pallas kernels for 0% -> 0%
where the time goes in v3:
time: 492 us; the launch traced here: 487 us
  blocking collectives  148 us (30%)
  matrix products  116 us (24%)
  waiting for transfers between devices  114 us (23%)
  local copies, waits for them, and re-layouts  39.5 us (8%)
  starting transfers between devices  28.5 us (6%)
  other arithmetic  26.9 us (5%)
  between operations  13.9 us (3%)
    all_to_all x1, blocking collectives, on_device(): lax.all_to_all(outgoing, 'ep', split_axis=0, concat_axis=0, tiled=True)  148 us
    reduce_scatter x4, waiting for transfers between devices, on_device(): lax.psum_scatter(expert_part.astype(jnp.bfloat16), 'tp', scatter_dimensio...  63.5 us
    psum x1, waiting for transfers between devices, on_device(): lax.psum(partial_value.astype(jnp.bfloat16), 'tp').astype(jnp.float32)  50.1 us
    dot_general x4, matrix products, on_device(): jnp.einsum('sjcf,jfd->sjcd', expert_hidden, expert_down, preferred_elemen...  36.1 us
    all_to_all x4, starting transfers between devices, on_device(): lax.all_to_all(expert_cols, 'ep', split_axis=0, concat_axis=0, tiled=True)  27.1 us
    dot_general x4, matrix products, on_device(): jnp.einsum('sjcd,jdf->sjcf', rows, expert_gate, preferred_element_type=jn...  25.4 us
    reduce_scatter x4, local copies, waits for them, and re-layouts, on_device(): lax.psum_scatter(expert_part.astype(jnp.bfloat16), 'tp', scatter_dimensio...  11.4 us
    dot_general x1, matrix products, on_device(): jnp.dot(shared_hidden, shared_down, preferred_element_type=jnp.float32)  10.3 us
  transfers between devices with their start and end apart: 10, of which 4 were waited for; matrix products, arithmetic and copies ran while one was open for 23% of the time, Pallas kernels for 0%

profile of v3, /device:TPU:0, one launch (start us, length us, event | category | flops | bytes accessed | tf_op | source)
XLA Modules:
  0.0 487.1 jit_solution(6363947200590720669)
XLA Ops:
  12.9 14.5 %while.11 = (s32[]{:T(128)}, bf16[4,512,128]{1,2,0:T(8,128)(2,1)}, bf16[4,512,128]{1,2,0:T(8,128)(2,1)}, bf16[4,512,128]{1,2,0:T(8,128)(2,1)}, bf16[4,512,128]{1,2,0:T(8,128)(2,1)}, /*index=5*/s32[512]{0:T(512)S(1)}, s32[]{:T(128)}) while((s32[]{:T(128)}, bf16[4,512,128]{1,2,0:T(8,128)(2,1)}, bf16[4,512,128]{1,2,0:T(8,128)(2,1)}, ...), condition=%wide.region_3.4_spmd.clone, body=%wide.region_0.3_spmd.clone.sunk | while | flops 137165824 | bytes 4210765 | solution.py:42
  27.3 4.4 convolution_convert_fusion.7
  34.3 8.6 %fusion.14 = pred[512,3072]{1,0:T(8,128)(4,1)} fusion(s32[512,4]{0,1:T(4,128)S(1)} %multiply_add_fusion), kind=kLoop, calls=%fused_computation.21 | loop fusion | flops 11010048 | bytes 1581056 | tf_op jit(solution)/shard_map/reduce_or | solution.py:93
  42.9 50.1 %all-reduce.2.cloned.1.call-done = bf16[512,2048]{1,0:T(8,128)(2,1)} async-done(((bf16[512,2048]{1,0:T(8,128)(2,1)}), bf16[512,2048]{1,0:T(8,128)(2,1)}) %all-reduce.2.cloned.1.call-update) | async-done | bytes 2097168 | tf_op jit(solution)/shard_map/psum | solution.py:69
  93.1 5.0 %convert_add_fusion = (f32[512,2048]{1,0:T(8,128)}, f32[512]{0:T(512)S(1)}) fusion(bf16[512,2048]{1,0:T(8,128)(2,1)} %all-reduce.2.cloned.1.call-done, bf16[512,2048]{1,0:T(8,128)(2,1)} %param.18), kind=kLoop, calls=%fused_computation.28 | loop fusion | flops 5242368 | bytes 8390656 | tf_op jit(solution)/shard_map/add | solution.py:69
  99.5 9.9 %convolution_convert_fusion.1 = bf16[3072,2048]{1,0:T(8,128)(2,1)} fusion(pred[512,3072]{1,0:T(8,128)(4,1)S(1)} %copy-done.6, bf16[512,2048]{1,0:T(8,128)(2,1)S(1)} %multiply_convert_fusion), kind=kOutput, calls=%fused_computation.24 | convolution fusion | flops 6448742400 | bytes 16252928 | tf_op jit(solution)/shard_map/dot_general | solution.py:94
  109.3 148.0 %all_to_all.25 = bf16[32,2,48,2048]{3,2,1,0:T(8,128)(2,1)S(1)} all-to-all(bf16[32,2,48,2048]{3,2,1,0:T(8,128)(2,1)} %bitcast.176), channel_id=1, replica_groups=mesh['ep'=32,'tp'=4] {'ep'}, dimensions={0} | all-to-all | bytes 25165824 | tf_op jit(solution)/shard_map/all_to_all | solution.py:96
  257.4 7.5 %fusion.170 = (bf16[32,2,12,2048]{3,2,1,0:T(8,128)(2,1)}, bf16[32,2,12,2048]{3,2,1,0:T(8,128)(2,1)}, bf16[32,2,12,2048]{3,2,1,0:T(8,128)(2,1)}, bf16[32,2,12,2048]{3,2,1,0:T(8,128)(2,1)}) fusion(bf16[32,2,48,2048]{3,2,1,0:T(8,128)(2,1)S(1)} %all_to_all.25), kind=kLoop, calls=%fused_computation.109 | loop fusion | bytes 25165824 | tf_op jit(solution)/shard_map/slice | solution.py:101
  264.8 6.3 %fusion.53 = f32[32,2,12,352]{3,0,2,1:T(8,128)} fusion(bf16[2,2048,352]{1,2,0:T(8,128)(2,1)} %param.27, bf16[32,2,12,2048]{3,2,1,0:T(8,128)(2,1)} %get-tuple-element.97), kind=kOutput, calls=%fused_computation.74 | convolution fusion | flops 1107296256 | bytes 7110656 | tf_op jit(solution)/shard_map/sjcd,jdf->sjcf/dot_general | solution.py:102
  271.1 9.0 %fusion.17 = bf16[32,2,12,2048]{3,0,2,1:T(8,128)(2,1)} fusion(bf16[2,352,2048]{2,1,0:T(8,128)(2,1)S(1)} %copy-done, bf16[2,2048,352]{1,2,0:T(8,128)(2,1)} %param.28, bf16[32,2,12,2048]{3,2,1,0:T(8,128)(2,1)} %get-tuple-element.97, f32[32,2,12,352]{3,0,2,1:T(8,128)} %fusion.53), kind=kOutput, calls=%fused_computation.36 | convolution fusion | flops 2217787392 | bytes 13139968 | tf_op jit(solution)/shard_map/sjcf,jfd->sjcd/dot_general | solution.py:107
  280.5 6.3 %fusion.58 = f32[32,2,12,352]{3,0,2,1:T(8,128)} fusion(bf16[2,2048,352]{1,2,0:T(8,128)(2,1)} %param.27, bf16[32,2,12,2048]{3,2,1,0:T(8,128)(2,1)} %get-tuple-element.99), kind=kOutput, calls=%fused_computation.75 | convolution fusion | flops 1107296256 | bytes 7110656 | tf_op jit(solution)/shard_map/sjcd,jdf->sjcf/dot_general | solution.py:102
  286.8 9.0 %fusion.18 = bf16[32,2,12,2048]{3,0,2,1:T(8,128)(2,1)} fusion(bf16[2,352,2048]{2,1,0:T(8,128)(2,1)S(1)} %copy-done, bf16[2,2048,352]{1,2,0:T(8,128)(2,1)} %param.28, bf16[32,2,12,2048]{3,2,1,0:T(8,128)(2,1)} %get-tuple-element.99, f32[32,2,12,352]{3,0,2,1:T(8,128)} %fusion.58), kind=kOutput, calls=%fused_computation.37 | convolution fusion | flops 2217787392 | bytes 13139968 | tf_op jit(solution)/shard_map/sjcf,jfd->sjcd/dot_general | solution.py:107
  296.3 6.4 %fusion.63 = f32[32,2,12,352]{3,0,2,1:T(8,128)} fusion(bf16[2,2048,352]{1,2,0:T(8,128)(2,1)} %param.27, bf16[32,2,12,2048]{3,2,1,0:T(8,128)(2,1)} %get-tuple-element.98), kind=kOutput, calls=%fused_computation.76 | convolution fusion | flops 1107296256 | bytes 7110656 | tf_op jit(solution)/shard_map/sjcd,jdf->sjcf/dot_general | solution.py:102
  302.7 9.1 %fusion.19 = bf16[32,2,12,2048]{3,0,2,1:T(8,128)(2,1)} fusion(bf16[2,352,2048]{2,1,0:T(8,128)(2,1)S(1)} %copy-done, bf16[2,2048,352]{1,2,0:T(8,128)(2,1)} %param.28, bf16[32,2,12,2048]{3,2,1,0:T(8,128)(2,1)} %get-tuple-element.98, f32[32,2,12,352]{3,0,2,1:T(8,128)} %fusion.63), kind=kOutput, calls=%fused_computation.38 | convolution fusion | flops 2217787392 | bytes 13139968 | tf_op jit(solution)/shard_map/sjcf,jfd->sjcd/dot_general | solution.py:107
  312.0 6.4 %fusion.68 = f32[32,2,12,352]{3,0,2,1:T(8,128)} fusion(bf16[2,2048,352]{1,2,0:T(8,128)(2,1)} %param.27, bf16[32,2,12,2048]{3,2,1,0:T(8,128)(2,1)} %get-tuple-element.100), kind=kOutput, calls=%fused_computation.77 | convolution fusion | flops 1107296256 | bytes 7110656 | tf_op jit(solution)/shard_map/sjcd,jdf->sjcf/dot_general | solution.py:102
  318.4 9.0 %fusion.20 = bf16[32,2,12,2048]{3,0,2,1:T(8,128)(2,1)} fusion(bf16[2,352,2048]{2,1,0:T(8,128)(2,1)S(1)} %copy-done, bf16[2,2048,352]{1,2,0:T(8,128)(2,1)} %param.28, bf16[32,2,12,2048]{3,2,1,0:T(8,128)(2,1)} %get-tuple-element.100, f32[32,2,12,352]{3,0,2,1:T(8,128)} %fusion.68), kind=kOutput, calls=%fused_computation.39 | convolution fusion | flops 2217787392 | bytes 13139968 | tf_op jit(solution)/shard_map/sjcf,jfd->sjcd/dot_general | solution.py:107
  327.5 6.2 %fusion.172 = f32[512,896]{1,0:T(8,128)} fusion(bf16[512,2048]{1,0:T(8,128)(2,1)} %copy-done.3, bf16[2048,896]{1,0:T(8,128)(2,1)} %param.30), kind=kOutput, calls=%fused_computation.111 | convolution fusion | flops 1879048192 | bytes 7602176 | tf_op jit(solution)/shard_map/dot_general | solution.py:75
  333.7 2.9 copy.108
  336.6 4.8 all-to-all-start.1
  341.6 10.3 %convolution_convert_fusion.6 = bf16[512,2048]{1,0:T(8,128)(2,1)} fusion(bf16[896,2048]{1,0:T(8,128)(2,1)} %param.32, f32[512,896]{1,0:T(8,128)} %fusion.172, bf16[512,2048]{1,0:T(8,128)(2,1)} %copy-done.3, bf16[2048,896]{1,0:T(8,128)(2,1)} %param.31), kind=kOutput, calls=%fused_computation.35 | convolution fusion | flops 3761897472 | bytes 13369344 | tf_op jit(solution)/shard_map/dot_general | solution.py:78
  351.9 3.3 reduce-scatter.10.cloned.1.call-done
  355.3 2.8 copy.110
  358.1 7.3 %all-to-all-start.2 = ((bf16[32,2,12,512]{3,1,2,0:T(2,128)(2,1)}), bf16[32,2,12,512]{3,1,2,0:T(2,128)(2,1)}, u32[]{:S(2)}, u32[]{:S(2)}) async-start(bf16[32,2,12,512]{3,1,2,0:T(2,128)(2,1)} %copy.110), calls=%async_computation.5 | async-start | bytes 1572864 | tf_op jit(solution)/shard_map/all_to_all | solution.py:113
  365.5 30.1 %reduce-scatter.12.cloned.1.call-done = bf16[32,2,12,512]{3,0,2,1:T(8,128)(2,1)} async-done(((bf16[32,2,12,2048]{3,0,2,1:T(8,128)(2,1)}), bf16[32,2,12,512]{3,0,2,1:T(8,128)(2,1)}) %reduce-scatter.12.cloned.1.call-update) | async-done | bytes 786448 | tf_op jit(solution)/shard_map/reduce_scatter | solution.py:110
  395.6 2.8 copy.112
  398.4 7.3 %all-to-all-start.3 = ((bf16[32,2,12,512]{3,1,2,0:T(2,128)(2,1)}), bf16[32,2,12,512]{3,1,2,0:T(2,128)(2,1)}, u32[]{:S(2)}, u32[]{:S(2)}) async-start(bf16[32,2,12,512]{3,1,2,0:T(2,128)(2,1)} %copy.112), calls=%async_computation.7 | async-start | bytes 1572864 | tf_op jit(solution)/shard_map/all_to_all | solution.py:113
  405.8 30.1 %reduce-scatter.14.cloned.1.call-done = bf16[32,2,12,512]{3,0,2,1:T(8,128)(2,1)} async-done(((bf16[32,2,12,2048]{3,0,2,1:T(8,128)(2,1)}), bf16[32,2,12,512]{3,0,2,1:T(8,128)(2,1)}) %reduce-scatter.14.cloned.1.call-update) | async-done | bytes 786448 | tf_op jit(solution)/shard_map/reduce_scatter | solution.py:110
  435.9 2.8 copy.114
  438.7 7.6 %all-to-all-start.4 = ((bf16[32,2,12,512]{3,1,2,0:T(2,128)(2,1)}), bf16[32,2,12,512]{3,1,2,0:T(2,128)(2,1)}, u32[]{:S(2)}, u32[]{:S(2)}) async-start(bf16[32,2,12,512]{3,1,2,0:T(2,128)(2,1)} %copy.114), calls=%async_computation.9 | async-start | bytes 1572864 | tf_op jit(solution)/shard_map/all_to_all | solution.py:113
  446.4 8.4 %select_reduce_fusion = f32[512,3072]{1,0:T(8,128)} fusion(f32[512,4]{0,1:T(4,128)S(1)} %copy-done.9, s32[512,4]{0,1:T(4,128)S(1)} %multiply_add_fusion), kind=kLoop, calls=%fused_computation.19 | loop fusion | flops 17301504 | bytes 6307840 | tf_op jit(solution)/shard_map/reduce_sum | solution.py:117
  465.6 3.0 pad_maximum_fusion
  473.0 7.0 %fusion.139 = bf16[512,512]{1,0:T(8,128)(2,1)} fusion(f32[512,512]{1,0:T(8,128)} %fusion.16, bf16[3072,512]{1,0:T(8,128)(2,1)} %bitcast.178, f32[512,3072]{1,0:T(8,128)} %select_reduce_fusion, bf16[512,512]{1,0:T(8,128)(2,1)} %reduce-scatter.6.cloned.1.call-done, f32[512,2048]{1,0:T(8,128)} %get-tuple-element.101, s32[]{:T(128)S(6)} %select_n.15, ...), kind=kOutput, calls=%fused_computation.92 | convolution fusion | flops 1613758464 | bytes 12584964 | tf_op jit(solution)/shard_map/dot_general | solution.py:120
  (83 shorter events, 41.3 us)
Async XLA Ops:
  6.5 264.6 %copy-start = (bf16[2,352,2048]{2,1,0:T(8,128)(2,1)S(1)}, bf16[2,352,2048]{2,1,0:T(8,128)(2,1)}, u32[]{:S(2)}) copy-start(bf16[2,352,2048]{2,1,0:T(8,128)(2,1)} %param.29) | copy-start | bytes 8650756
  6.5 6.3 %copy-start.11 = (s32[1,512]{1,0:T(1,128)S(1)}, s32[1,512]{1,0:T(1,128)}, u32[]{:S(2)}) copy-start(s32[1,512]{1,0:T(1,128)} %param.22) | copy-start | bytes 6148
  6.5 86.5 %all-reduce.2.cloned.1.call-start = ((), (), s32[]{:S(2)}) async-start(), calls=%async_computation.10 | async-start | bytes 4194304 | tf_op jit(solution)/shard_map/psum | solution.py:69
  27.3 4.6 copy-start.7
  31.7 302.0 %reduce-scatter.8.cloned.1.call-start = ((), (), s32[]{:S(2)}) async-start(), calls=%async_computation.12 | async-start | bytes 3932160 | tf_op jit(solution)/shard_map/reduce_scatter | solution.py:110
  42.9 55.1 %copy-start.8 = (f32[2048]{0:T(1024)S(1)}, f32[2048]{0:T(1024)}, u32[]{:S(2)}) copy-start(f32[2048]{0:T(1024)} %param.26) | copy-start | bytes 24580
  93.1 5.0 %copy-start.1 = (bf16[512,2048]{1,0:T(8,128)(2,1)S(1)}, bf16[512,2048]{1,0:T(8,128)(2,1)}, u32[]{:S(2)}) copy-start(bf16[512,2048]{1,0:T(8,128)(2,1)} %param.18) | copy-start | bytes 6291460
  93.1 5.0 %copy-start.2 = (bf16[512,2048]{1,0:T(8,128)(2,1)S(1)}, bf16[512,2048]{1,0:T(8,128)(2,1)}, u32[]{:S(2)}) copy-start(bf16[512,2048]{1,0:T(8,128)(2,1)} %all-reduce.2.cloned.1.call-done) | copy-start | bytes 6291460
  98.1 1.4 copy-start.6
  99.5 9.9 %copy-start.3 = (bf16[512,2048]{1,0:T(8,128)(2,1)}, bf16[512,2048]{1,0:T(8,128)(2,1)S(1)}, u32[]{:S(2)}) copy-start(bf16[512,2048]{1,0:T(8,128)(2,1)S(1)} %multiply_convert_fusion) | copy-start | bytes 6291460
  280.2 75.1 %reduce-scatter.10.cloned.1.call-start = ((), (), s32[]{:S(2)}) async-start(), calls=%async_computation.13 | async-start | bytes 3932160 | tf_op jit(solution)/shard_map/reduce_scatter | solution.py:110
  295.8 99.8 %reduce-scatter.12.cloned.1.call-start = ((), (), s32[]{:S(2)}) async-start(), calls=%async_computation.14 | async-start | bytes 3932160 | tf_op jit(solution)/shard_map/reduce_scatter | solution.py:110
  311.8 124.1 %reduce-scatter.14.cloned.1.call-start = ((), (), s32[]{:S(2)}) async-start(), calls=%async_computation.15 | async-start | bytes 3932160 | tf_op jit(solution)/shard_map/reduce_scatter | solution.py:110
  336.6 21.6 %all-to-all-start.1 = ((bf16[32,2,12,512]{3,1,2,0:T(2,128)(2,1)}), bf16[32,2,12,512]{3,1,2,0:T(2,128)(2,1)}, u32[]{:S(2)}, u32[]{:S(2)}) async-start(bf16[32,2,12,512]{3,1,2,0:T(2,128)(2,1)} %copy.108), calls=%async_computation.3 | async-start | bytes 1572864 | tf_op jit(solution)/shard_map/all_to_all | solution.py:113
  341.4 131.7 %reduce-scatter.6.cloned.1.call-start = ((), (), s32[]{:S(2)}) async-start(), calls=%async_computation.11 | async-start | bytes 2621440 | tf_op jit(solution)/shard_map/reduce_scatter | solution.py:79
  358.1 40.3 %all-to-all-start.2 = ((bf16[32,2,12,512]{3,1,2,0:T(2,128)(2,1)}), bf16[32,2,12,512]{3,1,2,0:T(2,128)(2,1)}, u32[]{:S(2)}, u32[]{:S(2)}) async-start(bf16[32,2,12,512]{3,1,2,0:T(2,128)(2,1)} %copy.110), calls=%async_computation.5 | async-start | bytes 1572864 | tf_op jit(solution)/shard_map/all_to_all | solution.py:113
  365.5 80.9 %copy-start.9 = (f32[512,4]{0,1:T(4,128)S(1)}, f32[512,4]{0,1:T(4,128)}, u32[]{:S(2)}) copy-start(f32[512,4]{0,1:T(4,128)} %param.24) | copy-start | bytes 24580
  398.4 40.3 %all-to-all-start.3 = ((bf16[32,2,12,512]{3,1,2,0:T(2,128)(2,1)}), bf16[32,2,12,512]{3,1,2,0:T(2,128)(2,1)}, u32[]{:S(2)}, u32[]{:S(2)}) async-start(bf16[32,2,12,512]{3,1,2,0:T(2,128)(2,1)} %copy.112), calls=%async_computation.7 | async-start | bytes 1572864 | tf_op jit(solution)/shard_map/all_to_all | solution.py:113
  438.7 25.5 %all-to-all-start.4 = ((bf16[32,2,12,512]{3,1,2,0:T(2,128)(2,1)}), bf16[32,2,12,512]{3,1,2,0:T(2,128)(2,1)}, u32[]{:S(2)}, u32[]{:S(2)}) async-start(bf16[32,2,12,512]{3,1,2,0:T(2,128)(2,1)} %copy.114), calls=%async_computation.9 | async-start | bytes 1572864 | tf_op jit(solution)/shard_map/all_to_all | solution.py:113
  446.3 8.5 %copy-start.10 = (bf16[2048]{0:T(1024)(128)(2,1)S(1)}, bf16[2048]{0:T(1024)(128)(2,1)}, u32[]{:S(2)}) copy-start(bf16[2048]{0:T(1024)(128)(2,1)} %param.33) | copy-start | bytes 12292
  465.6 4.7 copy-start.4
  468.6 1.7 copy-start.5
Sparse Core Ops, SparseCore 0:
  31.8 61.1 all-reduce.1
  280.3 34.5 reduce-scatter.7
  317.3 37.9 reduce-scatter.9
  357.5 37.9 reduce-scatter.11
  397.8 37.9 reduce-scatter.13
  438.1 29.4 reduce-scatter.5

commit v4 on v1

--- a/solution.py
+++ b/solution.py
@@ -24,23 +24,18 @@
     heads = query_block.shape[1] // HEAD
     places = jnp.arange(length, dtype=jnp.int32)
     allowed = (segment[:, None] == segment[None, :]) & (places[:, None] >= places[None, :])
-
-    def one_head(operands):
-        query_rows, key_rows, value_rows = operands
-        scores = jnp.dot(query_rows, key_rows.T, preferred_element_type=jnp.float32) * HEAD ** (
-            -0.5
-        )
-        scores = jnp.where(allowed, scores, -jnp.inf)
-        highest = jnp.max(scores, axis=1, keepdims=True)
-        weights = jnp.exp(scores - highest)
-        shares = (weights / jnp.sum(weights, axis=1, keepdims=True)).astype(jnp.bfloat16)
-        return jnp.dot(shares, value_rows, preferred_element_type=jnp.float32).astype(jnp.bfloat16)
-
-    def by_head(values):
-        return values.reshape(length, heads, HEAD).transpose(1, 0, 2)
-
-    attended = lax.map(one_head, (by_head(query_block), by_head(key_block), by_head(value_block)))
-    return attended.transpose(1, 0, 2).reshape(length, heads * HEAD)
+    query_heads = query_block.reshape(length, heads, HEAD)
+    key_heads = key_block.reshape(length, heads, HEAD)
+    value_heads = value_block.reshape(length, heads, HEAD)
+    scores = jnp.einsum(
+        "qhd,khd->hqk", query_heads, key_heads, preferred_element_type=jnp.float32
+    ) * HEAD ** (-0.5)
+    scores = jnp.where(allowed[None], scores, -jnp.inf)
+    highest = jnp.max(scores, axis=2, keepdims=True)
+    weights = jnp.exp(scores - highest)
+    shares = (weights / jnp.sum(weights, axis=2, keepdims=True)).astype(jnp.bfloat16)
+    attended = jnp.einsum("hqk,khd->qhd", shares, value_heads, preferred_element_type=jnp.float32)
+    return attended.astype(jnp.bfloat16).reshape(length, heads * HEAD)
 
 
 def on_device(
@@ -66,9 +61,11 @@
     tp_count = lax.axis_size("tp")
     attended = attend_local(queries, keys_in, values_in, segment_ids[0])
     partial_value = jnp.dot(attended, w_out, preferred_element_type=jnp.float32)
-    resid = stream.astype(jnp.float32) + lax.psum(partial_value.astype(jnp.bfloat16), "tp").astype(
-        jnp.float32
+    summed_cols = lax.psum_scatter(
+        partial_value.astype(jnp.bfloat16), "tp", scatter_dimension=1, tiled=True
     )
+    summed = lax.all_gather(summed_cols, "tp", axis=1, tiled=True)
+    resid = stream.astype(jnp.float32) + summed.astype(jnp.float32)
     normed = (
         resid * lax.rsqrt(jnp.mean(resid * resid, axis=1, keepdims=True) + 1e-06) * norm_gain
     ).astype(jnp.bfloat16)

time: 481 us -> 471 us (0.979)
  matrix products: 86.7 us -> 76.8 us
  local copies, waits for them, and re-layouts: 20.1 us -> 13 us
    psum x1 -> x0, waiting for transfers between devices: 50.2 us -> none  [on_device(): lax.psum(partial_value.astype(jnp.bfloat16), 'tp').astype(jnp.float32)]
    reduce_scatter x0 -> x1, waiting for transfers between devices: none -> 32.3 us  [on_device(): lax.psum_scatter(partial_value.astype(jnp.bfloat16), 'tp', scatter_dimens...]
    all_gather x0 -> x1, waiting for transfers between devices: none -> 21 us  [on_device(): summed = lax.all_gather(summed_cols, 'tp', axis=1, tiled=True)]
    dot_general x8 -> x2, matrix products: 10.5 us -> 2.43 us  [the longest x1 1.95 us: attend_local(): jnp.einsum('qhd,khd->hqk', query_heads, key_heads, preferred_element_type...]
    unnamed x31 -> x32, local copies, waits for them, and re-layouts: 12.6 us -> 7.41 us
  transfers between devices with their start and end apart: 4 -> 5, of which waited for: 3 -> 4; matrix products, arithmetic and copies ran while one was open for 10% -> 10% of each run, Pallas kernels for 0% -> 0%
where the time goes in v4:
time: 471 us; the launch traced here: 467 us
  waiting for transfers between devices  181 us (38%)
  blocking collectives  148 us (31%)
  matrix products  76.8 us (16%)
  other arithmetic  27 us (6%)
  between operations  13.5 us (3%)
  local copies, waits for them, and re-layouts  13 us (3%)
  starting transfers between devices  7.96 us (2%)
    all_to_all x1, blocking collectives, on_device(): lax.all_to_all(outgoing, 'ep', split_axis=0, concat_axis=0, tiled=True)  148 us
    reduce_scatter x1, waiting for transfers between devices, on_device(): lax.psum_scatter(expert_part.astype(jnp.bfloat16), 'tp', scatter_dimensio...  94.4 us
    all_to_all x1, waiting for transfers between devices, on_device(): lax.all_to_all(expert_cols, 'ep', split_axis=0, concat_axis=0, tiled=True)  32.9 us
    reduce_scatter x1, waiting for transfers between devices, on_device(): lax.psum_scatter(partial_value.astype(jnp.bfloat16), 'tp', scatter_dimens...  32.3 us
    all_gather x1, waiting for transfers between devices, on_device(): summed = lax.all_gather(summed_cols, 'tp', axis=1, tiled=True)  21 us
    dot_general x1, matrix products, on_device(): jnp.einsum('sjcf,jfd->sjcd', expert_hidden, expert_down, preferred_elemen...  20.3 us
    dot_general x1, matrix products, on_device(): jnp.dot(chosen, normed, preferred_element_type=jnp.float32)  10.1 us
    dot_general x1, matrix products, on_device(): jnp.dot(shared_hidden, shared_down, preferred_element_type=jnp.float32)  9.5 us
  transfers between devices with their start and end apart: 5, of which 4 were waited for; matrix products, arithmetic and copies ran while one was open for 10% of the time, Pallas kernels for 0%

profile of v4, /device:TPU:0, one launch (start us, length us, event | category | flops | bytes accessed | tf_op | source)
XLA Modules:
  0.0 467.3 jit_solution(8000766018058572855)
XLA Ops:
  6.5 1.8 fusion.45
  8.3 1.3 copy.69
  9.6 1.9 fusion.46
  11.5 2.1 fusion.56
  13.7 0.5 fusion.43
  14.2 1.1 copy-done.14
  15.3 2.6 convolution_convert_fusion.2
  18.0 32.3 %reduce-scatter.4.cloned.1.call-done = bf16[512,512]{1,0:T(8,128)(2,1)} async-done(((bf16[512,2048]{1,0:T(8,128)(2,1)}), bf16[512,512]{1,0:T(8,128)(2,1)}) %reduce-scatter.4.cloned.1.call-update) | async-done | bytes 524304 | tf_op jit(solution)/shard_map/reduce_scatter | solution.py:64
  50.3 0.2 reduce-scatter.8.cloned.1.call-start
  50.8 1.7 fusion.44
  52.5 0.3 convert_element_type.76
  52.9 8.5 %fusion.1 = pred[512,3072]{1,0:T(8,128)(4,1)} fusion(s32[512,4]{0,1:T(4,128)S(1)} %multiply_add_fusion), kind=kLoop, calls=%fused_computation.3 | loop fusion | flops 11010048 | bytes 1581056 | tf_op jit(solution)/shard_map/reduce_or | solution.py:90
  61.4 21.0 %all-gather.2.cloned.1.call-done = bf16[512,2048]{1,0:T(8,128)(2,1)} async-done(((bf16[512,512]{1,0:T(8,128)(2,1)}), bf16[512,2048]{1,0:T(8,128)(2,1)}) %all-gather.2.cloned.1.call-update) | async-done | bytes 2097168 | tf_op jit(solution)/shard_map/all_gather | solution.py:67
  82.5 5.0 %convert_add_fusion = (f32[512,2048]{1,0:T(8,128)}, f32[512]{0:T(512)S(1)}) fusion(bf16[512,2048]{1,0:T(8,128)(2,1)} %all-gather.2.cloned.1.call-done, bf16[512,2048]{1,0:T(8,128)(2,1)} %param.16), kind=kLoop, calls=%fused_computation.22 | loop fusion | flops 5242368 | bytes 8390656 | tf_op jit(solution)/shard_map/add | solution.py:68
  87.5 1.1 multiply_convert_fusion
  88.6 0.3 copy-done.7
  88.9 10.1 %convolution_convert_fusion = bf16[3072,2048]{1,0:T(8,128)(2,1)} fusion(pred[512,3072]{1,0:T(8,128)(4,1)S(1)} %copy-done.7, bf16[512,2048]{1,0:T(8,128)(2,1)S(1)} %multiply_convert_fusion), kind=kOutput, calls=%fused_computation.7 | convolution fusion | flops 6448742400 | bytes 16252928 | tf_op jit(solution)/shard_map/dot_general | solution.py:91
  99.0 148.3 %all_to_all.10 = bf16[32,2,48,2048]{3,2,1,0:T(8,128)(2,1)S(1)} all-to-all(bf16[32,2,48,2048]{3,2,1,0:T(8,128)(2,1)} %bitcast.76), channel_id=1, replica_groups=mesh['ep'=32,'tp'=4] {'ep'}, dimensions={0} | all-to-all | bytes 25165824 | tf_op jit(solution)/shard_map/all_to_all | solution.py:93
  247.3 4.5 copy-done.2
  251.7 8.6 %fusion.3 = f32[2,32,48,352]{3,2,1,0:T(8,128)} fusion(bf16[32,2,48,2048]{3,2,1,0:T(8,128)(2,1)S(1)} %all_to_all.10, bf16[2,2048,352]{1,2,0:T(8,128)(2,1)S(1)} %copy-done.13), kind=kOutput, calls=%fused_computation.8 | convolution fusion | flops 4429185024 | bytes 19791872 | tf_op jit(solution)/shard_map/sjcd,jdf->sjcf/dot_general | solution.py:97
  260.3 20.3 %convert_bitcast_fusion = bf16[32,2,48,2048]{3,2,0,1:T(8,128)(2,1)} fusion(bf16[2,352,2048]{2,1,0:T(8,128)(2,1)S(1)} %copy-done, f32[2,32,48,352]{3,2,1,0:T(8,128)} %fusion.3, bf16[32,2,48,2048]{3,2,1,0:T(8,128)(2,1)} %copy-done.2, bf16[2,2048,352]{1,2,0:T(8,128)(2,1)} %param.25), kind=kOutput, calls=%fused_computation.6 | convolution fusion | flops 8871149568 | bytes 35258368 | tf_op jit(solution)/shard_map/sjcf,jfd->sjcd/dot_general | solution.py:99
  280.9 1.3 copy-done.6
  282.2 5.6 %fusion.58 = f32[512,896]{1,0:T(8,128)} fusion(bf16[512,2048]{1,0:T(8,128)(2,1)S(1)} %copy-done.6, bf16[2048,896]{1,0:T(8,128)(2,1)} %param.28), kind=kOutput, calls=%fused_computation.66 | convolution fusion | flops 1879048192 | bytes 7602176 | tf_op jit(solution)/shard_map/dot_general | solution.py:72
  287.9 9.5 %convolution_convert_fusion.1 = bf16[512,2048]{1,0:T(8,128)(2,1)} fusion(bf16[896,2048]{1,0:T(8,128)(2,1)} %param.30, f32[512,896]{1,0:T(8,128)} %fusion.58, bf16[512,2048]{1,0:T(8,128)(2,1)S(1)} %copy-done.6, bf16[2048,896]{1,0:T(8,128)(2,1)} %param.29), kind=kOutput, calls=%fused_computation.28 | convolution fusion | flops 3761897472 | bytes 13369344 | tf_op jit(solution)/shard_map/dot_general | solution.py:75
  297.4 94.4 %reduce-scatter.8.cloned.1.call-done = bf16[32,2,48,512]{3,2,0,1:T(8,128)(2,1)} async-done(((bf16[32,2,48,2048]{3,2,0,1:T(8,128)(2,1)}), bf16[32,2,48,512]{3,2,0,1:T(8,128)(2,1)}) %reduce-scatter.8.cloned.1.call-update) | async-done | bytes 3145744 | tf_op jit(solution)/shard_map/reduce_scatter | solution.py:102
  391.8 3.8 copy.64
  395.6 7.5 %all-to-all-start.1 = ((bf16[32,2,48,512]{3,2,1,0:T(8,128)(2,1)}), bf16[32,2,48,512]{3,2,1,0:T(8,128)(2,1)}, u32[]{:S(2)}, u32[]{:S(2)}) async-start(bf16[32,2,48,512]{3,2,1,0:T(8,128)(2,1)} %copy.64), calls=%async_computation.4 | async-start | bytes 6291456 | tf_op jit(solution)/shard_map/all_to_all | solution.py:105
  403.2 8.4 %select_reduce_fusion = f32[512,3072]{1,0:T(8,128)} fusion(f32[512,4]{0,1:T(4,128)S(1)} %copy-done.11, s32[512,4]{0,1:T(4,128)S(1)} %multiply_add_fusion), kind=kLoop, calls=%fused_computation.1 | loop fusion | flops 17301504 | bytes 6307840 | tf_op jit(solution)/shard_map/reduce_sum | solution.py:108
  411.6 0.6 fusion.57
  412.3 32.9 %all-to-all-done.1 = bf16[32,2,48,512]{3,2,1,0:T(8,128)(2,1)} async-done(((bf16[32,2,48,512]{3,2,1,0:T(8,128)(2,1)}), bf16[32,2,48,512]{3,2,1,0:T(8,128)(2,1)}, u32[]{:S(2)}, u32[]{:S(2)}) %all-to-all-start.1) | async-done | bytes 3145760 | tf_op jit(solution)/shard_map/all_to_all | solution.py:105
  445.1 8.2 %fusion.12 = f32[512,512]{1,0:T(8,128)} fusion(bf16[3072,512]{1,0:T(8,128)(2,1)} %bitcast.15, f32[512,3072]{1,0:T(8,128)} %select_reduce_fusion), kind=kOutput, calls=%fused_computation.27 | convolution fusion | flops 1616904192 | bytes 10485760 | tf_op jit(solution)/shard_map/dot_general | solution.py:111
  453.4 7.2 %fusion.40 = bf16[512,512]{1,0:T(8,128)(2,1)} fusion(f32[512,512]{1,0:T(8,128)} %fusion.12, bf16[3072,512]{1,0:T(8,128)(2,1)} %bitcast.15, f32[512,3072]{1,0:T(8,128)} %select_reduce_fusion, bf16[512,512]{1,0:T(8,128)(2,1)} %reduce-scatter.6.cloned.1.call-done, f32[512,2048]{1,0:T(8,128)} %get-tuple-element.5, s32[]{:T(128)S(6)} %select_n.16, ...), kind=kOutput, calls=%fused_computation.45 | convolution fusion | flops 1613758464 | bytes 12584964 | tf_op jit(solution)/shard_map/dot_general | solution.py:111
  (42 shorter events, 0.8 us)
Async XLA Ops:
  6.5 253.8 %copy-start = (bf16[2,352,2048]{2,1,0:T(8,128)(2,1)S(1)}, bf16[2,352,2048]{2,1,0:T(8,128)(2,1)}, u32[]{:S(2)}) copy-start(bf16[2,352,2048]{2,1,0:T(8,128)(2,1)} %param.27) | copy-start | bytes 8650756
  6.5 43.7 %reduce-scatter.4.cloned.1.call-start = ((), (), s32[]{:S(2)}) async-start(), calls=%async_computation.5 | async-start | bytes 2621440 | tf_op jit(solution)/shard_map/reduce_scatter | solution.py:64
  9.5 2.0 copy-start.8
  13.7 1.6 copy-start.14
  15.3 35.2 %copy-start.9 = (s32[512,4]{0,1:T(4,128)S(1)}, s32[512,4]{0,1:T(4,128)}, u32[]{:S(2)}) copy-start(s32[512,4]{0,1:T(4,128)} %param.21) | copy-start | bytes 24580
  17.9 64.6 %all-gather.2.cloned.1.call-start = ((), (), s32[]{:S(2)}) async-start(), calls=%async_computation.6 | async-start | bytes 2621440 | tf_op jit(solution)/shard_map/all_gather | solution.py:67
  50.3 341.5 %reduce-scatter.8.cloned.1.call-start = ((), (), s32[]{:S(2)}) async-start(), calls=%async_computation.8 | async-start | bytes 15728640 | tf_op jit(solution)/shard_map/reduce_scatter | solution.py:102
  61.4 26.0 %copy-start.10 = (f32[2048]{0:T(1024)S(1)}, f32[2048]{0:T(1024)}, u32[]{:S(2)}) copy-start(f32[2048]{0:T(1024)} %param.24) | copy-start | bytes 24580
  82.5 5.0 %copy-start.3 = (bf16[512,2048]{1,0:T(8,128)(2,1)S(1)}, bf16[512,2048]{1,0:T(8,128)(2,1)}, u32[]{:S(2)}) copy-start(bf16[512,2048]{1,0:T(8,128)(2,1)} %param.16) | copy-start | bytes 6291460
  82.5 5.0 %copy-start.4 = (bf16[512,2048]{1,0:T(8,128)(2,1)S(1)}, bf16[512,2048]{1,0:T(8,128)(2,1)}, u32[]{:S(2)}) copy-start(bf16[512,2048]{1,0:T(8,128)(2,1)} %all-gather.2.cloned.1.call-done) | copy-start | bytes 6291460
  87.5 1.4 copy-start.7
  88.9 10.1 %copy-start.5 = (bf16[512,2048]{1,0:T(8,128)(2,1)}, bf16[512,2048]{1,0:T(8,128)(2,1)S(1)}, u32[]{:S(2)}) copy-start(bf16[512,2048]{1,0:T(8,128)(2,1)S(1)} %multiply_convert_fusion) | copy-start | bytes 6291460
  98.9 152.8 %copy-start.13 = (bf16[2,2048,352]{1,2,0:T(8,128)(2,1)S(1)}, bf16[2,2048,352]{1,2,0:T(8,128)(2,1)}, u32[]{:S(2)}) copy-start(bf16[2,2048,352]{1,2,0:T(8,128)(2,1)} %param.26) | copy-start | bytes 8650756
  247.2 4.5 copy-start.2
  280.6 1.6 copy-start.6
  280.7 172.7 %reduce-scatter.6.cloned.1.call-start = ((), (), s32[]{:S(2)}) async-start(), calls=%async_computation.7 | async-start | bytes 2621440 | tf_op jit(solution)/shard_map/reduce_scatter | solution.py:76
  395.6 7.5 %copy-start.12 = (bf16[2048]{0:T(1024)(128)(2,1)S(1)}, bf16[2048]{0:T(1024)(128)(2,1)}, u32[]{:S(2)}) copy-start(bf16[2048]{0:T(1024)(128)(2,1)} %param.31) | copy-start | bytes 12292
  395.6 7.5 %copy-start.11 = (f32[512,4]{0,1:T(4,128)S(1)}, f32[512,4]{0,1:T(4,128)}, u32[]{:S(2)}) copy-start(f32[512,4]{0,1:T(4,128)} %param.22) | copy-start | bytes 24580
  395.6 49.5 %all-to-all-start.1 = ((bf16[32,2,48,512]{3,2,1,0:T(8,128)(2,1)}), bf16[32,2,48,512]{3,2,1,0:T(8,128)(2,1)}, u32[]{:S(2)}, u32[]{:S(2)}) async-start(bf16[32,2,48,512]{3,2,1,0:T(8,128)(2,1)} %copy.64), calls=%async_computation.4 | async-start | bytes 6291456 | tf_op jit(solution)/shard_map/all_to_all | solution.py:105
  453.4 7.2 %copy-start.1 = (bf16[2,352,2048]{2,1,0:T(8,128)(2,1)S(1)}, bf16[2,352,2048]{2,1,0:T(8,128)(2,1)}, u32[]{:S(2)}) copy-start(bf16[2,352,2048]{2,1,0:T(8,128)(2,1)} %param.27) | copy-start | bytes 8650756
Sparse Core Ops, SparseCore 0:
  18.0 32.1 reduce-scatter.3
  51.9 30.4 all-gather.1
  280.8 110.9 reduce-scatter.7
  394.1 29.3 reduce-scatter.5

commit v5 on v4

--- a/solution.py
+++ b/solution.py
@@ -108,6 +108,7 @@
     mixing = jnp.sum(jnp.where(hits, route_weights[:, :, None], 0.0), axis=1)
     mixing_high = mixing.astype(jnp.bfloat16)
     mixing_low = (mixing - mixing_high.astype(jnp.float32)).astype(jnp.bfloat16)
+    mixing_high, mixing_low = lax.optimization_barrier((mixing_high, mixing_low))
     routed = jnp.dot(mixing_high, flat_results, preferred_element_type=jnp.float32) + jnp.dot(
         mixing_low, flat_results, preferred_element_type=jnp.float32
     )

time: 471 us -> 467 us (level)
  no operation moved by 1% of the time
where the time goes in v5:
time: 467 us; the launch traced here: 464 us
  waiting for transfers between devices  179 us (38%)
  blocking collectives  148 us (32%)
  matrix products  73.3 us (16%)
  other arithmetic  28.2 us (6%)
  between operations  13.5 us (3%)
  local copies, waits for them, and re-layouts  13.1 us (3%)
  starting transfers between devices  7.96 us (2%)
    all_to_all x1, blocking collectives, on_device(): lax.all_to_all(outgoing, 'ep', split_axis=0, concat_axis=0, tiled=True)  148 us
    reduce_scatter x1, waiting for transfers between devices, on_device(): lax.psum_scatter(expert_part.astype(jnp.bfloat16), 'tp', scatter_dimensio...  94.4 us
    reduce_scatter x1, waiting for transfers between devices, on_device(): lax.psum_scatter(partial_value.astype(jnp.bfloat16), 'tp', scatter_dimens...  32.3 us
    all_to_all x1, waiting for transfers between devices, on_device(): lax.all_to_all(expert_cols, 'ep', split_axis=0, concat_axis=0, tiled=True)  31.6 us
    all_gather x1, waiting for transfers between devices, on_device(): summed = lax.all_gather(summed_cols, 'tp', axis=1, tiled=True)  21 us
    dot_general x1, matrix products, on_device(): jnp.einsum('sjcf,jfd->sjcd', expert_hidden, expert_down, preferred_elemen...  20.3 us
    dot_general x1, matrix products, on_device(): jnp.dot(chosen, normed, preferred_element_type=jnp.float32)  10.1 us
    dot_general x1, matrix products, on_device(): jnp.dot(shared_hidden, shared_down, preferred_element_type=jnp.float32)  9.51 us
  transfers between devices with their start and end apart: 5, of which 4 were waited for; matrix products, arithmetic and copies ran while one was open for 10% of the time, Pallas kernels for 0%

profile of v5, /device:TPU:0, one launch (start us, length us, event | category | flops | bytes accessed | tf_op | source)
XLA Modules:
  0.0 463.8 jit_solution(1095014657146130017)
XLA Ops:
  6.5 1.8 fusion.34
  8.3 1.3 copy.69
  9.6 1.9 fusion.35
  11.5 2.1 fusion.45
  13.7 0.5 fusion.32
  14.2 1.1 copy-done.14
  15.3 2.6 convolution_convert_fusion.2
  18.0 32.3 %reduce-scatter.4.cloned.1.call-done = bf16[512,512]{1,0:T(8,128)(2,1)} async-done(((bf16[512,2048]{1,0:T(8,128)(2,1)}), bf16[512,512]{1,0:T(8,128)(2,1)}) %reduce-scatter.4.cloned.1.call-update) | async-done | bytes 524304 | tf_op jit(solution)/shard_map/reduce_scatter | solution.py:64
  50.9 1.7 fusion.33
  52.5 0.3 convert_element_type.76
  52.9 8.5 %fusion.1 = pred[512,3072]{1,0:T(8,128)(4,1)} fusion(s32[512,4]{0,1:T(4,128)S(1)} %multiply_add_fusion), kind=kLoop, calls=%fused_computation.3 | loop fusion | flops 11010048 | bytes 1581056 | tf_op jit(solution)/shard_map/reduce_or | solution.py:90
  61.5 21.0 %all-gather.2.cloned.1.call-done = bf16[512,2048]{1,0:T(8,128)(2,1)} async-done(((bf16[512,512]{1,0:T(8,128)(2,1)}), bf16[512,2048]{1,0:T(8,128)(2,1)}) %all-gather.2.cloned.1.call-update) | async-done | bytes 2097168 | tf_op jit(solution)/shard_map/all_gather | solution.py:67
  82.5 5.0 %convert_add_fusion = (f32[512,2048]{1,0:T(8,128)}, f32[512]{0:T(512)S(1)}) fusion(bf16[512,2048]{1,0:T(8,128)(2,1)} %all-gather.2.cloned.1.call-done, bf16[512,2048]{1,0:T(8,128)(2,1)} %param.16), kind=kLoop, calls=%fused_computation.22 | loop fusion | flops 5242368 | bytes 8390656 | tf_op jit(solution)/shard_map/add | solution.py:68
  87.5 1.1 multiply_convert_fusion
  88.6 0.3 copy-done.7
  88.9 10.1 %convolution_convert_fusion = bf16[3072,2048]{1,0:T(8,128)(2,1)} fusion(pred[512,3072]{1,0:T(8,128)(4,1)S(1)} %copy-done.7, bf16[512,2048]{1,0:T(8,128)(2,1)S(1)} %multiply_convert_fusion), kind=kOutput, calls=%fused_computation.7 | convolution fusion | flops 6448742400 | bytes 16252928 | tf_op jit(solution)/shard_map/dot_general | solution.py:91
  99.0 148.3 %all_to_all.10 = bf16[32,2,48,2048]{3,2,1,0:T(8,128)(2,1)S(1)} all-to-all(bf16[32,2,48,2048]{3,2,1,0:T(8,128)(2,1)} %bitcast.78), channel_id=1, replica_groups=mesh['ep'=32,'tp'=4] {'ep'}, dimensions={0} | all-to-all | bytes 25165824 | tf_op jit(solution)/shard_map/all_to_all | solution.py:93
  247.3 4.5 copy-done.2
  251.7 8.6 %fusion.3 = f32[2,32,48,352]{3,2,1,0:T(8,128)} fusion(bf16[32,2,48,2048]{3,2,1,0:T(8,128)(2,1)S(1)} %all_to_all.10, bf16[2,2048,352]{1,2,0:T(8,128)(2,1)S(1)} %copy-done.13), kind=kOutput, calls=%fused_computation.8 | convolution fusion | flops 4429185024 | bytes 19791872 | tf_op jit(solution)/shard_map/sjcd,jdf->sjcf/dot_general | solution.py:97
  260.4 20.3 %convert_bitcast_fusion = bf16[32,2,48,2048]{3,2,0,1:T(8,128)(2,1)} fusion(bf16[2,352,2048]{2,1,0:T(8,128)(2,1)S(1)} %copy-done, f32[2,32,48,352]{3,2,1,0:T(8,128)} %fusion.3, bf16[32,2,48,2048]{3,2,1,0:T(8,128)(2,1)} %copy-done.2, bf16[2,2048,352]{1,2,0:T(8,128)(2,1)} %param.25), kind=kOutput, calls=%fused_computation.6 | convolution fusion | flops 8871149568 | bytes 35258368 | tf_op jit(solution)/shard_map/sjcf,jfd->sjcd/dot_general | solution.py:99
  280.9 1.3 copy-done.6
  282.2 5.6 %fusion.47 = f32[512,896]{1,0:T(8,128)} fusion(bf16[512,2048]{1,0:T(8,128)(2,1)S(1)} %copy-done.6, bf16[2048,896]{1,0:T(8,128)(2,1)} %param.28), kind=kOutput, calls=%fused_computation.62 | convolution fusion | flops 1879048192 | bytes 7602176 | tf_op jit(solution)/shard_map/dot_general | solution.py:72
  287.9 9.5 %convolution_convert_fusion.1 = bf16[512,2048]{1,0:T(8,128)(2,1)} fusion(bf16[896,2048]{1,0:T(8,128)(2,1)} %param.30, f32[512,896]{1,0:T(8,128)} %fusion.47, bf16[512,2048]{1,0:T(8,128)(2,1)S(1)} %copy-done.6, bf16[2048,896]{1,0:T(8,128)(2,1)} %param.29), kind=kOutput, calls=%fused_computation.27 | convolution fusion | flops 3761897472 | bytes 13369344 | tf_op jit(solution)/shard_map/dot_general | solution.py:75
  297.4 94.4 %reduce-scatter.8.cloned.1.call-done = bf16[32,2,48,512]{3,2,0,1:T(8,128)(2,1)} async-done(((bf16[32,2,48,2048]{3,2,0,1:T(8,128)(2,1)}), bf16[32,2,48,512]{3,2,0,1:T(8,128)(2,1)}) %reduce-scatter.8.cloned.1.call-update) | async-done | bytes 3145744 | tf_op jit(solution)/shard_map/reduce_scatter | solution.py:102
  391.8 3.9 copy.64
  395.7 7.5 %all-to-all-start.1 = ((bf16[32,2,48,512]{3,2,1,0:T(8,128)(2,1)}), bf16[32,2,48,512]{3,2,1,0:T(8,128)(2,1)}, u32[]{:S(2)}, u32[]{:S(2)}) async-start(bf16[32,2,48,512]{3,2,1,0:T(8,128)(2,1)} %copy.64), calls=%async_computation.4 | async-start | bytes 6291456 | tf_op jit(solution)/shard_map/all_to_all | solution.py:105
  403.2 5.8 %select_reduce_fusion = f32[512,3072]{1,0:T(8,128)S(1)} fusion(f32[512,4]{0,1:T(4,128)S(1)} %copy-done.11, s32[512,4]{0,1:T(4,128)S(1)} %multiply_add_fusion), kind=kLoop, calls=%fused_computation.1 | loop fusion | flops 17301504 | bytes 6307840 | tf_op jit(solution)/shard_map/reduce_sum | solution.py:108
  409.0 3.9 subtract_convert_fusion
  412.9 0.6 fusion.46
  413.6 31.6 %all-to-all-done.1 = bf16[32,2,48,512]{3,2,1,0:T(8,128)(2,1)} async-done(((bf16[32,2,48,512]{3,2,1,0:T(8,128)(2,1)}), bf16[32,2,48,512]{3,2,1,0:T(8,128)(2,1)}, u32[]{:S(2)}, u32[]{:S(2)}) %all-to-all-start.1) | async-done | bytes 3145760 | tf_op jit(solution)/shard_map/all_to_all | solution.py:105
  445.2 5.6 %fusion.48 = f32[512,512]{1,0:T(8,128)} fusion(bf16[512,3072]{1,0:T(8,128)(2,1)} %get-tuple-element.7, bf16[3072,512]{1,0:T(8,128)(2,1)} %bitcast.15), kind=kOutput, calls=%fused_computation.63 | convolution fusion | flops 1610612736 | bytes 7340032 | tf_op jit(solution)/shard_map/dot_general | solution.py:112
  450.8 6.3 %fusion.31 = bf16[512,512]{1,0:T(8,128)(2,1)} fusion(f32[512,512]{1,0:T(8,128)} %fusion.48, bf16[512,3072]{1,0:T(8,128)(2,1)} %get-tuple-element.8, bf16[3072,512]{1,0:T(8,128)(2,1)} %bitcast.15, bf16[512,512]{1,0:T(8,128)(2,1)} %reduce-scatter.6.cloned.1.call-done, f32[512,2048]{1,0:T(8,128)} %get-tuple-element.11, s32[]{:T(128)S(6)} %select_n.16, ...), kind=kOutput, calls=%fused_computation.41 | convolution fusion | flops 1612185600 | bytes 9439236 | tf_op jit(solution)/shard_map/dot_general | solution.py:112
  (43 shorter events, 1.1 us)
Async XLA Ops:
  6.5 253.8 %copy-start = (bf16[2,352,2048]{2,1,0:T(8,128)(2,1)S(1)}, bf16[2,352,2048]{2,1,0:T(8,128)(2,1)}, u32[]{:S(2)}) copy-start(bf16[2,352,2048]{2,1,0:T(8,128)(2,1)} %param.27) | copy-start | bytes 8650756
  6.5 43.7 %reduce-scatter.4.cloned.1.call-start = ((), (), s32[]{:S(2)}) async-start(), calls=%async_computation.5 | async-start | bytes 2621440 | tf_op jit(solution)/shard_map/reduce_scatter | solution.py:64
  9.5 2.0 copy-start.8
  13.7 1.6 copy-start.14
  15.3 35.3 %copy-start.9 = (s32[512,4]{0,1:T(4,128)S(1)}, s32[512,4]{0,1:T(4,128)}, u32[]{:S(2)}) copy-start(s32[512,4]{0,1:T(4,128)} %param.21) | copy-start | bytes 24580
  17.9 64.6 %all-gather.2.cloned.1.call-start = ((), (), s32[]{:S(2)}) async-start(), calls=%async_computation.6 | async-start | bytes 2621440 | tf_op jit(solution)/shard_map/all_gather | solution.py:67
  50.3 341.5 %reduce-scatter.8.cloned.1.call-start = ((), (), s32[]{:S(2)}) async-start(), calls=%async_computation.8 | async-start | bytes 15728640 | tf_op jit(solution)/shard_map/reduce_scatter | solution.py:102
  61.5 26.0 %copy-start.10 = (f32[2048]{0:T(1024)S(1)}, f32[2048]{0:T(1024)}, u32[]{:S(2)}) copy-start(f32[2048]{0:T(1024)} %param.24) | copy-start | bytes 24580
  82.5 5.0 %copy-start.3 = (bf16[512,2048]{1,0:T(8,128)(2,1)S(1)}, bf16[512,2048]{1,0:T(8,128)(2,1)}, u32[]{:S(2)}) copy-start(bf16[512,2048]{1,0:T(8,128)(2,1)} %param.16) | copy-start | bytes 6291460
  82.5 5.0 %copy-start.4 = (bf16[512,2048]{1,0:T(8,128)(2,1)S(1)}, bf16[512,2048]{1,0:T(8,128)(2,1)}, u32[]{:S(2)}) copy-start(bf16[512,2048]{1,0:T(8,128)(2,1)} %all-gather.2.cloned.1.call-done) | copy-start | bytes 6291460
  87.5 1.4 copy-start.7
  88.9 10.1 %copy-start.5 = (bf16[512,2048]{1,0:T(8,128)(2,1)}, bf16[512,2048]{1,0:T(8,128)(2,1)S(1)}, u32[]{:S(2)}) copy-start(bf16[512,2048]{1,0:T(8,128)(2,1)S(1)} %multiply_convert_fusion) | copy-start | bytes 6291460
  99.0 152.8 %copy-start.13 = (bf16[2,2048,352]{1,2,0:T(8,128)(2,1)S(1)}, bf16[2,2048,352]{1,2,0:T(8,128)(2,1)}, u32[]{:S(2)}) copy-start(bf16[2,2048,352]{1,2,0:T(8,128)(2,1)} %param.26) | copy-start | bytes 8650756
  247.3 4.5 copy-start.2
  280.7 1.6 copy-start.6
  280.7 170.1 %reduce-scatter.6.cloned.1.call-start = ((), (), s32[]{:S(2)}) async-start(), calls=%async_computation.7 | async-start | bytes 2621440 | tf_op jit(solution)/shard_map/reduce_scatter | solution.py:76
  395.7 7.5 %copy-start.11 = (f32[512,4]{0,1:T(4,128)S(1)}, f32[512,4]{0,1:T(4,128)}, u32[]{:S(2)}) copy-start(f32[512,4]{0,1:T(4,128)} %param.22) | copy-start | bytes 24580
  395.7 49.5 %all-to-all-start.1 = ((bf16[32,2,48,512]{3,2,1,0:T(8,128)(2,1)}), bf16[32,2,48,512]{3,2,1,0:T(8,128)(2,1)}, u32[]{:S(2)}, u32[]{:S(2)}) async-start(bf16[32,2,48,512]{3,2,1,0:T(8,128)(2,1)} %copy.64), calls=%async_computation.4 | async-start | bytes 6291456 | tf_op jit(solution)/shard_map/all_to_all | solution.py:105
  409.0 3.9 copy-start.12
  450.8 6.3 %copy-start.1 = (bf16[2,352,2048]{2,1,0:T(8,128)(2,1)S(1)}, bf16[2,352,2048]{2,1,0:T(8,128)(2,1)}, u32[]{:S(2)}) copy-start(bf16[2,352,2048]{2,1,0:T(8,128)(2,1)} %param.27) | copy-start | bytes 8650756
Sparse Core Ops, SparseCore 0:
  18.0 32.1 reduce-scatter.3
  51.9 30.4 all-gather.1
  280.8 110.9 reduce-scatter.7
  394.1 29.4 reduce-scatter.5

commit v6 on v5

--- a/solution.py
+++ b/solution.py
@@ -96,22 +96,32 @@
     )
     up_rows = jnp.einsum("sjcd,jdf->sjcf", incoming, expert_up, preferred_element_type=jnp.float32)
     expert_hidden = (jax.nn.silu(gate_rows) * up_rows).astype(jnp.bfloat16)
-    expert_part = jnp.einsum(
-        "sjcf,jfd->sjcd", expert_hidden, expert_down, preferred_element_type=jnp.float32
-    )
-    expert_cols = lax.psum_scatter(
-        expert_part.astype(jnp.bfloat16), "tp", scatter_dimension=3, tiled=True
-    )
-    returned = lax.all_to_all(expert_cols, "ep", split_axis=0, concat_axis=0, tiled=True)
-    columns = returned.shape[3]
-    flat_results = returned.reshape(experts * capacity, columns)
     mixing = jnp.sum(jnp.where(hits, route_weights[:, :, None], 0.0), axis=1)
     mixing_high = mixing.astype(jnp.bfloat16)
     mixing_low = (mixing - mixing_high.astype(jnp.float32)).astype(jnp.bfloat16)
     mixing_high, mixing_low = lax.optimization_barrier((mixing_high, mixing_low))
-    routed = jnp.dot(mixing_high, flat_results, preferred_element_type=jnp.float32) + jnp.dot(
-        mixing_low, flat_results, preferred_element_type=jnp.float32
-    )
+    mixing_high = mixing_high.reshape(length, ep_count, local_experts, capacity)
+    mixing_low = mixing_low.reshape(length, ep_count, local_experts, capacity)
+    routed = None
+    for index in range(local_experts):
+        expert_part = jnp.einsum(
+            "scf,fd->scd",
+            expert_hidden[:, index],
+            expert_down[index],
+            preferred_element_type=jnp.float32,
+        )
+        expert_cols = lax.psum_scatter(
+            expert_part.astype(jnp.bfloat16), "tp", scatter_dimension=2, tiled=True
+        )
+        returned = lax.all_to_all(expert_cols, "ep", split_axis=0, concat_axis=0, tiled=True)
+        columns = returned.shape[2]
+        flat_results = returned.reshape(ep_count * capacity, columns)
+        high = mixing_high[:, :, index].reshape(length, ep_count * capacity)
+        low = mixing_low[:, :, index].reshape(length, ep_count * capacity)
+        term = jnp.dot(high, flat_results, preferred_element_type=jnp.float32) + jnp.dot(
+            low, flat_results, preferred_element_type=jnp.float32
+        )
+        routed = term if routed is None else routed + term
     resid_cols = lax.dynamic_slice_in_dim(resid, lax.axis_index("tp") * columns, columns, 1)
     return (resid_cols + shared_scale[:, None] * shared_cols + routed).astype(jnp.bfloat16)
 

time: 467 us -> 456 us (0.976)
  waiting for transfers between devices: 179 us -> 139 us
  other arithmetic: 28.2 us -> 36.3 us
  local copies, waits for them, and re-layouts: 13.1 us -> 20.6 us
  starting transfers between devices: 7.96 us -> 15.1 us
  matrix products: 73.3 us -> 78.5 us
    all_to_all x1 -> x2, waiting for transfers between devices: 31.6 us -> 0.01 us  [on_device(): lax.all_to_all(expert_cols, 'ep', split_axis=0, concat_axis=0, tiled=True)]
    optimization_barrier x0 -> x2, local copies, waits for them, and re-layouts: none -> 9.47 us  [on_device(): lax.optimization_barrier((mixing_high, mixing_low))]
    reduce_scatter x1 -> x2, waiting for transfers between devices: 94.4 us -> 85.5 us  [on_device(): lax.psum_scatter(expert_part.astype(jnp.bfloat16), 'tp', scatter_dimensio...]
    all_to_all x1 -> x2, starting transfers between devices: 7.49 us -> 14.7 us  [on_device(): lax.all_to_all(expert_cols, 'ep', split_axis=0, concat_axis=0, tiled=True)]
    convert_element_type x1, other arithmetic: 3.88 us -> 9.43 us  [on_device(): mixing_low = (mixing - mixing_high.astype(jnp.float32)).astype(jnp.bfloat16)]
    slice x0 -> x2, local copies, waits for them, and re-layouts: none -> 5.39 us  [the longest x1 3.44 us: on_device(): high = mixing_high[:, :, index].reshape(length, ep_count * capacity)]
    dot_general x3 -> x7, matrix products: 32.2 us -> 36.1 us  [the longest x2 13.6 us: on_device(): jnp.einsum('scf,fd->scd', expert_hidden[:, index], expert_down[index], pr...]
  transfers between devices with their start and end apart: 5 -> 7, of which waited for: 4 -> 4; matrix products, arithmetic and copies ran while one was open for 10% -> 17% of each run, Pallas kernels for 0% -> 0%
where the time goes in v6:
time: 456 us; the launch traced here: 451 us
  blocking collectives  148 us (32%)
  waiting for transfers between devices  139 us (30%)
  matrix products  78.5 us (17%)
  other arithmetic  36.3 us (8%)
  local copies, waits for them, and re-layouts  20.6 us (5%)
  starting transfers between devices  15.1 us (3%)
  between operations  13.5 us (3%)
    all_to_all x1, blocking collectives, on_device(): lax.all_to_all(outgoing, 'ep', split_axis=0, concat_axis=0, tiled=True)  148 us
    reduce_scatter x2, waiting for transfers between devices, on_device(): lax.psum_scatter(expert_part.astype(jnp.bfloat16), 'tp', scatter_dimensio...  85.5 us
    reduce_scatter x1, waiting for transfers between devices, on_device(): lax.psum_scatter(partial_value.astype(jnp.bfloat16), 'tp', scatter_dimens...  32.3 us
    all_gather x1, waiting for transfers between devices, on_device(): summed = lax.all_gather(summed_cols, 'tp', axis=1, tiled=True)  21 us
    all_to_all x2, starting transfers between devices, on_device(): lax.all_to_all(expert_cols, 'ep', split_axis=0, concat_axis=0, tiled=True)  14.7 us
    dot_general x2, matrix products, on_device(): jnp.einsum('scf,fd->scd', expert_hidden[:, index], expert_down[index], pr...  13.6 us
    dot_general x1, matrix products, on_device(): jnp.dot(shared_hidden, shared_down, preferred_element_type=jnp.float32)  11 us
    dot_general x1, matrix products, on_device(): jnp.einsum('sjcd,jdf->sjcf', incoming, expert_gate, preferred_element_typ...  10.5 us
  transfers between devices with their start and end apart: 7, of which 4 were waited for; matrix products, arithmetic and copies ran while one was open for 17% of the time, Pallas kernels for 0%

profile of v6, /device:TPU:0, one launch (start us, length us, event | category | flops | bytes accessed | tf_op | source)
XLA Modules:
  0.0 451.0 jit_solution(7034524680406849859)
XLA Ops:
  6.5 1.8 fusion.32
  8.3 1.3 copy.68
  9.6 1.9 fusion.33
  11.5 2.1 fusion.44
  15.3 2.6 convolution_convert_fusion.4
  18.0 32.3 %reduce-scatter.5.cloned.1.call-done = bf16[512,512]{1,0:T(8,128)(2,1)} async-done(((bf16[512,2048]{1,0:T(8,128)(2,1)}), bf16[512,512]{1,0:T(8,128)(2,1)}) %reduce-scatter.5.cloned.1.call-update) | async-done | bytes 524304 | tf_op jit(solution)/shard_map/reduce_scatter | solution.py:64
  50.9 1.7 fusion.31
  52.9 8.5 %fusion.1 = pred[512,3072]{1,0:T(8,128)(4,1)} fusion(s32[512,4]{0,1:T(4,128)S(1)} %multiply_add_fusion), kind=kLoop, calls=%fused_computation.3 | loop fusion | flops 11010048 | bytes 1581056 | tf_op jit(solution)/shard_map/reduce_or | solution.py:90
  61.5 21.0 %all-gather.2.cloned.1.call-done = bf16[512,2048]{1,0:T(8,128)(2,1)} async-done(((bf16[512,512]{1,0:T(8,128)(2,1)}), bf16[512,2048]{1,0:T(8,128)(2,1)}) %all-gather.2.cloned.1.call-update) | async-done | bytes 2097168 | tf_op jit(solution)/shard_map/all_gather | solution.py:67
  82.5 5.0 %convert_add_fusion = (f32[512,2048]{1,0:T(8,128)}, f32[512]{0:T(512)S(1)}) fusion(bf16[512,2048]{1,0:T(8,128)(2,1)} %all-gather.2.cloned.1.call-done, bf16[512,2048]{1,0:T(8,128)(2,1)} %param.16), kind=kLoop, calls=%fused_computation.23 | loop fusion | flops 5242368 | bytes 8390656 | tf_op jit(solution)/shard_map/add | solution.py:68
  88.9 9.9 %convolution_convert_fusion = bf16[3072,2048]{1,0:T(8,128)(2,1)} fusion(pred[512,3072]{1,0:T(8,128)(4,1)S(1)} %copy-done.9, bf16[512,2048]{1,0:T(8,128)(2,1)S(1)} %multiply_convert_fusion), kind=kOutput, calls=%fused_computation.6 | convolution fusion | flops 6448742400 | bytes 16252928 | tf_op jit(solution)/shard_map/dot_general | solution.py:91
  98.7 148.0 %all_to_all.15 = bf16[32,2,48,2048]{3,2,1,0:T(8,128)(2,1)S(1)} all-to-all(bf16[32,2,48,2048]{3,2,1,0:T(8,128)(2,1)} %bitcast.94), channel_id=1, replica_groups=mesh['ep'=32,'tp'=4] {'ep'}, dimensions={0} | all-to-all | bytes 25165824 | tf_op jit(solution)/shard_map/all_to_all | solution.py:93
  246.8 8.5 %fusion.3 = f32[2,32,48,352]{3,2,1,0:T(8,128)} fusion(bf16[32,2,48,2048]{3,2,1,0:T(8,128)(2,1)S(1)} %all_to_all.15, bf16[2,2048,352]{1,2,0:T(8,128)(2,1)S(1)} %copy-done), kind=kOutput, calls=%fused_computation.7 | convolution fusion | flops 4429185024 | bytes 19791872 | tf_op jit(solution)/shard_map/sjcd,jdf->sjcf/dot_general | solution.py:97
  255.3 10.5 %fusion.7 = bf16[32,2,48,352]{3,2,0,1:T(8,128)(2,1)} fusion(f32[2,32,48,352]{3,2,1,0:T(8,128)} %fusion.3, bf16[2,2048,352]{1,2,0:T(8,128)(2,1)S(1)} %copy-done.15, bf16[32,2,48,2048]{3,2,1,0:T(8,128)(2,1)S(1)} %all_to_all.15), kind=kOutput, calls=%fused_computation.13 | convolution fusion | flops 4435673088 | bytes 21954560 | tf_op jit(solution)/shard_map/sjcd,jdf->sjcf/dot_general | solution.py:94
  265.8 6.6 %convolution_convert_fusion.1 = bf16[32,48,2048]{2,1,0:T(8,128)(2,1)} fusion(bf16[2,352,2048]{2,1,0:T(8,128)(2,1)S(1)} %copy-done.16, bf16[32,2,48,352]{3,2,0,1:T(8,128)(2,1)} %fusion.7), kind=kOutput, calls=%fused_computation.19 | convolution fusion | flops 2217738240 | bytes 8912896 | tf_op jit(solution)/shard_map/scf,fd->scd/dot_general | solution.py:107
  272.5 7.0 %convolution_convert_fusion.2 = bf16[32,48,2048]{2,1,0:T(8,128)(2,1)} fusion(bf16[2,352,2048]{2,1,0:T(8,128)(2,1)S(1)} %copy-done.16, bf16[32,2,48,352]{3,2,0,1:T(8,128)(2,1)} %fusion.7), kind=kOutput, calls=%fused_computation.20 | convolution fusion | flops 2217738240 | bytes 8912896 | tf_op jit(solution)/shard_map/scf,fd->scd/dot_general | solution.py:107
  279.5 1.6 copy-done.6
  281.1 5.6 %fusion.46 = f32[512,896]{1,0:T(8,128)} fusion(bf16[512,2048]{1,0:T(8,128)(2,1)S(1)} %copy-done.6, bf16[2048,896]{1,0:T(8,128)(2,1)} %param.28), kind=kOutput, calls=%fused_computation.70 | convolution fusion | flops 1879048192 | bytes 7602176 | tf_op jit(solution)/shard_map/dot_general | solution.py:72
  286.7 46.3 %reduce-scatter.11.cloned.1.call-done = bf16[32,48,512]{2,1,0:T(8,128)(2,1)} async-done(((bf16[32,48,2048]{2,1,0:T(8,128)(2,1)}), bf16[32,48,512]{2,1,0:T(8,128)(2,1)}) %reduce-scatter.11.cloned.1.call-update) | async-done | bytes 1572880 | tf_op jit(solution)/shard_map/reduce_scatter | solution.py:113
  333.0 7.2 %all-to-all-start.2 = ((bf16[32,48,512]{2,1,0:T(8,128)(2,1)}), bf16[32,48,512]{2,1,0:T(8,128)(2,1)S(1)}, u32[]{:S(2)}, u32[]{:S(2)}) async-start(bf16[32,48,512]{2,1,0:T(8,128)(2,1)} %reduce-scatter.11.cloned.1.call-done), calls=%async_computation.6 | async-start | bytes 3145728 | tf_op jit(solution)/shard_map/all_to_all | solution.py:116
  340.3 11.0 %convolution_convert_fusion.3 = bf16[512,2048]{1,0:T(8,128)(2,1)} fusion(bf16[896,2048]{1,0:T(8,128)(2,1)} %param.30, f32[512,896]{1,0:T(8,128)} %fusion.46, bf16[512,2048]{1,0:T(8,128)(2,1)} %copy-done.5, bf16[2048,896]{1,0:T(8,128)(2,1)} %param.29), kind=kOutput, calls=%fused_computation.28 | convolution fusion | flops 3761897472 | bytes 13369344 | tf_op jit(solution)/shard_map/dot_general | solution.py:75
  351.4 8.4 %select_reduce_fusion = f32[512,3072]{1,0:T(8,128)} fusion(f32[512,4]{0,1:T(4,128)S(1)} %copy-done.13, s32[512,4]{0,1:T(4,128)S(1)} %multiply_add_fusion), kind=kLoop, calls=%fused_computation.1 | loop fusion | flops 17301504 | bytes 6307840 | tf_op jit(solution)/shard_map/reduce_sum | solution.py:99
  359.8 39.2 %reduce-scatter.9.cloned.1.call-done = bf16[32,48,512]{2,1,0:T(8,128)(2,1)} async-done(((bf16[32,48,2048]{2,1,0:T(8,128)(2,1)}), bf16[32,48,512]{2,1,0:T(8,128)(2,1)}) %reduce-scatter.9.cloned.1.call-update) | async-done | bytes 1572880 | tf_op jit(solution)/shard_map/reduce_scatter | solution.py:113
  399.0 7.5 %all-to-all-start.1 = ((bf16[32,48,512]{2,1,0:T(8,128)(2,1)}), bf16[32,48,512]{2,1,0:T(8,128)(2,1)}, u32[]{:S(2)}, u32[]{:S(2)}) async-start(bf16[32,48,512]{2,1,0:T(8,128)(2,1)} %reduce-scatter.9.cloned.1.call-done), calls=%async_computation.4 | async-start | bytes 3145728 | tf_op jit(solution)/shard_map/all_to_all | solution.py:116
  406.6 9.4 %subtract_convert_fusion = (bf16[512,3072]{1,0:T(8,128)(2,1)}, bf16[512,3072]{1,0:T(8,128)(2,1)}) fusion(f32[512,3072]{1,0:T(8,128)} %select_reduce_fusion), kind=kLoop, calls=%fused_computation.11 | loop fusion | flops 6291456 | bytes 12582912 | tf_op jit(solution)/shard_map/convert_element_type | solution.py:101
  416.0 4.7 %copy.61 = bf16[512,3072]{0,1:T(8,128)(2,1)} copy(bf16[512,3072]{1,0:T(8,128)(2,1)} %get-tuple-element.7) | data formatting | bytes 6291456 | tf_op jit(solution)/shard_map/optimization_barrier | solution.py:102
  420.7 4.8 %copy.64 = bf16[512,3072]{0,1:T(8,128)(2,1)} copy(bf16[512,3072]{1,0:T(8,128)(2,1)} %get-tuple-element.8) | data formatting | bytes 6291456 | tf_op jit(solution)/shard_map/optimization_barrier | solution.py:102
  425.5 3.4 fusion.43
  428.9 1.9 fusion.42
  433.3 4.0 fusion.47
  437.4 2.0 convolution_add_fusion
  439.3 4.9 %fusion.29 = bf16[512,512]{1,0:T(8,128)(2,1)} fusion(f32[512,512]{1,0:T(8,128)} %convolution_add_fusion, f32[512,512]{1,0:T(8,128)} %fusion.47, bf16[512,1536]{0,1:T(8,128)(2,1)} %bitcast.100, bf16[1536,512]{1,0:T(8,128)(2,1)} %bitcast.17, bf16[512,512]{1,0:T(8,128)(2,1)} %reduce-scatter.7.cloned.1.call-done, f32[512,2048]{1,0:T(8,128)} %get-tuple-element.11, ...), kind=kOutput, calls=%fused_computation.46 | convolution fusion | flops 807141376 | bytes 7342084 | tf_op jit(solution)/shard_map/dot_general | solution.py:121
  (61 shorter events, 6.6 us)
Async XLA Ops:
  6.5 240.2 %copy-start = (bf16[2,2048,352]{1,2,0:T(8,128)(2,1)S(1)}, bf16[2,2048,352]{1,2,0:T(8,128)(2,1)}, u32[]{:S(2)}) copy-start(bf16[2,2048,352]{1,2,0:T(8,128)(2,1)} %param.26) | copy-start | bytes 8650756
  6.5 43.7 %reduce-scatter.5.cloned.1.call-start = ((), (), s32[]{:S(2)}) async-start(), calls=%async_computation.7 | async-start | bytes 2621440 | tf_op jit(solution)/shard_map/reduce_scatter | solution.py:64
  9.5 2.0 copy-start.10
  13.7 1.6 copy-start.17
  15.3 35.2 %copy-start.11 = (s32[512,4]{0,1:T(4,128)S(1)}, s32[512,4]{0,1:T(4,128)}, u32[]{:S(2)}) copy-start(s32[512,4]{0,1:T(4,128)} %param.21) | copy-start | bytes 24580
  17.9 64.5 %all-gather.2.cloned.1.call-start = ((), (), s32[]{:S(2)}) async-start(), calls=%async_computation.8 | async-start | bytes 2621440 | tf_op jit(solution)/shard_map/all_gather | solution.py:67
  50.3 282.7 %reduce-scatter.11.cloned.1.call-start = ((), (), s32[]{:S(2)}) async-start(), calls=%async_computation.11 | async-start | bytes 7864320 | tf_op jit(solution)/shard_map/reduce_scatter | solution.py:113
  61.5 26.0 %copy-start.12 = (f32[2048]{0:T(1024)S(1)}, f32[2048]{0:T(1024)}, u32[]{:S(2)}) copy-start(f32[2048]{0:T(1024)} %param.24) | copy-start | bytes 24580
  82.5 5.0 %copy-start.3 = (bf16[512,2048]{1,0:T(8,128)(2,1)S(1)}, bf16[512,2048]{1,0:T(8,128)(2,1)}, u32[]{:S(2)}) copy-start(bf16[512,2048]{1,0:T(8,128)(2,1)} %param.16) | copy-start | bytes 6291460
  82.5 5.0 %copy-start.4 = (bf16[512,2048]{1,0:T(8,128)(2,1)S(1)}, bf16[512,2048]{1,0:T(8,128)(2,1)}, u32[]{:S(2)}) copy-start(bf16[512,2048]{1,0:T(8,128)(2,1)} %all-gather.2.cloned.1.call-done) | copy-start | bytes 6291460
  87.5 1.4 copy-start.9
  88.9 9.9 %copy-start.5 = (bf16[512,2048]{1,0:T(8,128)(2,1)}, bf16[512,2048]{1,0:T(8,128)(2,1)S(1)}, u32[]{:S(2)}) copy-start(bf16[512,2048]{1,0:T(8,128)(2,1)S(1)} %multiply_convert_fusion) | copy-start | bytes 6291460
  246.8 8.6 %copy-start.15 = (bf16[2,2048,352]{1,2,0:T(8,128)(2,1)S(1)}, bf16[2,2048,352]{1,2,0:T(8,128)(2,1)}, u32[]{:S(2)}) copy-start(bf16[2,2048,352]{1,2,0:T(8,128)(2,1)} %param.25) | copy-start | bytes 8650756
  255.3 10.5 %copy-start.16 = (bf16[2,352,2048]{2,1,0:T(8,128)(2,1)S(1)}, bf16[2,352,2048]{2,1,0:T(8,128)(2,1)}, u32[]{:S(2)}) copy-start(bf16[2,352,2048]{2,1,0:T(8,128)(2,1)} %param.27) | copy-start | bytes 8650756
  272.4 126.6 %reduce-scatter.9.cloned.1.call-start = ((), (), s32[]{:S(2)}) async-start(), calls=%async_computation.10 | async-start | bytes 7864320 | tf_op jit(solution)/shard_map/reduce_scatter | solution.py:113
  279.5 1.6 copy-start.6
  333.0 66.0 %all-to-all-start.2 = ((bf16[32,48,512]{2,1,0:T(8,128)(2,1)}), bf16[32,48,512]{2,1,0:T(8,128)(2,1)S(1)}, u32[]{:S(2)}, u32[]{:S(2)}) async-start(bf16[32,48,512]{2,1,0:T(8,128)(2,1)} %reduce-scatter.11.cloned.1.call-done), calls=%async_computation.6 | async-start | bytes 3145728 | tf_op jit(solution)/shard_map/all_to_all | solution.py:116
  340.3 11.1 %copy-start.13 = (f32[512,4]{0,1:T(4,128)S(1)}, f32[512,4]{0,1:T(4,128)}, u32[]{:S(2)}) copy-start(f32[512,4]{0,1:T(4,128)} %param.22) | copy-start | bytes 24580
  340.3 99.1 %reduce-scatter.7.cloned.1.call-start = ((), (), s32[]{:S(2)}) async-start(), calls=%async_computation.9 | async-start | bytes 2621440 | tf_op jit(solution)/shard_map/reduce_scatter | solution.py:76
  399.0 34.3 %all-to-all-start.1 = ((bf16[32,48,512]{2,1,0:T(8,128)(2,1)}), bf16[32,48,512]{2,1,0:T(8,128)(2,1)}, u32[]{:S(2)}, u32[]{:S(2)}) async-start(bf16[32,48,512]{2,1,0:T(8,128)(2,1)} %reduce-scatter.9.cloned.1.call-done), calls=%async_computation.4 | async-start | bytes 3145728 | tf_op jit(solution)/shard_map/all_to_all | solution.py:116
  420.7 4.8 %copy-start.14 = (bf16[2048]{0:T(1024)(128)(2,1)S(1)}, bf16[2048]{0:T(1024)(128)(2,1)}, u32[]{:S(2)}) copy-start(bf16[2048]{0:T(1024)(128)(2,1)} %param.31) | copy-start | bytes 12292
  425.5 3.5 copy-start.2
  428.9 2.7 copy-start.7
  433.3 4.0 copy-start.8
  439.3 4.9 %copy-start.1 = (bf16[2,2048,352]{1,2,0:T(8,128)(2,1)S(1)}, bf16[2,2048,352]{1,2,0:T(8,128)(2,1)}, u32[]{:S(2)}) copy-start(bf16[2,2048,352]{1,2,0:T(8,128)(2,1)} %param.26) | copy-start | bytes 8650756
Sparse Core Ops, SparseCore 0:
  18.0 32.1 reduce-scatter.4
  51.9 30.4 all-gather.1
  272.5 60.4 reduce-scatter.10
  335.3 63.6 reduce-scatter.8
  401.3 29.3 reduce-scatter.6

commit v7 on v6

--- a/solution.py
+++ b/solution.py
@@ -96,12 +96,18 @@
     )
     up_rows = jnp.einsum("sjcd,jdf->sjcf", incoming, expert_up, preferred_element_type=jnp.float32)
     expert_hidden = (jax.nn.silu(gate_rows) * up_rows).astype(jnp.bfloat16)
-    mixing = jnp.sum(jnp.where(hits, route_weights[:, :, None], 0.0), axis=1)
-    mixing_high = mixing.astype(jnp.bfloat16)
-    mixing_low = (mixing - mixing_high.astype(jnp.float32)).astype(jnp.bfloat16)
-    mixing_high, mixing_low = lax.optimization_barrier((mixing_high, mixing_low))
-    mixing_high = mixing_high.reshape(length, ep_count, local_experts, capacity)
-    mixing_low = mixing_low.reshape(length, ep_count, local_experts, capacity)
+    slot_grid = (
+        jnp.arange(ep_count, dtype=jnp.int32)[:, None, None] * local_experts
+        + jnp.arange(local_experts, dtype=jnp.int32)[None, :, None]
+    ) * capacity + jnp.arange(capacity, dtype=jnp.int32)[None, None, :]
+    mixes = []
+    for index in range(local_experts):
+        ids = slot_grid[:, index].reshape(-1)
+        hit = slot[:, :, None] == ids[None, None, :]
+        mixing = jnp.sum(jnp.where(hit, route_weights[:, :, None], 0.0), axis=1)
+        high = mixing.astype(jnp.bfloat16)
+        low = (mixing - high.astype(jnp.float32)).astype(jnp.bfloat16)
+        mixes.append((high, low))
     routed = None
     for index in range(local_experts):
         expert_part = jnp.einsum(
@@ -109,15 +115,14 @@
             expert_hidden[:, index],
             expert_down[index],
             preferred_element_type=jnp.float32,
-        )
-        expert_cols = lax.psum_scatter(
-            expert_part.astype(jnp.bfloat16), "tp", scatter_dimension=2, tiled=True
-        )
+        ).astype(jnp.bfloat16)
+        if index == local_experts - 1:
+            expert_part, mixes = lax.optimization_barrier((expert_part, mixes))
+        expert_cols = lax.psum_scatter(expert_part, "tp", scatter_dimension=2, tiled=True)
         returned = lax.all_to_all(expert_cols, "ep", split_axis=0, concat_axis=0, tiled=True)
         columns = returned.shape[2]
         flat_results = returned.reshape(ep_count * capacity, columns)
-        high = mixing_high[:, :, index].reshape(length, ep_count * capacity)
-        low = mixing_low[:, :, index].reshape(length, ep_count * capacity)
+        high, low = mixes[index]
         term = jnp.dot(high, flat_results, preferred_element_type=jnp.float32) + jnp.dot(
             low, flat_results, preferred_element_type=jnp.float32
         )

time: 456 us -> 452 us (level)
  waiting for transfers between devices: 139 us -> 157 us
  local copies, waits for them, and re-layouts: 20.6 us -> 6.79 us
  other arithmetic: 36.3 us -> 29.3 us
    all_to_all x2, waiting for transfers between devices: 0.01 us -> 19.4 us  [on_device(): lax.all_to_all(expert_cols, 'ep', split_axis=0, concat_axis=0, tiled=True)]
    optimization_barrier x2 -> x0, local copies, waits for them, and re-layouts: 9.47 us -> none  [on_device(): lax.optimization_barrier((mixing_high, mixing_low))]
    slice x2 -> x1, local copies, waits for them, and re-layouts: 5.39 us -> 0.09 us  [on_device(): ids = slot_grid[:, index].reshape(-1)]
    convert_element_type x1 -> x2, other arithmetic: 9.43 us -> 4.35 us  [on_device(): low = (mixing - high.astype(jnp.float32)).astype(jnp.bfloat16)]
  transfers between devices with their start and end apart: 7 -> 7, of which waited for: 4 -> 5; matrix products, arithmetic and copies ran while one was open for 17% -> 12% of each run, Pallas kernels for 0% -> 0%
where the time goes in v7:
time: 452 us; the launch traced here: 449 us
  waiting for transfers between devices  157 us (35%)
  blocking collectives  148 us (33%)
  matrix products  78.5 us (17%)
  other arithmetic  29.3 us (6%)
  starting transfers between devices  15.6 us (3%)
  between operations  13.9 us (3%)
  local copies, waits for them, and re-layouts  6.79 us (2%)
    all_to_all x1, blocking collectives, on_device(): lax.all_to_all(outgoing, 'ep', split_axis=0, concat_axis=0, tiled=True)  148 us
    reduce_scatter x2, waiting for transfers between devices, on_device(): lax.psum_scatter(expert_part, 'tp', scatter_dimension=2, tiled=True)  84.1 us
    reduce_scatter x1, waiting for transfers between devices, on_device(): lax.psum_scatter(partial_value.astype(jnp.bfloat16), 'tp', scatter_dimens...  32.3 us
    all_gather x1, waiting for transfers between devices, on_device(): summed = lax.all_gather(summed_cols, 'tp', axis=1, tiled=True)  21 us
    all_to_all x2, waiting for transfers between devices, on_device(): lax.all_to_all(expert_cols, 'ep', split_axis=0, concat_axis=0, tiled=True)  19.4 us
    all_to_all x2, starting transfers between devices, on_device(): lax.all_to_all(expert_cols, 'ep', split_axis=0, concat_axis=0, tiled=True)  15 us
    dot_general x2, matrix products, on_device(): jnp.einsum('scf,fd->scd', expert_hidden[:, index], expert_down[index], pr...  12 us
    dot_general x1, matrix products, on_device(): jnp.einsum('sjcd,jdf->sjcf', incoming, expert_gate, preferred_element_typ...  10.5 us
  transfers between devices with their start and end apart: 7, of which 5 were waited for; matrix products, arithmetic and copies ran while one was open for 12% of the time, Pallas kernels for 0%

profile of v7, /device:TPU:0, one launch (start us, length us, event | category | flops | bytes accessed | tf_op | source)
XLA Modules:
  0.0 448.9 jit_solution(17792729364290766088)
XLA Ops:
  6.5 1.8 fusion.32
  8.3 1.3 copy.66
  9.6 1.9 fusion.33
  11.5 2.1 fusion.42
  14.2 1.1 copy-done.16
  15.3 2.6 convolution_convert_fusion.4
  18.0 32.3 %reduce-scatter.5.cloned.1.call-done = bf16[512,512]{1,0:T(8,128)(2,1)} async-done(((bf16[512,2048]{1,0:T(8,128)(2,1)}), bf16[512,512]{1,0:T(8,128)(2,1)}) %reduce-scatter.5.cloned.1.call-update) | async-done | bytes 524304 | tf_op jit(solution)/shard_map/reduce_scatter | solution.py:64
  50.8 1.7 fusion.31
  52.9 8.5 %fusion.1 = pred[512,3072]{1,0:T(8,128)(4,1)} fusion(s32[512,4]{0,1:T(4,128)S(1)} %multiply_add_fusion), kind=kLoop, calls=%fused_computation.2 | loop fusion | flops 11010048 | bytes 1581056 | tf_op jit(solution)/shard_map/reduce_or | solution.py:90
  61.4 21.0 %all-gather.2.cloned.1.call-done = bf16[512,2048]{1,0:T(8,128)(2,1)} async-done(((bf16[512,512]{1,0:T(8,128)(2,1)}), bf16[512,2048]{1,0:T(8,128)(2,1)}) %all-gather.2.cloned.1.call-update) | async-done | bytes 2097168 | tf_op jit(solution)/shard_map/all_gather | solution.py:67
  82.5 5.0 %convert_add_fusion = (f32[512,2048]{1,0:T(8,128)}, f32[512]{0:T(512)S(1)}) fusion(bf16[512,2048]{1,0:T(8,128)(2,1)} %all-gather.2.cloned.1.call-done, bf16[512,2048]{1,0:T(8,128)(2,1)} %param.16), kind=kLoop, calls=%fused_computation.23 | loop fusion | flops 5242368 | bytes 8390656 | tf_op jit(solution)/shard_map/add | solution.py:68
  88.9 9.9 %convolution_convert_fusion = bf16[3072,2048]{1,0:T(8,128)(2,1)} fusion(pred[512,3072]{1,0:T(8,128)(4,1)S(1)} %copy-done.6, bf16[512,2048]{1,0:T(8,128)(2,1)S(1)} %multiply_convert_fusion), kind=kOutput, calls=%fused_computation.7 | convolution fusion | flops 6448742400 | bytes 16252928 | tf_op jit(solution)/shard_map/dot_general | solution.py:91
  98.7 148.0 %all_to_all.15 = bf16[32,2,48,2048]{3,2,1,0:T(8,128)(2,1)S(1)} all-to-all(bf16[32,2,48,2048]{3,2,1,0:T(8,128)(2,1)} %bitcast.86), channel_id=1, replica_groups=mesh['ep'=32,'tp'=4] {'ep'}, dimensions={0} | all-to-all | bytes 25165824 | tf_op jit(solution)/shard_map/all_to_all | solution.py:93
  246.8 8.6 %fusion.3 = f32[2,32,48,352]{3,2,1,0:T(8,128)} fusion(bf16[32,2,48,2048]{3,2,1,0:T(8,128)(2,1)S(1)} %all_to_all.15, bf16[2,2048,352]{1,2,0:T(8,128)(2,1)S(1)} %copy-done), kind=kOutput, calls=%fused_computation.8 | convolution fusion | flops 4429185024 | bytes 19791872 | tf_op jit(solution)/shard_map/sjcd,jdf->sjcf/dot_general | solution.py:97
  255.3 10.5 %fusion.7 = bf16[32,2,48,352]{3,2,0,1:T(8,128)(2,1)} fusion(f32[2,32,48,352]{3,2,1,0:T(8,128)} %fusion.3, bf16[2,2048,352]{1,2,0:T(8,128)(2,1)S(1)} %copy-done.13, bf16[32,2,48,2048]{3,2,1,0:T(8,128)(2,1)S(1)} %all_to_all.15), kind=kOutput, calls=%fused_computation.13 | convolution fusion | flops 4435673088 | bytes 21954560 | tf_op jit(solution)/shard_map/sjcd,jdf->sjcf/dot_general | solution.py:94
  265.9 6.6 %convolution_convert_fusion.2 = bf16[32,48,2048]{2,1,0:T(8,128)(2,1)} fusion(bf16[2,352,2048]{2,1,0:T(8,128)(2,1)S(1)} %copy-done.14, bf16[32,2,48,352]{3,2,0,1:T(8,128)(2,1)} %fusion.7), kind=kOutput, calls=%fused_computation.20 | convolution fusion | flops 2217738240 | bytes 8912896 | tf_op jit(solution)/shard_map/scf,fd->scd/dot_general | solution.py:113
  273.3 6.2 %select_reduce_fusion = (f32[512,1536]{1,0:T(8,128)S(1)}, f32[512,1536]{1,0:T(8,128)S(1)}) fusion(s32[1536]{0:T(1024)S(1)} %eq.90, f32[512,4]{0,1:T(4,128)S(1)} %copy-done.11, s32[512,4]{0,1:T(4,128)S(1)} %multiply_add_fusion, s32[1536]{0:T(1024)S(1)} %eq.84), kind=kLoop, calls=%fused_computation.5 | loop fusion | flops 17301504 | bytes 6320128 | tf_op jit(solution)/shard_map/reduce_sum | solution.py:107
  279.5 2.2 subtract_convert_fusion.1
  281.7 2.1 subtract_convert_fusion
  285.4 5.4 %convolution_convert_fusion.1 = bf16[32,48,2048]{2,1,0:T(8,128)(2,1)} fusion(bf16[2,352,2048]{2,1,0:T(8,128)(2,1)S(1)} %copy-done.15, bf16[32,2,48,352]{3,2,0,1:T(8,128)(2,1)S(1)} %copy-done.17), kind=kOutput, calls=%fused_computation.19 | convolution fusion | flops 2217738240 | bytes 8912896 | tf_op jit(solution)/shard_map/scf,fd->scd/dot_general | solution.py:113
  290.8 1.6 copy-done.5
  292.4 5.6 %fusion.44 = f32[512,896]{1,0:T(8,128)} fusion(bf16[512,2048]{1,0:T(8,128)(2,1)S(1)} %copy-done.5, bf16[2048,896]{1,0:T(8,128)(2,1)} %param.28), kind=kOutput, calls=%fused_computation.75 | convolution fusion | flops 1879048192 | bytes 7602176 | tf_op jit(solution)/shard_map/dot_general | solution.py:72
  298.0 9.7 %convolution_convert_fusion.3 = bf16[512,2048]{1,0:T(8,128)(2,1)} fusion(bf16[896,2048]{1,0:T(8,128)(2,1)} %param.30, f32[512,896]{1,0:T(8,128)} %fusion.44, bf16[512,2048]{1,0:T(8,128)(2,1)S(1)} %copy-done.5, bf16[2048,896]{1,0:T(8,128)(2,1)} %param.29), kind=kOutput, calls=%fused_computation.30 | convolution fusion | flops 3761897472 | bytes 13369344 | tf_op jit(solution)/shard_map/dot_general | solution.py:75
  307.7 25.4 %reduce-scatter.9.cloned.1.call-done = bf16[32,48,512]{2,1,0:T(8,128)(2,1)} async-done(((bf16[32,48,2048]{2,1,0:T(8,128)(2,1)}), bf16[32,48,512]{2,1,0:T(8,128)(2,1)}) %reduce-scatter.9.cloned.1.call-update) | async-done | bytes 1572880 | tf_op jit(solution)/shard_map/reduce_scatter | solution.py:121
  333.1 7.4 %all-to-all-start.1 = ((bf16[32,48,512]{2,1,0:T(8,128)(2,1)}), bf16[32,48,512]{2,1,0:T(8,128)(2,1)}, u32[]{:S(2)}, u32[]{:S(2)}) async-start(bf16[32,48,512]{2,1,0:T(8,128)(2,1)} %reduce-scatter.9.cloned.1.call-done), calls=%async_computation.4 | async-start | bytes 3145728 | tf_op jit(solution)/shard_map/all_to_all | solution.py:122
  340.5 58.6 %reduce-scatter.11.cloned.1.call-done = bf16[32,48,512]{2,1,0:T(8,128)(2,1)} async-done(((bf16[32,48,2048]{2,1,0:T(8,128)(2,1)}), bf16[32,48,512]{2,1,0:T(8,128)(2,1)}) %reduce-scatter.11.cloned.1.call-update) | async-done | bytes 1572880 | tf_op jit(solution)/shard_map/reduce_scatter | solution.py:121
  399.1 7.6 %all-to-all-start.2 = ((bf16[32,48,512]{2,1,0:T(8,128)(2,1)}), bf16[32,48,512]{2,1,0:T(8,128)(2,1)}, u32[]{:S(2)}, u32[]{:S(2)}) async-start(bf16[32,48,512]{2,1,0:T(8,128)(2,1)} %reduce-scatter.11.cloned.1.call-done), calls=%async_computation.6 | async-start | bytes 3145728 | tf_op jit(solution)/shard_map/all_to_all | solution.py:122
  407.5 3.8 fusion.45
  411.3 19.4 %all-to-all-done.2 = bf16[32,48,512]{2,1,0:T(8,128)(2,1)} async-done(((bf16[32,48,512]{2,1,0:T(8,128)(2,1)}), bf16[32,48,512]{2,1,0:T(8,128)(2,1)}, u32[]{:S(2)}, u32[]{:S(2)}) %all-to-all-start.2) | async-done | bytes 1572896 | tf_op jit(solution)/shard_map/all_to_all | solution.py:122
  430.7 2.9 fusion.46
  433.5 3.4 convolution_add_fusion
  436.9 4.9 %fusion.29 = bf16[512,512]{1,0:T(8,128)(2,1)} fusion(f32[512,512]{1,0:T(8,128)} %convolution_add_fusion, f32[512,512]{1,0:T(8,128)} %fusion.45, bf16[512,1536]{1,0:T(8,128)(2,1)} %get-tuple-element.17, bf16[1536,512]{1,0:T(8,128)(2,1)} %bitcast.15, bf16[512,512]{1,0:T(8,128)(2,1)} %reduce-scatter.7.cloned.1.call-done, f32[512,2048]{1,0:T(8,128)} %get-tuple-element.19, ...), kind=kOutput, calls=%fused_computation.48 | convolution fusion | flops 807141376 | bytes 7342084 | tf_op jit(solution)/shard_map/dot_general | solution.py:126
  (64 shorter events, 5.9 us)
Async XLA Ops:
  6.5 240.2 %copy-start = (bf16[2,2048,352]{1,2,0:T(8,128)(2,1)S(1)}, bf16[2,2048,352]{1,2,0:T(8,128)(2,1)}, u32[]{:S(2)}) copy-start(bf16[2,2048,352]{1,2,0:T(8,128)(2,1)} %param.26) | copy-start | bytes 8650756
  6.5 43.7 %reduce-scatter.5.cloned.1.call-start = ((), (), s32[]{:S(2)}) async-start(), calls=%async_computation.7 | async-start | bytes 2621440 | tf_op jit(solution)/shard_map/reduce_scatter | solution.py:64
  9.5 2.0 copy-start.8
  13.7 1.6 copy-start.16
  15.3 35.2 %copy-start.9 = (s32[512,4]{0,1:T(4,128)S(1)}, s32[512,4]{0,1:T(4,128)}, u32[]{:S(2)}) copy-start(s32[512,4]{0,1:T(4,128)} %param.21) | copy-start | bytes 24580
  17.9 64.5 %all-gather.2.cloned.1.call-start = ((), (), s32[]{:S(2)}) async-start(), calls=%async_computation.8 | async-start | bytes 2621440 | tf_op jit(solution)/shard_map/all_gather | solution.py:67
  50.3 282.8 %reduce-scatter.9.cloned.1.call-start = ((), (), s32[]{:S(2)}) async-start(), calls=%async_computation.10 | async-start | bytes 7864320 | tf_op jit(solution)/shard_map/reduce_scatter | solution.py:121
  61.4 26.0 %copy-start.10 = (f32[2048]{0:T(1024)S(1)}, f32[2048]{0:T(1024)}, u32[]{:S(2)}) copy-start(f32[2048]{0:T(1024)} %param.24) | copy-start | bytes 24580
  82.5 5.0 %copy-start.2 = (bf16[512,2048]{1,0:T(8,128)(2,1)S(1)}, bf16[512,2048]{1,0:T(8,128)(2,1)}, u32[]{:S(2)}) copy-start(bf16[512,2048]{1,0:T(8,128)(2,1)} %param.16) | copy-start | bytes 6291460
  82.5 5.0 %copy-start.3 = (bf16[512,2048]{1,0:T(8,128)(2,1)S(1)}, bf16[512,2048]{1,0:T(8,128)(2,1)}, u32[]{:S(2)}) copy-start(bf16[512,2048]{1,0:T(8,128)(2,1)} %all-gather.2.cloned.1.call-done) | copy-start | bytes 6291460
  87.5 1.4 copy-start.6
  88.9 9.9 %copy-start.4 = (bf16[512,2048]{1,0:T(8,128)(2,1)}, bf16[512,2048]{1,0:T(8,128)(2,1)S(1)}, u32[]{:S(2)}) copy-start(bf16[512,2048]{1,0:T(8,128)(2,1)S(1)} %multiply_convert_fusion) | copy-start | bytes 6291460
  246.8 8.6 %copy-start.13 = (bf16[2,2048,352]{1,2,0:T(8,128)(2,1)S(1)}, bf16[2,2048,352]{1,2,0:T(8,128)(2,1)}, u32[]{:S(2)}) copy-start(bf16[2,2048,352]{1,2,0:T(8,128)(2,1)} %param.25) | copy-start | bytes 8650756
  255.3 10.5 %copy-start.14 = (bf16[2,352,2048]{2,1,0:T(8,128)(2,1)S(1)}, bf16[2,352,2048]{2,1,0:T(8,128)(2,1)}, u32[]{:S(2)}) copy-start(bf16[2,352,2048]{2,1,0:T(8,128)(2,1)} %param.27) | copy-start | bytes 8650756
  272.5 0.8 copy-start.11
  272.5 126.6 %reduce-scatter.11.cloned.1.call-start = ((), (), s32[]{:S(2)}) async-start(), calls=%async_computation.11 | async-start | bytes 7864320 | tf_op jit(solution)/shard_map/reduce_scatter | solution.py:121
  281.7 2.9 copy-start.15
  281.7 3.7 copy-start.17
  290.7 1.7 copy-start.5
  290.8 146.2 %reduce-scatter.7.cloned.1.call-start = ((), (), s32[]{:S(2)}) async-start(), calls=%async_computation.9 | async-start | bytes 2621440 | tf_op jit(solution)/shard_map/reduce_scatter | solution.py:76
  307.7 99.1 %copy-start.12 = (bf16[2048]{0:T(1024)(128)(2,1)S(1)}, bf16[2048]{0:T(1024)(128)(2,1)}, u32[]{:S(2)}) copy-start(bf16[2048]{0:T(1024)(128)(2,1)} %param.31) | copy-start | bytes 12292
  333.1 66.0 %all-to-all-start.1 = ((bf16[32,48,512]{2,1,0:T(8,128)(2,1)}), bf16[32,48,512]{2,1,0:T(8,128)(2,1)}, u32[]{:S(2)}, u32[]{:S(2)}) async-start(bf16[32,48,512]{2,1,0:T(8,128)(2,1)} %reduce-scatter.9.cloned.1.call-done), calls=%async_computation.4 | async-start | bytes 3145728 | tf_op jit(solution)/shard_map/all_to_all | solution.py:122
  399.1 31.5 %all-to-all-start.2 = ((bf16[32,48,512]{2,1,0:T(8,128)(2,1)}), bf16[32,48,512]{2,1,0:T(8,128)(2,1)}, u32[]{:S(2)}, u32[]{:S(2)}) async-start(bf16[32,48,512]{2,1,0:T(8,128)(2,1)} %reduce-scatter.11.cloned.1.call-done), calls=%async_computation.6 | async-start | bytes 3145728 | tf_op jit(solution)/shard_map/all_to_all | solution.py:122
  411.3 22.2 %copy-start.7 = (bf16[512,1536]{1,0:T(8,128)(2,1)S(1)}, bf16[512,1536]{1,0:T(8,128)(2,1)}, u32[]{:S(2)}) copy-start(bf16[512,1536]{1,0:T(8,128)(2,1)} %get-tuple-element.10) | copy-start | bytes 4718596
  436.9 4.9 %copy-start.1 = (bf16[2,2048,352]{1,2,0:T(8,128)(2,1)S(1)}, bf16[2,2048,352]{1,2,0:T(8,128)(2,1)}, u32[]{:S(2)}) copy-start(bf16[2,2048,352]{1,2,0:T(8,128)(2,1)} %param.26) | copy-start | bytes 8650756
Sparse Core Ops, SparseCore 0:
  18.0 32.1 reduce-scatter.4
  51.9 30.4 all-gather.1
  272.6 60.4 reduce-scatter.8
  335.4 63.6 reduce-scatter.10
  401.4 29.4 reduce-scatter.6

commit v8 on v7

--- a/solution.py
+++ b/solution.py
@@ -91,11 +91,6 @@
     outgoing = jnp.dot(chosen, normed, preferred_element_type=jnp.float32).astype(jnp.bfloat16)
     outgoing = outgoing.reshape(ep_count, local_experts, capacity, width)
     incoming = lax.all_to_all(outgoing, "ep", split_axis=0, concat_axis=0, tiled=True)
-    gate_rows = jnp.einsum(
-        "sjcd,jdf->sjcf", incoming, expert_gate, preferred_element_type=jnp.float32
-    )
-    up_rows = jnp.einsum("sjcd,jdf->sjcf", incoming, expert_up, preferred_element_type=jnp.float32)
-    expert_hidden = (jax.nn.silu(gate_rows) * up_rows).astype(jnp.bfloat16)
     slot_grid = (
         jnp.arange(ep_count, dtype=jnp.int32)[:, None, None] * local_experts
         + jnp.arange(local_experts, dtype=jnp.int32)[None, :, None]
@@ -110,9 +105,17 @@
         mixes.append((high, low))
     routed = None
     for index in range(local_experts):
+        rows = incoming[:, index]
+        gate_rows = jnp.einsum(
+            "scd,df->scf", rows, expert_gate[index], preferred_element_type=jnp.float32
+        )
+        up_rows = jnp.einsum(
+            "scd,df->scf", rows, expert_up[index], preferred_element_type=jnp.float32
+        )
+        expert_hidden = (jax.nn.silu(gate_rows) * up_rows).astype(jnp.bfloat16)
         expert_part = jnp.einsum(
             "scf,fd->scd",
-            expert_hidden[:, index],
+            expert_hidden,
             expert_down[index],
             preferred_element_type=jnp.float32,
         ).astype(jnp.bfloat16)

time: 452 us -> 442 us (0.978)
  waiting for transfers between devices: 157 us -> 144 us
    reduce_scatter x2, waiting for transfers between devices: 84.1 us -> 70.9 us  [on_device(): lax.psum_scatter(expert_part, 'tp', scatter_dimension=2, tiled=True)]
    dot_general x4, matrix products: 31.1 us -> 36 us  [the longest x2 23.3 us: on_device(): jnp.einsum('scf,fd->scd', expert_hidden, expert_down[index], preferred_el...]
  transfers between devices with their start and end apart: 7 -> 7, of which waited for: 5 -> 5; matrix products, arithmetic and copies ran while one was open for 12% -> 15% of each run, Pallas kernels for 0% -> 0%
where the time goes in v8:
time: 442 us; the launch traced here: 439 us
  blocking collectives  148 us (33%)
  waiting for transfers between devices  144 us (33%)
  matrix products  79.6 us (18%)
  other arithmetic  27.9 us (6%)
  starting transfers between devices  15.7 us (4%)
  between operations  13.7 us (3%)
  local copies, waits for them, and re-layouts  9.41 us (2%)
    all_to_all x1, blocking collectives, on_device(): lax.all_to_all(outgoing, 'ep', split_axis=0, concat_axis=0, tiled=True)  148 us
    reduce_scatter x2, waiting for transfers between devices, on_device(): lax.psum_scatter(expert_part, 'tp', scatter_dimension=2, tiled=True)  70.9 us
    reduce_scatter x1, waiting for transfers between devices, on_device(): lax.psum_scatter(partial_value.astype(jnp.bfloat16), 'tp', scatter_dimens...  32.3 us
    dot_general x2, matrix products, on_device(): jnp.einsum('scf,fd->scd', expert_hidden, expert_down[index], preferred_el...  23.3 us
    all_gather x1, waiting for transfers between devices, on_device(): summed = lax.all_gather(summed_cols, 'tp', axis=1, tiled=True)  20.7 us
    all_to_all x2, waiting for transfers between devices, on_device(): lax.all_to_all(expert_cols, 'ep', split_axis=0, concat_axis=0, tiled=True)  20.3 us
    all_to_all x2, starting transfers between devices, on_device(): lax.all_to_all(expert_cols, 'ep', split_axis=0, concat_axis=0, tiled=True)  14.7 us
    dot_general x2, matrix products, on_device(): jnp.einsum('scd,df->scf', rows, expert_gate[index], preferred_element_typ...  12.7 us
  transfers between devices with their start and end apart: 7, of which 5 were waited for; matrix products, arithmetic and copies ran while one was open for 15% of the time, Pallas kernels for 0%

profile of v8, /device:TPU:0, one launch (start us, length us, event | category | flops | bytes accessed | tf_op | source)
XLA Modules:
  0.0 438.6 jit_solution(13100347129434381819)
XLA Ops:
  7.6 1.3 copy.64
  8.9 1.9 fusion.35
  10.8 2.1 fusion.46
  13.4 2.6 convolution_convert_fusion.4
  16.1 32.3 %reduce-scatter.5.cloned.1.call-done = bf16[512,512]{1,0:T(8,128)(2,1)} async-done(((bf16[512,2048]{1,0:T(8,128)(2,1)}), bf16[512,512]{1,0:T(8,128)(2,1)}) %reduce-scatter.5.cloned.1.call-update) | async-done | bytes 524304 | tf_op jit(solution)/shard_map/reduce_scatter | solution.py:64
  49.4 1.7 fusion.29
  51.4 8.5 %fusion.1 = pred[512,3072]{1,0:T(8,128)(4,1)} fusion(s32[512,4]{0,1:T(4,128)S(1)} %multiply_add_fusion), kind=kLoop, calls=%fused_computation.2 | loop fusion | flops 11010048 | bytes 1581056 | tf_op jit(solution)/shard_map/reduce_or | solution.py:90
  60.0 20.7 %all-gather.2.cloned.1.call-done = bf16[512,2048]{1,0:T(8,128)(2,1)} async-done(((bf16[512,512]{1,0:T(8,128)(2,1)}), bf16[512,2048]{1,0:T(8,128)(2,1)}) %all-gather.2.cloned.1.call-update) | async-done | bytes 2097168 | tf_op jit(solution)/shard_map/all_gather | solution.py:67
  80.6 4.4 convert_add_fusion
  85.0 1.0 multiply_convert_fusion
  86.4 7.2 %convolution_convert_fusion = bf16[3072,2048]{1,0:T(8,128)(2,1)S(1)} fusion(pred[512,3072]{1,0:T(8,128)(4,1)S(1)} %copy-done.7, bf16[512,2048]{1,0:T(8,128)(2,1)S(1)} %multiply_convert_fusion), kind=kOutput, calls=%fused_computation.7 | convolution fusion | flops 6448742400 | bytes 16252928 | tf_op jit(solution)/shard_map/dot_general | solution.py:91
  93.7 148.1 %all_to_all.15 = bf16[32,2,48,2048]{3,2,1,0:T(8,128)(2,1)S(1)} all-to-all(bf16[32,2,48,2048]{3,2,1,0:T(8,128)(2,1)S(1)} %bitcast.91), channel_id=1, replica_groups=mesh['ep'=32,'tp'=4] {'ep'}, dimensions={0} | all-to-all | bytes 25165824 | tf_op jit(solution)/shard_map/all_to_all | solution.py:93
  241.7 4.6 %copy-done.2 = bf16[32,2,48,2048]{3,2,1,0:T(8,128)(2,1)} copy-done((bf16[32,2,48,2048]{3,2,1,0:T(8,128)(2,1)}, bf16[32,2,48,2048]{3,2,1,0:T(8,128)(2,1)S(1)}, u32[]{:S(2)}) %copy-start.2) | copy-done | bytes 12582936
  246.3 5.0 %fusion.4 = f32[32,48,352]{2,1,0:T(8,128)} fusion(bf16[32,2,48,2048]{3,2,1,0:T(8,128)(2,1)S(1)} %all_to_all.15, bf16[2,2048,352]{1,2,0:T(8,128)(2,1)S(1)} %copy-done.13), kind=kOutput, calls=%fused_computation.11 | convolution fusion | flops 2214592512 | bytes 9895936 | tf_op jit(solution)/shard_map/scd,df->scf/dot_general | solution.py:109
  251.3 11.6 %convolution_convert_fusion.2 = bf16[32,48,2048]{2,1,0:T(8,128)(2,1)} fusion(bf16[2,352,2048]{2,1,0:T(8,128)(2,1)} %param.27, f32[32,48,352]{2,1,0:T(8,128)} %fusion.4, bf16[32,2,48,2048]{3,2,1,0:T(8,128)(2,1)} %copy-done.2, bf16[2,2048,352]{1,2,0:T(8,128)(2,1)} %param.26), kind=kOutput, calls=%fused_computation.15 | convolution fusion | flops 4435574784 | bytes 17825792 | tf_op jit(solution)/shard_map/scf,fd->scd/dot_general | solution.py:116
  263.6 6.4 %select_reduce_fusion = (f32[512,1536]{1,0:T(8,128)S(1)}, f32[512,1536]{1,0:T(8,128)S(1)}) fusion(s32[1536]{0:T(1024)S(1)} %eq.90, f32[512,4]{0,1:T(4,128)S(1)} %copy-done.11, s32[512,4]{0,1:T(4,128)S(1)} %multiply_add_fusion, s32[1536]{0:T(1024)S(1)} %eq.84), kind=kLoop, calls=%fused_computation.5 | loop fusion | flops 17301504 | bytes 6320128 | tf_op jit(solution)/shard_map/reduce_sum | solution.py:102
  270.0 2.0 subtract_convert_fusion.1
  272.1 2.1 subtract_convert_fusion
  275.0 7.8 %fusion.6 = f32[32,48,352]{2,1,0:T(8,128)} fusion(bf16[32,2,48,2048]{3,2,1,0:T(8,128)(2,1)} %copy-done.2, bf16[2,2048,352]{1,2,0:T(8,128)(2,1)S(1)} %copy-done.14), kind=kOutput, calls=%fused_computation.13 | convolution fusion | flops 2214592512 | bytes 9895936 | tf_op jit(solution)/shard_map/scd,df->scf/dot_general | solution.py:109
  282.7 11.6 %convolution_convert_fusion.1 = bf16[32,48,2048]{2,1,0:T(8,128)(2,1)} fusion(bf16[2,352,2048]{2,1,0:T(8,128)(2,1)} %param.27, f32[32,48,352]{2,1,0:T(8,128)} %fusion.6, bf16[32,2,48,2048]{3,2,1,0:T(8,128)(2,1)} %copy-done.2, bf16[2,2048,352]{1,2,0:T(8,128)(2,1)} %param.26), kind=kOutput, calls=%fused_computation.14 | convolution fusion | flops 4435574784 | bytes 17825792 | tf_op jit(solution)/shard_map/scf,fd->scd/dot_general | solution.py:116
  294.7 1.3 copy-done.6
  296.0 5.6 %fusion.48 = f32[512,896]{1,0:T(8,128)} fusion(bf16[512,2048]{1,0:T(8,128)(2,1)S(1)} %copy-done.6, bf16[2048,896]{1,0:T(8,128)(2,1)} %param.28), kind=kOutput, calls=%fused_computation.78 | convolution fusion | flops 1879048192 | bytes 7602176 | tf_op jit(solution)/shard_map/dot_general | solution.py:72
  301.6 9.7 %convolution_convert_fusion.3 = bf16[512,2048]{1,0:T(8,128)(2,1)} fusion(bf16[896,2048]{1,0:T(8,128)(2,1)} %param.30, f32[512,896]{1,0:T(8,128)} %fusion.48, bf16[512,2048]{1,0:T(8,128)(2,1)S(1)} %copy-done.6, bf16[2048,896]{1,0:T(8,128)(2,1)} %param.29), kind=kOutput, calls=%fused_computation.25 | convolution fusion | flops 3761897472 | bytes 13369344 | tf_op jit(solution)/shard_map/dot_general | solution.py:75
  311.3 12.2 %reduce-scatter.9.cloned.1.call-done = bf16[32,48,512]{2,1,0:T(8,128)(2,1)} async-done(((bf16[32,48,2048]{2,1,0:T(8,128)(2,1)}), bf16[32,48,512]{2,1,0:T(8,128)(2,1)}) %reduce-scatter.9.cloned.1.call-update) | async-done | bytes 1572880 | tf_op jit(solution)/shard_map/reduce_scatter | solution.py:124
  323.5 7.4 %all-to-all-start.1 = ((bf16[32,48,512]{2,1,0:T(8,128)(2,1)}), bf16[32,48,512]{2,1,0:T(8,128)(2,1)}, u32[]{:S(2)}, u32[]{:S(2)}) async-start(bf16[32,48,512]{2,1,0:T(8,128)(2,1)} %reduce-scatter.9.cloned.1.call-done), calls=%async_computation.4 | async-start | bytes 3145728 | tf_op jit(solution)/shard_map/all_to_all | solution.py:125
  330.9 58.6 %reduce-scatter.11.cloned.1.call-done = bf16[32,48,512]{2,1,0:T(8,128)(2,1)} async-done(((bf16[32,48,2048]{2,1,0:T(8,128)(2,1)}), bf16[32,48,512]{2,1,0:T(8,128)(2,1)}) %reduce-scatter.11.cloned.1.call-update) | async-done | bytes 1572880 | tf_op jit(solution)/shard_map/reduce_scatter | solution.py:124
  389.5 7.4 %all-to-all-start.2 = ((bf16[32,48,512]{2,1,0:T(8,128)(2,1)}), bf16[32,48,512]{2,1,0:T(8,128)(2,1)}, u32[]{:S(2)}, u32[]{:S(2)}) async-start(bf16[32,48,512]{2,1,0:T(8,128)(2,1)} %reduce-scatter.11.cloned.1.call-done), calls=%async_computation.6 | async-start | bytes 3145728 | tf_op jit(solution)/shard_map/all_to_all | solution.py:125
  397.6 2.9 fusion.49
  400.5 20.3 %all-to-all-done.2 = bf16[32,48,512]{2,1,0:T(8,128)(2,1)} async-done(((bf16[32,48,512]{2,1,0:T(8,128)(2,1)}), bf16[32,48,512]{2,1,0:T(8,128)(2,1)}, u32[]{:S(2)}, u32[]{:S(2)}) %all-to-all-start.2) | async-done | bytes 1572896 | tf_op jit(solution)/shard_map/all_to_all | solution.py:125
  420.8 3.0 fusion.50
  423.8 3.4 convolution_add_fusion
  427.2 4.7 %fusion.27 = bf16[512,512]{1,0:T(8,128)(2,1)} fusion(f32[512,512]{1,0:T(8,128)} %convolution_add_fusion, f32[512,512]{1,0:T(8,128)S(1)} %fusion.49, bf16[512,1536]{1,0:T(8,128)(2,1)} %get-tuple-element.17, bf16[1536,512]{1,0:T(8,128)(2,1)} %bitcast.13, bf16[512,512]{1,0:T(8,128)(2,1)} %reduce-scatter.7.cloned.1.call-done, ...), kind=kOutput, calls=%fused_computation.51 | convolution fusion | flops 807141376 | bytes 7342084 | tf_op jit(solution)/shard_map/dot_general | solution.py:129
  (58 shorter events, 5.7 us)
Async XLA Ops:
  6.5 6.9 %copy-start = (bf16[512,2048]{1,0:T(8,128)(2,1)S(1)}, bf16[512,2048]{1,0:T(8,128)(2,1)}, u32[]{:S(2)}) copy-start(bf16[512,2048]{1,0:T(8,128)(2,1)} %param.23) | copy-start | bytes 6291460
  6.5 41.9 %reduce-scatter.5.cloned.1.call-start = ((), (), s32[]{:S(2)}) async-start(), calls=%async_computation.7 | async-start | bytes 2621440 | tf_op jit(solution)/shard_map/reduce_scatter | solution.py:64
  16.0 33.0 %copy-start.9 = (s32[512,4]{0,1:T(4,128)S(1)}, s32[512,4]{0,1:T(4,128)}, u32[]{:S(2)}) copy-start(s32[512,4]{0,1:T(4,128)} %param.21) | copy-start | bytes 24580
  16.1 64.6 %all-gather.2.cloned.1.call-start = ((), (), s32[]{:S(2)}) async-start(), calls=%async_computation.8 | async-start | bytes 2621440 | tf_op jit(solution)/shard_map/all_gather | solution.py:67
  48.5 275.1 %reduce-scatter.9.cloned.1.call-start = ((), (), s32[]{:S(2)}) async-start(), calls=%async_computation.10 | async-start | bytes 7864320 | tf_op jit(solution)/shard_map/reduce_scatter | solution.py:124
  51.0 29.6 %copy-start.3 = (bf16[512,2048]{1,0:T(8,128)(2,1)S(1)}, bf16[512,2048]{1,0:T(8,128)(2,1)}, u32[]{:S(2)}) copy-start(bf16[512,2048]{1,0:T(8,128)(2,1)} %param.16) | copy-start | bytes 6291460
  60.0 25.1 %copy-start.10 = (f32[2048]{0:T(1024)S(1)}, f32[2048]{0:T(1024)}, u32[]{:S(2)}) copy-start(f32[2048]{0:T(1024)} %param.24) | copy-start | bytes 24580
  80.6 4.4 copy-start.4
  85.0 1.4 copy-start.7
  86.4 7.2 %copy-start.5 = (bf16[512,2048]{1,0:T(8,128)(2,1)}, bf16[512,2048]{1,0:T(8,128)(2,1)S(1)}, u32[]{:S(2)}) copy-start(bf16[512,2048]{1,0:T(8,128)(2,1)S(1)} %multiply_convert_fusion) | copy-start | bytes 6291460
  93.6 152.7 %copy-start.13 = (bf16[2,2048,352]{1,2,0:T(8,128)(2,1)S(1)}, bf16[2,2048,352]{1,2,0:T(8,128)(2,1)}, u32[]{:S(2)}) copy-start(bf16[2,2048,352]{1,2,0:T(8,128)(2,1)} %param.25) | copy-start | bytes 8650756
  241.7 4.6 %copy-start.2 = (bf16[32,2,48,2048]{3,2,1,0:T(8,128)(2,1)}, bf16[32,2,48,2048]{3,2,1,0:T(8,128)(2,1)S(1)}, u32[]{:S(2)}) copy-start(bf16[32,2,48,2048]{3,2,1,0:T(8,128)(2,1)S(1)} %all_to_all.15) | copy-start | bytes 37748740
  262.9 0.7 copy-start.11
  262.9 126.6 %reduce-scatter.11.cloned.1.call-start = ((), (), s32[]{:S(2)}) async-start(), calls=%async_computation.11 | async-start | bytes 7864320 | tf_op jit(solution)/shard_map/reduce_scatter | solution.py:124
  272.1 2.9 copy-start.14
  294.4 1.6 copy-start.6
  294.4 132.8 %reduce-scatter.7.cloned.1.call-start = ((), (), s32[]{:S(2)}) async-start(), calls=%async_computation.9 | async-start | bytes 2621440 | tf_op jit(solution)/shard_map/reduce_scatter | solution.py:76
  323.5 66.0 %all-to-all-start.1 = ((bf16[32,48,512]{2,1,0:T(8,128)(2,1)}), bf16[32,48,512]{2,1,0:T(8,128)(2,1)}, u32[]{:S(2)}, u32[]{:S(2)}) async-start(bf16[32,48,512]{2,1,0:T(8,128)(2,1)} %reduce-scatter.9.cloned.1.call-done), calls=%async_computation.4 | async-start | bytes 3145728 | tf_op jit(solution)/shard_map/all_to_all | solution.py:125
  330.9 66.0 %copy-start.12 = (bf16[2048]{0:T(1024)(128)(2,1)S(1)}, bf16[2048]{0:T(1024)(128)(2,1)}, u32[]{:S(2)}) copy-start(bf16[2048]{0:T(1024)(128)(2,1)} %param.31) | copy-start | bytes 12292
  389.5 31.3 %all-to-all-start.2 = ((bf16[32,48,512]{2,1,0:T(8,128)(2,1)}), bf16[32,48,512]{2,1,0:T(8,128)(2,1)}, u32[]{:S(2)}, u32[]{:S(2)}) async-start(bf16[32,48,512]{2,1,0:T(8,128)(2,1)} %reduce-scatter.11.cloned.1.call-done), calls=%async_computation.6 | async-start | bytes 3145728 | tf_op jit(solution)/shard_map/all_to_all | solution.py:125
  420.8 3.0 copy-start.8
  427.2 4.7 %copy-start.1 = (bf16[512,2048]{1,0:T(8,128)(2,1)S(1)}, bf16[512,2048]{1,0:T(8,128)(2,1)}, u32[]{:S(2)}) copy-start(bf16[512,2048]{1,0:T(8,128)(2,1)} %param.23) | copy-start | bytes 6291460
Sparse Core Ops, SparseCore 0:
  16.2 32.1 reduce-scatter.4
  50.1 30.4 all-gather.1
  263.0 60.4 reduce-scatter.8
  325.8 63.6 reduce-scatter.10
  391.8 29.4 reduce-scatter.6

commit v9 on v8

--- a/solution.py
+++ b/solution.py
@@ -88,9 +88,7 @@
     slot_ids = jnp.arange(experts * capacity, dtype=jnp.int32)
     hits = slot[:, :, None] == slot_ids[None, None, :]
     chosen = jnp.any(hits, axis=1).T.astype(jnp.bfloat16)
-    outgoing = jnp.dot(chosen, normed, preferred_element_type=jnp.float32).astype(jnp.bfloat16)
-    outgoing = outgoing.reshape(ep_count, local_experts, capacity, width)
-    incoming = lax.all_to_all(outgoing, "ep", split_axis=0, concat_axis=0, tiled=True)
+    chosen = chosen.reshape(ep_count, local_experts, capacity, length)
     slot_grid = (
         jnp.arange(ep_count, dtype=jnp.int32)[:, None, None] * local_experts
         + jnp.arange(local_experts, dtype=jnp.int32)[None, :, None]
@@ -105,7 +103,10 @@
         mixes.append((high, low))
     routed = None
     for index in range(local_experts):
-        rows = incoming[:, index]
+        outgoing = jnp.einsum(
+            "sct,td->scd", chosen[:, index], normed, preferred_element_type=jnp.float32
+        ).astype(jnp.bfloat16)
+        rows = lax.all_to_all(outgoing, "ep", split_axis=0, concat_axis=0, tiled=True)
         gate_rows = jnp.einsum(
             "scd,df->scf", rows, expert_gate[index], preferred_element_type=jnp.float32
         )

time: 442 us -> 414 us (0.937)
  blocking collectives: 148 us -> 80.7 us
  waiting for transfers between devices: 144 us -> 175 us
    all_to_all x1, blocking collectives: 148 us -> 80.7 us  [on_device(): lax.all_to_all(outgoing, 'ep', split_axis=0, concat_axis=0, tiled=True)]
    all_to_all x0 -> x1, waiting for transfers between devices: none -> 66.8 us  [on_device(): lax.all_to_all(outgoing, 'ep', split_axis=0, concat_axis=0, tiled=True)]
    reduce_scatter x2, waiting for transfers between devices: 70.9 us -> 39.7 us  [on_device(): lax.psum_scatter(expert_part, 'tp', scatter_dimension=2, tiled=True)]
    all_to_all x0 -> x1, starting transfers between devices: none -> 5.25 us  [on_device(): lax.all_to_all(outgoing, 'ep', split_axis=0, concat_axis=0, tiled=True)]
    all_gather x1, waiting for transfers between devices: 20.7 us -> 16 us  [on_device(): summed = lax.all_gather(summed_cols, 'tp', axis=1, tiled=True)]
    transpose x0 -> x1, local copies, waits for them, and re-layouts: none -> 4.67 us  [on_device(): chosen = jnp.any(hits, axis=1).T.astype(jnp.bfloat16)]
    dot_general x3 -> x4, matrix products: 19.9 us -> 23.1 us  [the longest x2 13 us: on_device(): jnp.einsum('scd,df->scf', rows, expert_up[index], preferred_element_type=...]
  transfers between devices with their start and end apart: 7 -> 8, of which waited for: 5 -> 5; matrix products, arithmetic and copies ran while one was open for 15% -> 19% of each run, Pallas kernels for 0% -> 0%
where the time goes in v9:
time: 414 us; the launch traced here: 410 us
  waiting for transfers between devices  175 us (42%)
  matrix products  83 us (20%)
  blocking collectives  80.7 us (19%)
  other arithmetic  28 us (7%)
  starting transfers between devices  18.3 us (4%)
  between operations  13.7 us (3%)
  local copies, waits for them, and re-layouts  11.5 us (3%)
    all_to_all x1, blocking collectives, on_device(): lax.all_to_all(outgoing, 'ep', split_axis=0, concat_axis=0, tiled=True)  80.7 us
    all_to_all x1, waiting for transfers between devices, on_device(): lax.all_to_all(outgoing, 'ep', split_axis=0, concat_axis=0, tiled=True)  66.8 us
    reduce_scatter x2, waiting for transfers between devices, on_device(): lax.psum_scatter(expert_part, 'tp', scatter_dimension=2, tiled=True)  39.7 us
    reduce_scatter x1, waiting for transfers between devices, on_device(): lax.psum_scatter(partial_value.astype(jnp.bfloat16), 'tp', scatter_dimens...  32.3 us
    dot_general x2, matrix products, on_device(): jnp.einsum('scf,fd->scd', expert_hidden, expert_down[index], preferred_el...  23.4 us
    all_to_all x2, waiting for transfers between devices, on_device(): lax.all_to_all(expert_cols, 'ep', split_axis=0, concat_axis=0, tiled=True)  20.3 us
    all_gather x1, waiting for transfers between devices, on_device(): summed = lax.all_gather(summed_cols, 'tp', axis=1, tiled=True)  16 us
    dot_general x2, matrix products, on_device(): jnp.einsum('scd,df->scf', rows, expert_up[index], preferred_element_type=...  13 us
  transfers between devices with their start and end apart: 8, of which 5 were waited for; matrix products, arithmetic and copies ran while one was open for 19% of the time, Pallas kernels for 0%

profile of v9, /device:TPU:0, one launch (start us, length us, event | category | flops | bytes accessed | tf_op | source)
XLA Modules:
  0.0 410.3 jit_solution(2158450491494048193)
XLA Ops:
  8.9 1.9 fusion.35
  10.8 2.1 fusion.46
  13.4 2.6 convolution_convert_fusion.5
  16.1 32.3 %reduce-scatter.5.cloned.1.call-done = bf16[512,512]{1,0:T(8,128)(2,1)} async-done(((bf16[512,2048]{1,0:T(8,128)(2,1)}), bf16[512,512]{1,0:T(8,128)(2,1)}) %reduce-scatter.5.cloned.1.call-update) | async-done | bytes 524304 | tf_op jit(solution)/shard_map/reduce_scatter | solution.py:64
  49.4 1.7 fusion.29
  51.4 8.5 %fusion.1 = pred[512,3072]{1,0:T(8,128)(4,1)} fusion(s32[512,4]{0,1:T(4,128)S(1)} %multiply_add_fusion), kind=kLoop, calls=%fused_computation.2 | loop fusion | flops 11010048 | bytes 1581056 | tf_op jit(solution)/shard_map/reduce_or | solution.py:90
  60.0 4.7 %copy.52 = pred[3072,512]{1,0:T(8,128)(4,1)} copy(pred[3072,512]{0,1:T(8,128)(4,1)} %bitcast.89) | data formatting | bytes 3145728 | tf_op jit(solution)/shard_map/transpose | solution.py:90
  64.6 16.0 %all-gather.2.cloned.1.call-done = bf16[512,2048]{1,0:T(8,128)(2,1)} async-done(((bf16[512,512]{1,0:T(8,128)(2,1)}), bf16[512,2048]{1,0:T(8,128)(2,1)}) %all-gather.2.cloned.1.call-update) | async-done | bytes 2097168 | tf_op jit(solution)/shard_map/all_gather | solution.py:67
  80.6 4.4 %convert_add_fusion = (f32[512,2048]{1,0:T(8,128)}, f32[512]{0:T(512)S(1)}) fusion(bf16[512,2048]{1,0:T(8,128)(2,1)} %all-gather.2.cloned.1.call-done, bf16[512,2048]{1,0:T(8,128)(2,1)S(1)} %copy-done.2), kind=kLoop, calls=%fused_computation.13 | loop fusion | flops 5242368 | bytes 8390656 | tf_op jit(solution)/shard_map/add | solution.py:68
  86.5 3.6 convolution_convert_fusion.3
  90.2 80.7 %all_to_all.20 = bf16[32,48,2048]{2,1,0:T(8,128)(2,1)S(1)} all-to-all(bf16[32,48,2048]{2,1,0:T(8,128)(2,1)S(1)} %convolution_convert_fusion.3), channel_id=1, replica_groups=mesh['ep'=32,'tp'=4] {'ep'}, dimensions={0} | all-to-all | bytes 12582912 | tf_op jit(solution)/shard_map/all_to_all | solution.py:109
  170.8 2.7 copy-done.6
  173.5 5.0 %fusion.16 = f32[32,48,352]{2,1,0:T(8,128)} fusion(bf16[32,48,2048]{2,1,0:T(8,128)(2,1)S(1)} %all_to_all.20, bf16[2,2048,352]{1,2,0:T(8,128)(2,1)S(1)} %copy-done.13), kind=kOutput, calls=%fused_computation.39 | convolution fusion | flops 2214592512 | bytes 9895936 | tf_op jit(solution)/shard_map/scd,df->scf/dot_general | solution.py:113
  178.5 11.7 %convolution_convert_fusion.1 = bf16[32,48,2048]{2,1,0:T(8,128)(2,1)} fusion(bf16[2,352,2048]{2,1,0:T(8,128)(2,1)} %param.27, f32[32,48,352]{2,1,0:T(8,128)} %fusion.16, bf16[32,48,2048]{2,1,0:T(8,128)(2,1)} %copy-done.6, bf16[2,2048,352]{1,2,0:T(8,128)(2,1)} %param.25), kind=kOutput, calls=%fused_computation.8 | convolution fusion | flops 4435574784 | bytes 17825792 | tf_op jit(solution)/shard_map/scf,fd->scd/dot_general | solution.py:117
  191.8 6.5 %convolution_convert_fusion.2 = bf16[32,48,2048]{2,1,0:T(8,128)(2,1)} fusion(pred[32,2,48,512]{3,2,1,0:T(8,128)(4,1)} %bitcast.90, bf16[512,2048]{1,0:T(8,128)(2,1)S(1)} %copy-done.5), kind=kOutput, calls=%fused_computation.9 | convolution fusion | flops 3224371200 | bytes 9175040 | tf_op jit(solution)/shard_map/sct,td->scd/dot_general | solution.py:106
  198.3 5.2 %all-to-all-start.2 = ((bf16[32,48,2048]{2,1,0:T(8,128)(2,1)}), bf16[32,48,2048]{2,1,0:T(8,128)(2,1)}, u32[]{:S(2)}, u32[]{:S(2)}) async-start(bf16[32,48,2048]{2,1,0:T(8,128)(2,1)} %convolution_convert_fusion.2), calls=%async_computation.5 | async-start | bytes 12582912 | tf_op jit(solution)/shard_map/all_to_all | solution.py:109
  204.0 6.2 %select_reduce_fusion = (f32[512,1536]{1,0:T(8,128)S(1)}, f32[512,1536]{1,0:T(8,128)S(1)}) fusion(s32[1536]{0:T(1024)S(1)} %eq.90, f32[512,4]{0,1:T(4,128)S(1)} %copy-done.11, s32[512,4]{0,1:T(4,128)S(1)} %multiply_add_fusion, s32[1536]{0:T(1024)S(1)} %eq.84), kind=kLoop, calls=%fused_computation.5 | loop fusion | flops 17301504 | bytes 6320128 | tf_op jit(solution)/shard_map/reduce_sum | solution.py:100
  210.2 2.2 subtract_convert_fusion.1
  212.4 2.2 subtract_convert_fusion
  214.6 66.8 %all-to-all-done.2 = bf16[32,48,2048]{2,1,0:T(8,128)(2,1)} async-done(((bf16[32,48,2048]{2,1,0:T(8,128)(2,1)}), bf16[32,48,2048]{2,1,0:T(8,128)(2,1)}, u32[]{:S(2)}, u32[]{:S(2)}) %all-to-all-start.2) | async-done | bytes 6291488 | tf_op jit(solution)/shard_map/all_to_all | solution.py:109
  281.4 8.1 %fusion.12 = f32[32,48,352]{2,1,0:T(8,128)} fusion(bf16[32,48,2048]{2,1,0:T(8,128)(2,1)} %all-to-all-done.2, bf16[2,2048,352]{1,2,0:T(8,128)(2,1)} %param.26), kind=kOutput, calls=%fused_computation.35 | convolution fusion | flops 2214592512 | bytes 9895936 | tf_op jit(solution)/shard_map/scd,df->scf/dot_general | solution.py:113
  289.5 11.7 %convolution_convert_fusion = bf16[32,48,2048]{2,1,0:T(8,128)(2,1)} fusion(bf16[2,352,2048]{2,1,0:T(8,128)(2,1)} %param.27, f32[32,48,352]{2,1,0:T(8,128)} %fusion.12, bf16[32,48,2048]{2,1,0:T(8,128)(2,1)} %all-to-all-done.2, bf16[2,2048,352]{1,2,0:T(8,128)(2,1)} %param.25), kind=kOutput, calls=%fused_computation.7 | convolution fusion | flops 4435574784 | bytes 17825792 | tf_op jit(solution)/shard_map/scf,fd->scd/dot_general | solution.py:117
  301.5 5.6 %fusion.48 = f32[512,896]{1,0:T(8,128)} fusion(bf16[512,2048]{1,0:T(8,128)(2,1)S(1)} %copy-done.5, bf16[2048,896]{1,0:T(8,128)(2,1)} %param.28), kind=kOutput, calls=%fused_computation.79 | convolution fusion | flops 1879048192 | bytes 7602176 | tf_op jit(solution)/shard_map/dot_general | solution.py:72
  307.1 9.6 %convolution_convert_fusion.4 = bf16[512,2048]{1,0:T(8,128)(2,1)} fusion(bf16[896,2048]{1,0:T(8,128)(2,1)} %param.30, f32[512,896]{1,0:T(8,128)} %fusion.48, bf16[512,2048]{1,0:T(8,128)(2,1)S(1)} %copy-done.5, bf16[2048,896]{1,0:T(8,128)(2,1)} %param.29), kind=kOutput, calls=%fused_computation.22 | convolution fusion | flops 3761897472 | bytes 13369344 | tf_op jit(solution)/shard_map/dot_general | solution.py:75
  316.8 4.7 %all-to-all-start.1 = ((bf16[32,48,512]{2,1,0:T(8,128)(2,1)}), bf16[32,48,512]{2,1,0:T(8,128)(2,1)}, u32[]{:S(2)}, u32[]{:S(2)}) async-start(bf16[32,48,512]{2,1,0:T(8,128)(2,1)} %reduce-scatter.9.cloned.1.call-done), calls=%async_computation.4 | async-start | bytes 3145728 | tf_op jit(solution)/shard_map/all_to_all | solution.py:126
  321.5 39.7 %reduce-scatter.11.cloned.1.call-done = bf16[32,48,512]{2,1,0:T(8,128)(2,1)} async-done(((bf16[32,48,2048]{2,1,0:T(8,128)(2,1)}), bf16[32,48,512]{2,1,0:T(8,128)(2,1)}) %reduce-scatter.11.cloned.1.call-update) | async-done | bytes 1572880 | tf_op jit(solution)/shard_map/reduce_scatter | solution.py:125
  361.2 7.4 %all-to-all-start.3 = ((bf16[32,48,512]{2,1,0:T(8,128)(2,1)}), bf16[32,48,512]{2,1,0:T(8,128)(2,1)}, u32[]{:S(2)}, u32[]{:S(2)}) async-start(bf16[32,48,512]{2,1,0:T(8,128)(2,1)} %reduce-scatter.11.cloned.1.call-done), calls=%async_computation.7 | async-start | bytes 3145728 | tf_op jit(solution)/shard_map/all_to_all | solution.py:126
  369.2 2.9 fusion.49
  372.1 20.3 %all-to-all-done.3 = bf16[32,48,512]{2,1,0:T(8,128)(2,1)} async-done(((bf16[32,48,512]{2,1,0:T(8,128)(2,1)}), bf16[32,48,512]{2,1,0:T(8,128)(2,1)}, u32[]{:S(2)}, u32[]{:S(2)}) %all-to-all-start.3) | async-done | bytes 1572896 | tf_op jit(solution)/shard_map/all_to_all | solution.py:126
  392.4 3.0 fusion.50
  395.4 3.4 convolution_add_fusion
  398.8 4.7 %fusion.27 = bf16[512,512]{1,0:T(8,128)(2,1)} fusion(f32[512,512]{1,0:T(8,128)} %convolution_add_fusion, f32[512,512]{1,0:T(8,128)S(1)} %fusion.49, bf16[512,1536]{1,0:T(8,128)(2,1)} %get-tuple-element.17, bf16[1536,512]{1,0:T(8,128)(2,1)} %bitcast.15, bf16[512,512]{1,0:T(8,128)(2,1)} %reduce-scatter.7.cloned.1.call-done, ...), kind=kOutput, calls=%fused_computation.52 | convolution fusion | flops 807141376 | bytes 7342084 | tf_op jit(solution)/shard_map/dot_general | solution.py:130
  (60 shorter events, 8.6 us)
Async XLA Ops:
  6.5 6.9 %copy-start = (bf16[512,2048]{1,0:T(8,128)(2,1)S(1)}, bf16[512,2048]{1,0:T(8,128)(2,1)}, u32[]{:S(2)}) copy-start(bf16[512,2048]{1,0:T(8,128)(2,1)} %param.23) | copy-start | bytes 6291460
  6.5 41.9 %reduce-scatter.5.cloned.1.call-start = ((), (), s32[]{:S(2)}) async-start(), calls=%async_computation.8 | async-start | bytes 2621440 | tf_op jit(solution)/shard_map/reduce_scatter | solution.py:64
  16.0 33.0 %copy-start.9 = (s32[512,4]{0,1:T(4,128)S(1)}, s32[512,4]{0,1:T(4,128)}, u32[]{:S(2)}) copy-start(s32[512,4]{0,1:T(4,128)} %param.21) | copy-start | bytes 24580
  16.1 64.6 %all-gather.2.cloned.1.call-start = ((), (), s32[]{:S(2)}) async-start(), calls=%async_computation.9 | async-start | bytes 2621440 | tf_op jit(solution)/shard_map/all_gather | solution.py:67
  48.5 268.3 %reduce-scatter.9.cloned.1.call-start = ((), (), s32[]{:S(2)}) async-start(), calls=%async_computation.11 | async-start | bytes 7864320 | tf_op jit(solution)/shard_map/reduce_scatter | solution.py:125
  51.4 29.2 %copy-start.2 = (bf16[512,2048]{1,0:T(8,128)(2,1)S(1)}, bf16[512,2048]{1,0:T(8,128)(2,1)}, u32[]{:S(2)}) copy-start(bf16[512,2048]{1,0:T(8,128)(2,1)} %param.16) | copy-start | bytes 6291460
  64.6 20.4 %copy-start.10 = (f32[2048]{0:T(1024)S(1)}, f32[2048]{0:T(1024)}, u32[]{:S(2)}) copy-start(f32[2048]{0:T(1024)} %param.24) | copy-start | bytes 24580
  80.6 4.4 %copy-start.3 = (bf16[512,2048]{1,0:T(8,128)(2,1)S(1)}, bf16[512,2048]{1,0:T(8,128)(2,1)}, u32[]{:S(2)}) copy-start(bf16[512,2048]{1,0:T(8,128)(2,1)} %all-gather.2.cloned.1.call-done) | copy-start | bytes 6291460
  85.1 1.4 copy-start.7
  86.1 4.0 copy-start.4
  90.1 83.3 %copy-start.13 = (bf16[2,2048,352]{1,2,0:T(8,128)(2,1)S(1)}, bf16[2,2048,352]{1,2,0:T(8,128)(2,1)}, u32[]{:S(2)}) copy-start(bf16[2,2048,352]{1,2,0:T(8,128)(2,1)} %param.26) | copy-start | bytes 8650756
  170.8 2.7 copy-start.6
  190.2 1.6 copy-start.5
  198.3 5.7 %copy-start.11 = (f32[512,4]{0,1:T(4,128)S(1)}, f32[512,4]{0,1:T(4,128)}, u32[]{:S(2)}) copy-start(f32[512,4]{0,1:T(4,128)} %param.22) | copy-start | bytes 24580
  198.3 83.1 %all-to-all-start.2 = ((bf16[32,48,2048]{2,1,0:T(8,128)(2,1)}), bf16[32,48,2048]{2,1,0:T(8,128)(2,1)}, u32[]{:S(2)}, u32[]{:S(2)}) async-start(bf16[32,48,2048]{2,1,0:T(8,128)(2,1)} %convolution_convert_fusion.2), calls=%async_computation.5 | async-start | bytes 12582912 | tf_op jit(solution)/shard_map/all_to_all | solution.py:109
  203.5 157.6 %reduce-scatter.11.cloned.1.call-start = ((), (), s32[]{:S(2)}) async-start(), calls=%async_computation.12 | async-start | bytes 7864320 | tf_op jit(solution)/shard_map/reduce_scatter | solution.py:125
  301.2 97.6 %reduce-scatter.7.cloned.1.call-start = ((), (), s32[]{:S(2)}) async-start(), calls=%async_computation.10 | async-start | bytes 2621440 | tf_op jit(solution)/shard_map/reduce_scatter | solution.py:76
  316.8 44.4 %all-to-all-start.1 = ((bf16[32,48,512]{2,1,0:T(8,128)(2,1)}), bf16[32,48,512]{2,1,0:T(8,128)(2,1)}, u32[]{:S(2)}, u32[]{:S(2)}) async-start(bf16[32,48,512]{2,1,0:T(8,128)(2,1)} %reduce-scatter.9.cloned.1.call-done), calls=%async_computation.4 | async-start | bytes 3145728 | tf_op jit(solution)/shard_map/all_to_all | solution.py:126
  321.5 47.0 %copy-start.12 = (bf16[2048]{0:T(1024)(128)(2,1)S(1)}, bf16[2048]{0:T(1024)(128)(2,1)}, u32[]{:S(2)}) copy-start(bf16[2048]{0:T(1024)(128)(2,1)} %param.31) | copy-start | bytes 12292
  361.2 31.3 %all-to-all-start.3 = ((bf16[32,48,512]{2,1,0:T(8,128)(2,1)}), bf16[32,48,512]{2,1,0:T(8,128)(2,1)}, u32[]{:S(2)}, u32[]{:S(2)}) async-start(bf16[32,48,512]{2,1,0:T(8,128)(2,1)} %reduce-scatter.11.cloned.1.call-done), calls=%async_computation.7 | async-start | bytes 3145728 | tf_op jit(solution)/shard_map/all_to_all | solution.py:126
  392.4 3.0 copy-start.8
  398.8 4.7 %copy-start.1 = (bf16[512,2048]{1,0:T(8,128)(2,1)S(1)}, bf16[512,2048]{1,0:T(8,128)(2,1)}, u32[]{:S(2)}) copy-start(bf16[512,2048]{1,0:T(8,128)(2,1)} %param.23) | copy-start | bytes 6291460
Sparse Core Ops, SparseCore 0:
  16.2 32.1 reduce-scatter.4
  50.1 30.4 all-gather.1
  190.3 60.4 reduce-scatter.8
  301.3 59.8 reduce-scatter.10
  363.4 29.4 reduce-scatter.6

commit v10 on v9

--- a/solution.py
+++ b/solution.py
@@ -93,9 +93,15 @@
         jnp.arange(ep_count, dtype=jnp.int32)[:, None, None] * local_experts
         + jnp.arange(local_experts, dtype=jnp.int32)[None, :, None]
     ) * capacity + jnp.arange(capacity, dtype=jnp.int32)[None, None, :]
+    pieces = [(0, 0, capacity)] if local_experts < 2 else []
+    for index in range(local_experts):
+        if index == local_experts - 1 and capacity % 2 == 0 and local_experts > 1:
+            pieces += [(index, 0, capacity // 2), (index, capacity // 2, capacity)]
+        elif local_experts > 1:
+            pieces.append((index, 0, capacity))
     mixes = []
-    for index in range(local_experts):
-        ids = slot_grid[:, index].reshape(-1)
+    for index, first, last in pieces:
+        ids = slot_grid[:, index, first:last].reshape(-1)
         hit = slot[:, :, None] == ids[None, None, :]
         mixing = jnp.sum(jnp.where(hit, route_weights[:, :, None], 0.0), axis=1)
         high = mixing.astype(jnp.bfloat16)
@@ -114,23 +120,26 @@
             "scd,df->scf", rows, expert_up[index], preferred_element_type=jnp.float32
         )
         expert_hidden = (jax.nn.silu(gate_rows) * up_rows).astype(jnp.bfloat16)
-        expert_part = jnp.einsum(
-            "scf,fd->scd",
-            expert_hidden,
-            expert_down[index],
-            preferred_element_type=jnp.float32,
-        ).astype(jnp.bfloat16)
-        if index == local_experts - 1:
-            expert_part, mixes = lax.optimization_barrier((expert_part, mixes))
-        expert_cols = lax.psum_scatter(expert_part, "tp", scatter_dimension=2, tiled=True)
-        returned = lax.all_to_all(expert_cols, "ep", split_axis=0, concat_axis=0, tiled=True)
-        columns = returned.shape[2]
-        flat_results = returned.reshape(ep_count * capacity, columns)
-        high, low = mixes[index]
-        term = jnp.dot(high, flat_results, preferred_element_type=jnp.float32) + jnp.dot(
-            low, flat_results, preferred_element_type=jnp.float32
-        )
-        routed = term if routed is None else routed + term
+        for place, (owner, first, last) in enumerate(pieces):
+            if owner != index:
+                continue
+            expert_part = jnp.einsum(
+                "scf,fd->scd",
+                expert_hidden[:, first:last],
+                expert_down[index],
+                preferred_element_type=jnp.float32,
+            ).astype(jnp.bfloat16)
+            if place == len(pieces) - 2:
+                expert_part, mixes = lax.optimization_barrier((expert_part, mixes))
+            expert_cols = lax.psum_scatter(expert_part, "tp", scatter_dimension=2, tiled=True)
+            returned = lax.all_to_all(expert_cols, "ep", split_axis=0, concat_axis=0, tiled=True)
+            columns = returned.shape[2]
+            flat_results = returned.reshape(-1, columns)
+            high, low = mixes[place]
+            term = jnp.dot(high, flat_results, preferred_element_type=jnp.float32) + jnp.dot(
+                low, flat_results, preferred_element_type=jnp.float32
+            )
+            routed = term if routed is None else routed + term
     resid_cols = lax.dynamic_slice_in_dim(resid, lax.axis_index("tp") * columns, columns, 1)
     return (resid_cols + shared_scale[:, None] * shared_cols + routed).astype(jnp.bfloat16)
 

time: 414 us -> 407 us (0.983)
  waiting for transfers between devices: 175 us -> 148 us
  blocking collectives: 80.7 us -> 99.1 us
    reduce_scatter x2 -> x3, waiting for transfers between devices: 39.7 us -> 6.78 us  [on_device(): lax.psum_scatter(expert_part, 'tp', scatter_dimension=2, tiled=True)]
    all_to_all x0 -> x1, blocking collectives: none -> 18.4 us  [on_device(): lax.all_to_all(expert_cols, 'ep', split_axis=0, concat_axis=0, tiled=True)]
    all_to_all x2, waiting for transfers between devices: 20.3 us -> 30.5 us  [on_device(): lax.all_to_all(expert_cols, 'ep', split_axis=0, concat_axis=0, tiled=True)]
    all_to_all x1, waiting for transfers between devices: 66.8 us -> 62.1 us  [on_device(): lax.all_to_all(outgoing, 'ep', split_axis=0, concat_axis=0, tiled=True)]
    dot_general x2 -> x3, matrix products: 8.05 us -> 10.2 us  [on_device(): jnp.dot(low, flat_results, preferred_element_type=jnp.float32)]
    dot_general x2 -> x4, matrix products: 23.4 us -> 22.4 us  [the longest x3 18.7 us: on_device(): jnp.einsum('scf,fd->scd', expert_hidden[:, first:last], expert_down[index...]
  transfers between devices with their start and end apart: 8 -> 9, of which waited for: 5 -> 6; matrix products, arithmetic and copies ran while one was open for 19% -> 22% of each run, Pallas kernels for 0% -> 0%
where the time goes in v10:
time: 407 us; the launch traced here: 403 us
  waiting for transfers between devices  148 us (36%)
  blocking collectives  99.1 us (24%)
  matrix products  84.3 us (21%)
  other arithmetic  31.8 us (8%)
  starting transfers between devices  17.5 us (4%)
  between operations  14.1 us (3%)
  local copies, waits for them, and re-layouts  8.69 us (2%)
    all_to_all x1, blocking collectives, on_device(): lax.all_to_all(outgoing, 'ep', split_axis=0, concat_axis=0, tiled=True)  80.7 us
    all_to_all x1, waiting for transfers between devices, on_device(): lax.all_to_all(outgoing, 'ep', split_axis=0, concat_axis=0, tiled=True)  62.1 us
    reduce_scatter x1, waiting for transfers between devices, on_device(): lax.psum_scatter(partial_value.astype(jnp.bfloat16), 'tp', scatter_dimens...  32.3 us
    all_to_all x2, waiting for transfers between devices, on_device(): lax.all_to_all(expert_cols, 'ep', split_axis=0, concat_axis=0, tiled=True)  30.5 us
    dot_general x3, matrix products, on_device(): jnp.einsum('scf,fd->scd', expert_hidden[:, first:last], expert_down[index...  18.7 us
    all_to_all x1, blocking collectives, on_device(): lax.all_to_all(expert_cols, 'ep', split_axis=0, concat_axis=0, tiled=True)  18.4 us
    all_gather x1, waiting for transfers between devices, on_device(): summed = lax.all_gather(summed_cols, 'tp', axis=1, tiled=True)  16 us
    all_to_all x2, starting transfers between devices, on_device(): lax.all_to_all(expert_cols, 'ep', split_axis=0, concat_axis=0, tiled=True)  12 us
  transfers between devices with their start and end apart: 9, of which 6 were waited for; matrix products, arithmetic and copies ran while one was open for 22% of the time, Pallas kernels for 0%

profile of v10, /device:TPU:0, one launch (start us, length us, event | category | flops | bytes accessed | tf_op | source)
XLA Modules:
  0.0 403.3 jit_solution(7167755341591162272)
XLA Ops:
  16.1 32.3 %reduce-scatter.6.cloned.1.call-done = bf16[512,512]{1,0:T(8,128)(2,1)} async-done(((bf16[512,2048]{1,0:T(8,128)(2,1)}), bf16[512,512]{1,0:T(8,128)(2,1)}) %reduce-scatter.6.cloned.1.call-update) | async-done | bytes 524304 | tf_op jit(solution)/shard_map/reduce_scatter | solution.py:64
  51.1 8.5 %fusion.1 = pred[512,3072]{1,0:T(8,128)(4,1)} fusion(s32[512,4]{0,1:T(4,128)S(1)} %multiply_add_fusion), kind=kLoop, calls=%fused_computation.2 | loop fusion | flops 11010048 | bytes 1581056 | tf_op jit(solution)/shard_map/reduce_or | solution.py:90
  59.6 5.0 %copy.56 = pred[3072,512]{1,0:T(8,128)(4,1)} copy(pred[3072,512]{0,1:T(8,128)(4,1)} %bitcast.102) | data formatting | bytes 3145728 | tf_op jit(solution)/shard_map/transpose | solution.py:90
  64.6 16.0 %all-gather.2.cloned.1.call-done = bf16[512,2048]{1,0:T(8,128)(2,1)} async-done(((bf16[512,512]{1,0:T(8,128)(2,1)}), bf16[512,2048]{1,0:T(8,128)(2,1)}) %all-gather.2.cloned.1.call-update) | async-done | bytes 2097168 | tf_op jit(solution)/shard_map/all_gather | solution.py:67
  80.7 4.3 %convert_add_fusion = (f32[512,2048]{1,0:T(8,128)}, f32[512]{0:T(512)S(1)}) fusion(bf16[512,2048]{1,0:T(8,128)(2,1)} %all-gather.2.cloned.1.call-done, bf16[512,2048]{1,0:T(8,128)(2,1)S(1)} %copy-done.2), kind=kLoop, calls=%fused_computation.13 | loop fusion | flops 5242368 | bytes 8390656 | tf_op jit(solution)/shard_map/add | solution.py:68
  86.4 3.6 convolution_convert_fusion.1
  90.1 80.7 %all_to_all.25 = bf16[32,48,2048]{2,1,0:T(8,128)(2,1)S(1)} all-to-all(bf16[32,48,2048]{2,1,0:T(8,128)(2,1)S(1)} %convolution_convert_fusion.1), channel_id=1, replica_groups=mesh['ep'=32,'tp'=4] {'ep'}, dimensions={0} | all-to-all | bytes 12582912 | tf_op jit(solution)/shard_map/all_to_all | solution.py:115
  170.8 3.5 fusion.13
  174.3 3.7 multiply_convert_fusion.1
  178.0 3.4 convolution_convert_fusion.3
  182.2 3.3 select_reduce_fusion.1
  185.5 6.5 %convolution_convert_fusion.2 = bf16[32,48,2048]{2,1,0:T(8,128)(2,1)} fusion(pred[32,2,48,512]{3,2,1,0:T(8,128)(4,1)} %bitcast.103, bf16[512,2048]{1,0:T(8,128)(2,1)S(1)} %copy-done.5), kind=kOutput, calls=%fused_computation.10 | convolution fusion | flops 3224371200 | bytes 9175040 | tf_op jit(solution)/shard_map/sct,td->scd/dot_general | solution.py:112
  191.9 4.9 %all-to-all-start = ((bf16[32,48,2048]{2,1,0:T(8,128)(2,1)}), bf16[32,48,2048]{2,1,0:T(8,128)(2,1)}, u32[]{:S(2)}, u32[]{:S(2)}) async-start(bf16[32,48,2048]{2,1,0:T(8,128)(2,1)} %convolution_convert_fusion.2), calls=%async_computation.2 | async-start | bytes 12582912 | tf_op jit(solution)/shard_map/all_to_all | solution.py:115
  196.9 5.0 %subtract_convert_fusion.1 = (bf16[512,768]{1,0:T(8,128)(2,1)}, bf16[512,768]{1,0:T(8,128)(2,1)}, bf16[512,768]{1,0:T(8,128)(2,1)}, bf16[512,768]{1,0:T(8,128)(2,1)}) fusion(f32[512,768]{1,0:T(8,128)} %get-tuple-element.15, f32[512,768]{1,0:T(8,128)} %get-tuple-element.16), kind=kLoop, calls=%fused_computation.35 | loop fusion | flops 3145728 | bytes 6291456 | tf_op jit(solution)/shard_map/convert_element_type | solution.py:108
  201.9 4.2 %select_reduce_fusion = f32[512,1536]{1,0:T(8,128)S(1)} fusion(f32[512,4]{0,1:T(4,128)S(1)} %copy-done.10, s32[1536]{0:T(1024)S(1)} %eq.99, s32[512,4]{0,1:T(4,128)S(1)} %multiply_add_fusion), kind=kLoop, calls=%fused_computation.5 | loop fusion | flops 8650752 | bytes 3168256 | tf_op jit(solution)/shard_map/reduce_sum | solution.py:106
  209.0 3.5 convolution_convert_fusion.4
  212.6 62.1 %all-to-all-done = bf16[32,48,2048]{2,1,0:T(8,128)(2,1)} async-done(((bf16[32,48,2048]{2,1,0:T(8,128)(2,1)}), bf16[32,48,2048]{2,1,0:T(8,128)(2,1)}, u32[]{:S(2)}, u32[]{:S(2)}) %all-to-all-start) | async-done | bytes 6291488 | tf_op jit(solution)/shard_map/all_to_all | solution.py:115
  274.7 8.1 %fusion.17 = f32[32,48,352]{2,1,0:T(8,128)} fusion(bf16[32,48,2048]{2,1,0:T(8,128)(2,1)} %all-to-all-done, bf16[2,2048,352]{1,2,0:T(8,128)(2,1)} %param.26), kind=kOutput, calls=%fused_computation.43 | convolution fusion | flops 2214592512 | bytes 9895936 | tf_op jit(solution)/shard_map/scd,df->scf/dot_general | solution.py:119
  282.8 11.7 %convolution_convert_fusion = bf16[32,48,2048]{2,1,0:T(8,128)(2,1)} fusion(bf16[2,352,2048]{2,1,0:T(8,128)(2,1)} %param.27, f32[32,48,352]{2,1,0:T(8,128)} %fusion.17, bf16[32,48,2048]{2,1,0:T(8,128)(2,1)} %all-to-all-done, bf16[2,2048,352]{1,2,0:T(8,128)(2,1)} %param.25), kind=kOutput, calls=%fused_computation.8 | convolution fusion | flops 4435574784 | bytes 17825792 | tf_op jit(solution)/shard_map/scf,fd->scd/dot_general | solution.py:126
  294.8 5.6 %fusion.51 = f32[512,896]{1,0:T(8,128)} fusion(bf16[512,2048]{1,0:T(8,128)(2,1)S(1)} %copy-done.5, bf16[2048,896]{1,0:T(8,128)(2,1)} %param.28), kind=kOutput, calls=%fused_computation.86 | convolution fusion | flops 1879048192 | bytes 7602176 | tf_op jit(solution)/shard_map/dot_general | solution.py:72
  300.4 9.6 %convolution_convert_fusion.5 = bf16[512,2048]{1,0:T(8,128)(2,1)} fusion(bf16[896,2048]{1,0:T(8,128)(2,1)} %param.30, f32[512,896]{1,0:T(8,128)} %fusion.51, bf16[512,2048]{1,0:T(8,128)(2,1)S(1)} %copy-done.5, bf16[2048,896]{1,0:T(8,128)(2,1)} %param.29), kind=kOutput, calls=%fused_computation.23 | convolution fusion | flops 3761897472 | bytes 13369344 | tf_op jit(solution)/shard_map/dot_general | solution.py:75
  310.0 4.6 %all-to-all-start.4 = ((bf16[32,24,512]{2,1,0:T(8,128)(2,1)}), bf16[32,24,512]{2,1,0:T(8,128)(2,1)}, u32[]{:S(2)}, u32[]{:S(2)}) async-start(bf16[32,24,512]{2,1,0:T(8,128)(2,1)} %reduce-scatter.14.cloned.1.call-done), calls=%async_computation.9 | async-start | bytes 1572864 | tf_op jit(solution)/shard_map/all_to_all | solution.py:135
  314.7 14.5 %all-to-all-done.4 = bf16[32,24,512]{2,1,0:T(8,128)(2,1)} async-done(((bf16[32,24,512]{2,1,0:T(8,128)(2,1)}), bf16[32,24,512]{2,1,0:T(8,128)(2,1)}, u32[]{:S(2)}, u32[]{:S(2)}) %all-to-all-start.4) | async-done | bytes 786464 | tf_op jit(solution)/shard_map/all_to_all | solution.py:135
  329.2 18.4 %all_to_all.26 = bf16[32,24,512]{2,1,0:T(8,128)(2,1)S(1)} all-to-all(bf16[32,24,512]{2,1,0:T(8,128)(2,1)} %reduce-scatter.12.cloned.1.call-done), channel_id=1, replica_groups=mesh['ep'=32,'tp'=4] {'ep'}, dimensions={0} | all-to-all | bytes 1572864 | tf_op jit(solution)/shard_map/all_to_all | solution.py:135
  347.6 6.7 %reduce-scatter.10.cloned.1.call-done = bf16[32,48,512]{2,1,0:T(8,128)(2,1)} async-done(((bf16[32,48,2048]{2,1,0:T(8,128)(2,1)}), bf16[32,48,512]{2,1,0:T(8,128)(2,1)}) %reduce-scatter.10.cloned.1.call-update) | async-done | bytes 1572880 | tf_op jit(solution)/shard_map/reduce_scatter | solution.py:134
  354.3 7.4 %all-to-all-start.1 = ((bf16[32,48,512]{2,1,0:T(8,128)(2,1)}), bf16[32,48,512]{2,1,0:T(8,128)(2,1)}, u32[]{:S(2)}, u32[]{:S(2)}) async-start(bf16[32,48,512]{2,1,0:T(8,128)(2,1)} %reduce-scatter.10.cloned.1.call-done), calls=%async_computation.4 | async-start | bytes 3145728 | tf_op jit(solution)/shard_map/all_to_all | solution.py:135
  362.4 2.8 fusion.53
  366.9 2.7 convolution_add_fusion
  369.6 16.0 %all-to-all-done.1 = bf16[32,48,512]{2,1,0:T(8,128)(2,1)} async-done(((bf16[32,48,512]{2,1,0:T(8,128)(2,1)}), bf16[32,48,512]{2,1,0:T(8,128)(2,1)}, u32[]{:S(2)}, u32[]{:S(2)}) %all-to-all-start.1) | async-done | bytes 1572896 | tf_op jit(solution)/shard_map/all_to_all | solution.py:135
  385.6 3.0 fusion.52
  388.6 3.4 convolution_add_fusion.2
  392.0 4.2 %fusion.28 = bf16[512,512]{1,0:T(8,128)(2,1)} fusion(f32[512,512]{1,0:T(8,128)} %convolution_add_fusion, f32[512,512]{1,0:T(8,128)} %convolution_add_fusion.2, f32[512,512]{1,0:T(8,128)} %fusion.53, bf16[512,768]{1,0:T(8,128)(2,1)} %get-tuple-element.12, bf16[768,512]{1,0:T(8,128)(2,1)S(1)} %bitcast.101, ...), kind=kOutput, calls=%fused_computation.57 | convolution fusion | flops 404750336 | bytes 6817796 | tf_op jit(solution)/shard_map/dot_general | solution.py:139
  (79 shorter events, 20.0 us)
Async XLA Ops:
  6.5 6.9 %copy-start = (bf16[512,2048]{1,0:T(8,128)(2,1)S(1)}, bf16[512,2048]{1,0:T(8,128)(2,1)}, u32[]{:S(2)}) copy-start(bf16[512,2048]{1,0:T(8,128)(2,1)} %param.23) | copy-start | bytes 6291460
  6.5 41.9 %reduce-scatter.6.cloned.1.call-start = ((), (), s32[]{:S(2)}) async-start(), calls=%async_computation.10 | async-start | bytes 2621440 | tf_op jit(solution)/shard_map/reduce_scatter | solution.py:64
  16.1 32.7 %copy-start.11 = (s32[512,4]{0,1:T(4,128)S(1)}, s32[512,4]{0,1:T(4,128)}, u32[]{:S(2)}) copy-start(s32[512,4]{0,1:T(4,128)} %param.21) | copy-start | bytes 24580
  16.1 64.6 %all-gather.2.cloned.1.call-start = ((), (), s32[]{:S(2)}) async-start(), calls=%async_computation.11 | async-start | bytes 2621440 | tf_op jit(solution)/shard_map/all_gather | solution.py:67
  48.5 261.6 %reduce-scatter.14.cloned.1.call-start = ((), (), s32[]{:S(2)}) async-start(), calls=%async_computation.15 | async-start | bytes 3932160 | tf_op jit(solution)/shard_map/reduce_scatter | solution.py:134
  51.1 29.5 %copy-start.2 = (bf16[512,2048]{1,0:T(8,128)(2,1)S(1)}, bf16[512,2048]{1,0:T(8,128)(2,1)}, u32[]{:S(2)}) copy-start(bf16[512,2048]{1,0:T(8,128)(2,1)} %param.16) | copy-start | bytes 6291460
  64.6 20.4 %copy-start.12 = (f32[2048]{0:T(1024)S(1)}, f32[2048]{0:T(1024)}, u32[]{:S(2)}) copy-start(f32[2048]{0:T(1024)} %param.24) | copy-start | bytes 24580
  80.7 4.4 %copy-start.3 = (bf16[512,2048]{1,0:T(8,128)(2,1)S(1)}, bf16[512,2048]{1,0:T(8,128)(2,1)}, u32[]{:S(2)}) copy-start(bf16[512,2048]{1,0:T(8,128)(2,1)} %all-gather.2.cloned.1.call-done) | copy-start | bytes 6291460
  85.0 1.4 copy-start.8
  86.1 4.0 copy-start.4
  90.1 80.7 %copy-start.14 = (bf16[2,2048,352]{1,2,0:T(8,128)(2,1)S(1)}, bf16[2,2048,352]{1,2,0:T(8,128)(2,1)}, u32[]{:S(2)}) copy-start(bf16[2,2048,352]{1,2,0:T(8,128)(2,1)} %param.26) | copy-start | bytes 8650756
  170.8 3.5 copy-start.17
  174.3 3.7 copy-start.15
  181.5 0.7 copy-start.10
  181.5 4.0 copy-start.5
  191.9 82.8 %all-to-all-start = ((bf16[32,48,2048]{2,1,0:T(8,128)(2,1)}), bf16[32,48,2048]{2,1,0:T(8,128)(2,1)}, u32[]{:S(2)}, u32[]{:S(2)}) async-start(bf16[32,48,2048]{2,1,0:T(8,128)(2,1)} %convolution_convert_fusion.2), calls=%async_computation.2 | async-start | bytes 12582912 | tf_op jit(solution)/shard_map/all_to_all | solution.py:115
  196.8 117.9 %reduce-scatter.12.cloned.1.call-start = ((), (), s32[]{:S(2)}) async-start(), calls=%async_computation.14 | async-start | bytes 3932160 | tf_op jit(solution)/shard_map/reduce_scatter | solution.py:134
  206.1 2.9 copy-start.16
  212.5 141.8 %reduce-scatter.10.cloned.1.call-start = ((), (), s32[]{:S(2)}) async-start(), calls=%async_computation.13 | async-start | bytes 7864320 | tf_op jit(solution)/shard_map/reduce_scatter | solution.py:134
  294.5 97.5 %reduce-scatter.8.cloned.1.call-start = ((), (), s32[]{:S(2)}) async-start(), calls=%async_computation.12 | async-start | bytes 2621440 | tf_op jit(solution)/shard_map/reduce_scatter | solution.py:76
  310.0 19.2 %all-to-all-start.4 = ((bf16[32,24,512]{2,1,0:T(8,128)(2,1)}), bf16[32,24,512]{2,1,0:T(8,128)(2,1)}, u32[]{:S(2)}, u32[]{:S(2)}) async-start(bf16[32,24,512]{2,1,0:T(8,128)(2,1)} %reduce-scatter.14.cloned.1.call-done), calls=%async_computation.9 | async-start | bytes 1572864 | tf_op jit(solution)/shard_map/all_to_all | solution.py:135
  314.7 47.0 %copy-start.13 = (bf16[2048]{0:T(1024)(128)(2,1)S(1)}, bf16[2048]{0:T(1024)(128)(2,1)}, u32[]{:S(2)}) copy-start(bf16[2048]{0:T(1024)(128)(2,1)} %param.31) | copy-start | bytes 12292
  354.3 31.3 %all-to-all-start.1 = ((bf16[32,48,512]{2,1,0:T(8,128)(2,1)}), bf16[32,48,512]{2,1,0:T(8,128)(2,1)}, u32[]{:S(2)}, u32[]{:S(2)}) async-start(bf16[32,48,512]{2,1,0:T(8,128)(2,1)} %reduce-scatter.10.cloned.1.call-done), calls=%async_computation.4 | async-start | bytes 3145728 | tf_op jit(solution)/shard_map/all_to_all | solution.py:135
  361.7 3.5 copy-start.7
  362.4 4.5 %copy-start.6 = (bf16[512,768]{1,0:T(8,128)(2,1)S(1)}, bf16[512,768]{1,0:T(8,128)(2,1)}, u32[]{:S(2)}) copy-start(bf16[512,768]{1,0:T(8,128)(2,1)} %get-tuple-element.14) | copy-start | bytes 2359300
  385.6 3.0 copy-start.9
  392.0 4.2 %copy-start.1 = (bf16[512,2048]{1,0:T(8,128)(2,1)S(1)}, bf16[512,2048]{1,0:T(8,128)(2,1)}, u32[]{:S(2)}) copy-start(bf16[512,2048]{1,0:T(8,128)(2,1)} %param.23) | copy-start | bytes 6291460
Sparse Core Ops, SparseCore 0:
  16.2 32.1 reduce-scatter.5
  50.1 30.5 all-gather.1
  181.6 34.7 reduce-scatter.13
  218.7 38.0 reduce-scatter.11
  294.7 59.6 reduce-scatter.9
  356.6 29.4 reduce-scatter.7

commit v11 on v10

--- a/solution.py
+++ b/solution.py
@@ -93,12 +93,10 @@
         jnp.arange(ep_count, dtype=jnp.int32)[:, None, None] * local_experts
         + jnp.arange(local_experts, dtype=jnp.int32)[None, :, None]
     ) * capacity + jnp.arange(capacity, dtype=jnp.int32)[None, None, :]
-    pieces = [(0, 0, capacity)] if local_experts < 2 else []
+    split = capacity * 3 // 4 if capacity % 4 == 0 else capacity // 2
+    pieces = []
     for index in range(local_experts):
-        if index == local_experts - 1 and capacity % 2 == 0 and local_experts > 1:
-            pieces += [(index, 0, capacity // 2), (index, capacity // 2, capacity)]
-        elif local_experts > 1:
-            pieces.append((index, 0, capacity))
+        pieces += [(index, 0, split), (index, split, capacity)]
     mixes = []
     for index, first, last in pieces:
         ids = slot_grid[:, index, first:last].reshape(-1)

time: 407 us -> 465 us (1.14)
  waiting for transfers between devices: 148 us -> 274 us
  blocking collectives: 99.1 us -> 0 us
  starting transfers between devices: 17.5 us -> 35.4 us
  local copies, waits for them, and re-layouts: 8.69 us -> 22.3 us
    all_to_all x2 -> x0, blocking collectives: 99.1 us -> none  [the longest x1 80.7 us: on_device(): lax.all_to_all(outgoing, 'ep', split_axis=0, concat_axis=0, tiled=True)]
    all_to_all x1 -> x2, waiting for transfers between devices: 62.1 us -> 134 us  [on_device(): lax.all_to_all(outgoing, 'ep', split_axis=0, concat_axis=0, tiled=True)]
    reduce_scatter x3 -> x4, waiting for transfers between devices: 6.78 us -> 73.4 us  [on_device(): lax.psum_scatter(expert_part, 'tp', scatter_dimension=2, tiled=True)]
    all_to_all x2 -> x4, waiting for transfers between devices: 30.5 us -> 18.1 us  [on_device(): lax.all_to_all(expert_cols, 'ep', split_axis=0, concat_axis=0, tiled=True)]
    all_to_all x2 -> x4, starting transfers between devices: 12 us -> 22.6 us  [on_device(): lax.all_to_all(expert_cols, 'ep', split_axis=0, concat_axis=0, tiled=True)]
    dot_general x1 -> x2, matrix products: 3.73 us -> 13.3 us  [on_device(): jnp.einsum('scd,df->scf', rows, expert_gate[index], preferred_element_typ...]
    all_to_all x1 -> x2, starting transfers between devices: 4.9 us -> 12.4 us  [on_device(): lax.all_to_all(outgoing, 'ep', split_axis=0, concat_axis=0, tiled=True)]
    reshape x0 -> x4, local copies, waits for them, and re-layouts: none -> 5.58 us  [on_device(): flat_results = returned.reshape(-1, columns)]
  transfers between devices with their start and end apart: 9 -> 13, of which waited for: 6 -> 9; matrix products, arithmetic and copies ran while one was open for 22% -> 24% of each run, Pallas kernels for 0% -> 0%
where the time goes in v11:
time: 465 us; the launch traced here: 461 us
  waiting for transfers between devices  274 us (59%)
  matrix products  87.8 us (19%)
  starting transfers between devices  35.4 us (8%)
  other arithmetic  27.2 us (6%)
  local copies, waits for them, and re-layouts  22.3 us (5%)
  between operations  14.2 us (3%)
    all_to_all x2, waiting for transfers between devices, on_device(): lax.all_to_all(outgoing, 'ep', split_axis=0, concat_axis=0, tiled=True)  134 us
    reduce_scatter x4, waiting for transfers between devices, on_device(): lax.psum_scatter(expert_part, 'tp', scatter_dimension=2, tiled=True)  73.4 us
    reduce_scatter x1, waiting for transfers between devices, on_device(): lax.psum_scatter(partial_value.astype(jnp.bfloat16), 'tp', scatter_dimens...  32.1 us
    all_to_all x4, starting transfers between devices, on_device(): lax.all_to_all(expert_cols, 'ep', split_axis=0, concat_axis=0, tiled=True)  22.6 us
    all_to_all x4, waiting for transfers between devices, on_device(): lax.all_to_all(expert_cols, 'ep', split_axis=0, concat_axis=0, tiled=True)  18.1 us
    all_gather x1, waiting for transfers between devices, on_device(): summed = lax.all_gather(summed_cols, 'tp', axis=1, tiled=True)  16.6 us
    dot_general x4, matrix products, on_device(): jnp.einsum('scf,fd->scd', expert_hidden[:, first:last], expert_down[index...  15 us
    dot_general x2, matrix products, on_device(): jnp.einsum('scd,df->scf', rows, expert_gate[index], preferred_element_typ...  13.3 us
  transfers between devices with their start and end apart: 13, of which 9 were waited for; matrix products, arithmetic and copies ran while one was open for 24% of the time, Pallas kernels for 0%

profile of v11, /device:TPU:0, one launch (start us, length us, event | category | flops | bytes accessed | tf_op | source)
XLA Modules:
  0.0 460.8 jit_solution(17623599203259864075)
XLA Ops:
  13.4 2.6 convolution_convert_fusion.5
  16.3 32.1 %reduce-scatter.7.cloned.1.call-done = bf16[512,512]{1,0:T(8,128)(2,1)} async-done(((bf16[512,2048]{1,0:T(8,128)(2,1)}), bf16[512,512]{1,0:T(8,128)(2,1)}) %reduce-scatter.7.cloned.1.call-update) | async-done | bytes 524304 | tf_op jit(solution)/shard_map/reduce_scatter | solution.py:64
  50.9 8.5 %fusion.1 = pred[512,3072]{1,0:T(8,128)(4,1)} fusion(s32[512,4]{0,1:T(4,128)S(1)} %multiply_add_fusion), kind=kLoop, calls=%fused_computation.2 | loop fusion | flops 11010048 | bytes 1581056 | tf_op jit(solution)/shard_map/reduce_or | solution.py:90
  59.4 4.7 %copy.81 = pred[3072,512]{1,0:T(8,128)(4,1)} copy(pred[3072,512]{0,1:T(8,128)(4,1)} %bitcast.103) | data formatting | bytes 3145728 | tf_op jit(solution)/shard_map/transpose | solution.py:90
  64.1 16.6 %all-gather.2.cloned.1.call-done = bf16[512,2048]{1,0:T(8,128)(2,1)} async-done(((bf16[512,512]{1,0:T(8,128)(2,1)}), bf16[512,2048]{1,0:T(8,128)(2,1)}) %all-gather.2.cloned.1.call-update) | async-done | bytes 2097168 | tf_op jit(solution)/shard_map/all_gather | solution.py:67
  80.7 4.3 convert_add_fusion
  87.5 5.3 %convolution_convert_fusion.1 = bf16[32,48,2048]{2,1,0:T(8,128)(2,1)} fusion(pred[32,2,48,512]{3,2,1,0:T(8,128)(4,1)S(1)} %bitcast.105, bf16[512,2048]{1,0:T(8,128)(2,1)S(1)} %multiply_convert_fusion), kind=kOutput, calls=%fused_computation.8 | convolution fusion | flops 3224371200 | bytes 9175040 | tf_op jit(solution)/shard_map/sct,td->scd/dot_general | solution.py:110
  92.8 7.5 %all-to-all-start = ((bf16[32,48,2048]{2,1,0:T(8,128)(2,1)}), bf16[32,48,2048]{2,1,0:T(8,128)(2,1)}, u32[]{:S(2)}, u32[]{:S(2)}) async-start(bf16[32,48,2048]{2,1,0:T(8,128)(2,1)} %convolution_convert_fusion.1), calls=%async_computation.2 | async-start | bytes 12582912 | tf_op jit(solution)/shard_map/all_to_all | solution.py:113
  100.3 6.5 %convolution_convert_fusion = bf16[32,48,2048]{2,1,0:T(8,128)(2,1)} fusion(pred[32,2,48,512]{3,2,1,0:T(8,128)(4,1)} %bitcast.104, bf16[512,2048]{1,0:T(8,128)(2,1)S(1)} %copy-done.5), kind=kOutput, calls=%fused_computation.7 | convolution fusion | flops 3224371200 | bytes 9175040 | tf_op jit(solution)/shard_map/sct,td->scd/dot_general | solution.py:110
  106.7 71.4 %all-to-all-done = bf16[32,48,2048]{2,1,0:T(8,128)(2,1)} async-done(((bf16[32,48,2048]{2,1,0:T(8,128)(2,1)}), bf16[32,48,2048]{2,1,0:T(8,128)(2,1)}, u32[]{:S(2)}, u32[]{:S(2)}) %all-to-all-start) | async-done | bytes 6291488 | tf_op jit(solution)/shard_map/all_to_all | solution.py:113
  178.1 4.9 %all-to-all-start.3 = ((bf16[32,48,2048]{2,1,0:T(8,128)(2,1)}), bf16[32,48,2048]{2,1,0:T(8,128)(2,1)}, u32[]{:S(2)}, u32[]{:S(2)}) async-start(bf16[32,48,2048]{2,1,0:T(8,128)(2,1)} %convolution_convert_fusion), calls=%async_computation.7 | async-start | bytes 12582912 | tf_op jit(solution)/shard_map/all_to_all | solution.py:113
  183.1 6.6 %fusion.18 = f32[32,48,352]{2,1,0:T(8,128)S(1)} fusion(bf16[32,48,2048]{2,1,0:T(8,128)(2,1)} %all-to-all-done, bf16[2,2048,352]{1,2,0:T(8,128)(2,1)} %param.26), kind=kOutput, calls=%fused_computation.45 | convolution fusion | flops 2214592512 | bytes 9895936 | tf_op jit(solution)/shard_map/scd,df->scf/dot_general | solution.py:117
  189.7 6.7 %multiply_convert_fusion.2 = bf16[32,48,352]{2,1,0:T(8,128)(2,1)S(1)} fusion(f32[32,48,352]{2,1,0:T(8,128)S(1)} %fusion.18, bf16[32,48,2048]{2,1,0:T(8,128)(2,1)} %all-to-all-done, bf16[2,2048,352]{1,2,0:T(8,128)(2,1)S(1)} %copy-done.22), kind=kOutput, calls=%fused_computation.29 | convolution fusion | flops 2217836544 | bytes 11173888 | tf_op jit(solution)/shard_map/scd,df->scf/dot_general | solution.py:114
  198.8 62.2 %all-to-all-done.3 = bf16[32,48,2048]{2,1,0:T(8,128)(2,1)} async-done(((bf16[32,48,2048]{2,1,0:T(8,128)(2,1)}), bf16[32,48,2048]{2,1,0:T(8,128)(2,1)}, u32[]{:S(2)}, u32[]{:S(2)}) %all-to-all-start.3) | async-done | bytes 6291488 | tf_op jit(solution)/shard_map/all_to_all | solution.py:113
  260.9 6.1 %fusion.13 = f32[32,48,352]{2,1,0:T(8,128)S(1)} fusion(bf16[32,48,2048]{2,1,0:T(8,128)(2,1)} %all-to-all-done.3, bf16[2,2048,352]{1,2,0:T(8,128)(2,1)} %param.26), kind=kOutput, calls=%fused_computation.40 | convolution fusion | flops 2214592512 | bytes 9895936 | tf_op jit(solution)/shard_map/scd,df->scf/dot_general | solution.py:117
  267.1 6.7 %multiply_convert_fusion.1 = bf16[32,48,352]{2,1,0:T(8,128)(2,1)S(1)} fusion(f32[32,48,352]{2,1,0:T(8,128)S(1)} %fusion.13, bf16[32,48,2048]{2,1,0:T(8,128)(2,1)} %all-to-all-done.3, bf16[2,2048,352]{1,2,0:T(8,128)(2,1)S(1)} %copy-done.23), kind=kOutput, calls=%fused_computation.27 | convolution fusion | flops 2217836544 | bytes 11173888 | tf_op jit(solution)/shard_map/scd,df->scf/dot_general | solution.py:114
  280.6 3.6 select_reduce_fusion
  289.0 4.7 %convolution_convert_fusion.2 = bf16[32,36,2048]{2,1,0:T(8,128)(2,1)} fusion(bf16[2,352,2048]{2,1,0:T(8,128)(2,1)S(1)} %copy-done.26, bf16[32,48,352]{2,1,0:T(8,128)(2,1)S(1)} %copy-done.17), kind=kOutput, calls=%fused_computation.15 | convolution fusion | flops 1663303680 | bytes 7143424 | tf_op jit(solution)/shard_map/scf,fd->scd/dot_general | solution.py:124
  293.7 6.0 %convolution_convert_fusion.3 = bf16[32,36,2048]{2,1,0:T(8,128)(2,1)} fusion(bf16[2,352,2048]{2,1,0:T(8,128)(2,1)} %param.27, bf16[32,48,352]{2,1,0:T(8,128)(2,1)S(1)} %multiply_convert_fusion.2), kind=kOutput, calls=%fused_computation.16 | convolution fusion | flops 1663303680 | bytes 7143424 | tf_op jit(solution)/shard_map/scf,fd->scd/dot_general | solution.py:124
  301.8 3.9 all-to-all-start.2
  305.7 5.7 %fusion.54 = f32[512,896]{1,0:T(8,128)} fusion(bf16[512,2048]{1,0:T(8,128)(2,1)S(1)} %copy-done.5, bf16[2048,896]{1,0:T(8,128)(2,1)} %param.28), kind=kOutput, calls=%fused_computation.95 | convolution fusion | flops 1879048192 | bytes 7602176 | tf_op jit(solution)/shard_map/dot_general | solution.py:72
  313.4 3.9 all-to-all-done.2
  317.3 3.9 all-to-all-start.5
  321.3 9.7 %convolution_convert_fusion.4 = bf16[512,2048]{1,0:T(8,128)(2,1)} fusion(bf16[896,2048]{1,0:T(8,128)(2,1)} %param.30, f32[512,896]{1,0:T(8,128)} %fusion.54, bf16[512,2048]{1,0:T(8,128)(2,1)S(1)} %copy-done.5, bf16[2048,896]{1,0:T(8,128)(2,1)} %param.29), kind=kOutput, calls=%fused_computation.22 | convolution fusion | flops 3761897472 | bytes 13369344 | tf_op jit(solution)/shard_map/dot_general | solution.py:75
  332.8 23.2 %reduce-scatter.15.cloned.1.call-done = bf16[32,36,512]{2,1,0:T(8,128)(2,1)} async-done(((bf16[32,36,2048]{2,1,0:T(8,128)(2,1)}), bf16[32,36,512]{2,1,0:T(8,128)(2,1)}) %reduce-scatter.15.cloned.1.call-update) | async-done | bytes 1179664 | tf_op jit(solution)/shard_map/reduce_scatter | solution.py:132
  356.0 7.2 %all-to-all-start.4 = ((bf16[32,36,512]{2,1,0:T(8,128)(2,1)}), bf16[32,36,512]{2,1,0:T(8,128)(2,1)S(1)}, u32[]{:S(2)}, u32[]{:S(2)}) async-start(bf16[32,36,512]{2,1,0:T(8,128)(2,1)} %reduce-scatter.15.cloned.1.call-done), calls=%async_computation.9 | async-start | bytes 2621440 | tf_op jit(solution)/shard_map/all_to_all | solution.py:133
  363.3 50.2 %reduce-scatter.11.cloned.1.call-done = bf16[32,36,512]{2,1,0:T(8,128)(2,1)} async-done(((bf16[32,36,2048]{2,1,0:T(8,128)(2,1)}), bf16[32,36,512]{2,1,0:T(8,128)(2,1)}) %reduce-scatter.11.cloned.1.call-update) | async-done | bytes 1179664 | tf_op jit(solution)/shard_map/reduce_scatter | solution.py:132
  413.4 7.6 %all-to-all-start.1 = ((bf16[32,36,512]{2,1,0:T(8,128)(2,1)}), bf16[32,36,512]{2,1,0:T(8,128)(2,1)}, u32[]{:S(2)}, u32[]{:S(2)}) async-start(bf16[32,36,512]{2,1,0:T(8,128)(2,1)} %reduce-scatter.11.cloned.1.call-done), calls=%async_computation.4 | async-start | bytes 2621440 | tf_op jit(solution)/shard_map/all_to_all | solution.py:133
  425.6 2.4 fusion.58
  429.2 12.4 %all-to-all-done.1 = bf16[32,36,512]{2,1,0:T(8,128)(2,1)} async-done(((bf16[32,36,512]{2,1,0:T(8,128)(2,1)}), bf16[32,36,512]{2,1,0:T(8,128)(2,1)}, u32[]{:S(2)}, u32[]{:S(2)}) %all-to-all-start.1) | async-done | bytes 1179680 | tf_op jit(solution)/shard_map/all_to_all | solution.py:133
  443.7 2.3 fusion.55
  450.6 3.2 fusion.29
  (119 shorter events, 44.3 us)
Async XLA Ops:
  6.5 6.9 %copy-start = (bf16[512,2048]{1,0:T(8,128)(2,1)S(1)}, bf16[512,2048]{1,0:T(8,128)(2,1)}, u32[]{:S(2)}) copy-start(bf16[512,2048]{1,0:T(8,128)(2,1)} %param.23) | copy-start | bytes 6291460
  6.5 41.9 %reduce-scatter.7.cloned.1.call-start = ((), (), s32[]{:S(2)}) async-start(), calls=%async_computation.12 | async-start | bytes 2621440 | tf_op jit(solution)/shard_map/reduce_scatter | solution.py:64
  16.1 32.4 %copy-start.19 = (s32[512,4]{0,1:T(4,128)S(1)}, s32[512,4]{0,1:T(4,128)}, u32[]{:S(2)}) copy-start(s32[512,4]{0,1:T(4,128)} %param.21) | copy-start | bytes 24580
  16.1 64.6 %all-gather.2.cloned.1.call-start = ((), (), s32[]{:S(2)}) async-start(), calls=%async_computation.13 | async-start | bytes 2621440 | tf_op jit(solution)/shard_map/all_gather | solution.py:67
  50.9 29.8 %copy-start.2 = (bf16[512,2048]{1,0:T(8,128)(2,1)S(1)}, bf16[512,2048]{1,0:T(8,128)(2,1)}, u32[]{:S(2)}) copy-start(bf16[512,2048]{1,0:T(8,128)(2,1)} %param.16) | copy-start | bytes 6291460
  64.1 20.9 %copy-start.20 = (f32[2048]{0:T(1024)S(1)}, f32[2048]{0:T(1024)}, u32[]{:S(2)}) copy-start(f32[2048]{0:T(1024)} %param.24) | copy-start | bytes 24580
  80.7 4.4 copy-start.3
  85.0 2.4 copy-start.10
  92.8 7.5 %copy-start.5 = (bf16[512,2048]{1,0:T(8,128)(2,1)S(1)}, bf16[512,2048]{1,0:T(8,128)(2,1)}, u32[]{:S(2)}) copy-start(bf16[512,2048]{1,0:T(8,128)(2,1)} %copy-done.4) | copy-start | bytes 6291460
  92.8 85.4 %all-to-all-start = ((bf16[32,48,2048]{2,1,0:T(8,128)(2,1)}), bf16[32,48,2048]{2,1,0:T(8,128)(2,1)}, u32[]{:S(2)}, u32[]{:S(2)}) async-start(bf16[32,48,2048]{2,1,0:T(8,128)(2,1)} %convolution_convert_fusion.1), calls=%async_computation.2 | async-start | bytes 12582912 | tf_op jit(solution)/shard_map/all_to_all | solution.py:113
  178.1 82.8 %all-to-all-start.3 = ((bf16[32,48,2048]{2,1,0:T(8,128)(2,1)}), bf16[32,48,2048]{2,1,0:T(8,128)(2,1)}, u32[]{:S(2)}, u32[]{:S(2)}) async-start(bf16[32,48,2048]{2,1,0:T(8,128)(2,1)} %convolution_convert_fusion), calls=%async_computation.7 | async-start | bytes 12582912 | tf_op jit(solution)/shard_map/all_to_all | solution.py:113
  183.0 116.7 %reduce-scatter.13.cloned.1.call-start = ((), (), s32[]{:S(2)}) async-start(), calls=%async_computation.16 | async-start | bytes 1966080 | tf_op jit(solution)/shard_map/reduce_scatter | solution.py:132
  183.1 6.6 %copy-start.22 = (bf16[2,2048,352]{1,2,0:T(8,128)(2,1)S(1)}, bf16[2,2048,352]{1,2,0:T(8,128)(2,1)}, u32[]{:S(2)}) copy-start(bf16[2,2048,352]{1,2,0:T(8,128)(2,1)} %param.25) | copy-start | bytes 8650756
  189.7 6.8 %copy-start.24 = (bf16[2,352,2048]{2,1,0:T(8,128)(2,1)S(1)}, bf16[2,352,2048]{2,1,0:T(8,128)(2,1)}, u32[]{:S(2)}) copy-start(bf16[2,352,2048]{2,1,0:T(8,128)(2,1)} %param.27) | copy-start | bytes 8650756
  198.6 112.8 %reduce-scatter.17.cloned.1.call-start = ((), (), s32[]{:S(2)}) async-start(), calls=%async_computation.18 | async-start | bytes 1966080 | tf_op jit(solution)/shard_map/reduce_scatter | solution.py:132
  260.9 6.1 %copy-start.23 = (bf16[2,2048,352]{1,2,0:T(8,128)(2,1)S(1)}, bf16[2,2048,352]{1,2,0:T(8,128)(2,1)}, u32[]{:S(2)}) copy-start(bf16[2,2048,352]{1,2,0:T(8,128)(2,1)} %param.25) | copy-start | bytes 8650756
  267.0 7.8 %copy-start.25 = (bf16[2,352,2048]{2,1,0:T(8,128)(2,1)S(1)}, bf16[2,352,2048]{2,1,0:T(8,128)(2,1)}, u32[]{:S(2)}) copy-start(bf16[2,352,2048]{2,1,0:T(8,128)(2,1)} %param.27) | copy-start | bytes 8650756
  274.9 2.7 copy-start.18
  277.0 79.0 %reduce-scatter.15.cloned.1.call-start = ((), (), s32[]{:S(2)}) async-start(), calls=%async_computation.17 | async-start | bytes 6553600 | tf_op jit(solution)/shard_map/reduce_scatter | solution.py:132
  285.9 3.1 copy-start.26
  293.7 119.8 %reduce-scatter.11.cloned.1.call-start = ((), (), s32[]{:S(2)}) async-start(), calls=%async_computation.15 | async-start | bytes 6553600 | tf_op jit(solution)/shard_map/reduce_scatter | solution.py:132
  301.8 15.5 %all-to-all-start.2 = ((bf16[32,12,512]{2,1,0:T(8,128)(2,1)}), bf16[32,12,512]{2,1,0:T(8,128)(2,1)S(1)}, u32[]{:S(2)}, u32[]{:S(2)}) async-start(bf16[32,12,512]{2,1,0:T(8,128)(2,1)} %copy.84), calls=%async_computation.6 | async-start | bytes 1048576 | tf_op jit(solution)/shard_map/all_to_all | solution.py:133
  317.3 13.6 %copy-start.8 = (bf16[32,12,512]{2,1,0:T(8,128)(2,1)}, bf16[32,12,512]{2,1,0:T(8,128)(2,1)S(1)}, u32[]{:S(2)}) copy-start(bf16[32,12,512]{2,1,0:T(8,128)(2,1)S(1)} %all-to-all-done.2) | copy-start | bytes 1179652
  317.3 15.5 %all-to-all-start.5 = ((bf16[32,12,512]{2,1,0:T(8,128)(2,1)}), bf16[32,12,512]{2,1,0:T(8,128)(2,1)S(1)}, u32[]{:S(2)}, u32[]{:S(2)}) async-start(bf16[32,12,512]{2,1,0:T(8,128)(2,1)} %copy.87), calls=%async_computation.11 | async-start | bytes 1048576 | tf_op jit(solution)/shard_map/all_to_all | solution.py:133
  321.2 128.8 %reduce-scatter.9.cloned.1.call-start = ((), (), s32[]{:S(2)}) async-start(), calls=%async_computation.14 | async-start | bytes 2621440 | tf_op jit(solution)/shard_map/reduce_scatter | solution.py:76
  330.9 90.1 %copy-start.21 = (bf16[2048]{0:T(1024)(128)(2,1)S(1)}, bf16[2048]{0:T(1024)(128)(2,1)}, u32[]{:S(2)}) copy-start(bf16[2048]{0:T(1024)(128)(2,1)} %param.31) | copy-start | bytes 12292
  332.8 23.2 %copy-start.9 = (bf16[32,12,512]{2,1,0:T(8,128)(2,1)}, bf16[32,12,512]{2,1,0:T(8,128)(2,1)S(1)}, u32[]{:S(2)}) copy-start(bf16[32,12,512]{2,1,0:T(8,128)(2,1)S(1)} %all-to-all-done.5) | copy-start | bytes 1179652
  356.0 57.4 %all-to-all-start.4 = ((bf16[32,36,512]{2,1,0:T(8,128)(2,1)}), bf16[32,36,512]{2,1,0:T(8,128)(2,1)S(1)}, u32[]{:S(2)}, u32[]{:S(2)}) async-start(bf16[32,36,512]{2,1,0:T(8,128)(2,1)} %reduce-scatter.15.cloned.1.call-done), calls=%async_computation.9 | async-start | bytes 2621440 | tf_op jit(solution)/shard_map/all_to_all | solution.py:133
  413.4 28.1 %all-to-all-start.1 = ((bf16[32,36,512]{2,1,0:T(8,128)(2,1)}), bf16[32,36,512]{2,1,0:T(8,128)(2,1)}, u32[]{:S(2)}, u32[]{:S(2)}) async-start(bf16[32,36,512]{2,1,0:T(8,128)(2,1)} %reduce-scatter.11.cloned.1.call-done), calls=%async_computation.4 | async-start | bytes 2621440 | tf_op jit(solution)/shard_map/all_to_all | solution.py:133
  424.0 5.2 %copy-start.6 = (bf16[384,512]{1,0:T(8,128)(2,1)}, bf16[384,512]{1,0:T(8,128)(2,1)S(1)}, u32[]{:S(2)}) copy-start(bf16[384,512]{1,0:T(8,128)(2,1)S(1)} %reshape.136) | copy-start | bytes 1179652
  443.7 2.3 copy-start.12
  450.0 3.7 copy-start.1
  (8 other events, 10.9 us)
Sparse Core Ops, SparseCore 0:
  16.2 32.1 reduce-scatter.6
  50.1 30.5 all-gather.1
  198.7 25.7 reduce-scatter.12
  277.2 21.3 reduce-scatter.16
  300.8 55.1 reduce-scatter.14
  358.3 55.1 reduce-scatter.10
  415.8 29.4 reduce-scatter.8
